TPU v7x, 32 devices: a whole 2x2x4 slice. The times are simulated.
32 devices in a mesh: freq: 2 (over x), row: 4 (over z), col: 4 (over y, core).
Axes of the slice: x: 2, y: 2, z: 4, core: 2. Of those that a mesh axis runs over, the one named last changes fastest.
Arguments:
- sky_maps: bfloat16 [512, 128, 512], P('freq', 'row', 'col'), may hold values from -32 to 32
- beam_sigma: float32 [512], P('freq'), may hold values from 1.5 to 4
- whitening: bfloat16 [512, 512], replicated, may hold values from -0.25 to 0.25
- unmix_init: float32 [128, 512], replicated, may hold values from -0.25 to 0.25
Outputs:
- unmixing: float32 [128, 512], replicated
- sources: bfloat16 [128, 65536], P(None, ('freq', 'row', 'col'))
All inputs are finite; a program needn't handle non-finite values.
Results may differ from a plain program's by a relative error of at most 0.0025.
The roundings to bfloat16 on the way count: a program that leaves them out, or rounds other values in their place, can miss the bound.
Values may be sent and summed in bfloat16 or wider, within the bound.
No kernel may reach another device: no remote copies, remote signals or barrier semaphores. Data moves between devices by JAX's collectives and lax.ppermute only.
A program may use at most 64 MiB of HBM per device.

v0:
```python
import jax
import jax.numpy as jnp
from jax import lax
from jax.sharding import PartitionSpec as P

HALF = 8
ITERS = 2
NS_STEPS = 5


def with_halo(cells, sides, width):
    for axis, dim in sides:
        count = lax.axis_size(axis)
        ends = count - 1
        head = lax.slice_in_dim(cells, 0, width, axis=dim)
        tail = lax.slice_in_dim(cells, cells.shape[dim] - width, cells.shape[dim], axis=dim)
        cells = jnp.concatenate(
            [
                lax.ppermute(tail, axis, [(i, (i + 1) % count) for i in range(ends)]),
                cells,
                lax.ppermute(head, axis, [((i + 1) % count, i) for i in range(ends)]),
            ],
            axis=dim,
        )
    return cells


def make_taps(beam_sigma):
    offsets = jnp.arange(2 * HALF + 1, dtype=jnp.float32) - HALF
    shaped = jnp.exp(
        -(offsets[None, :] * offsets[None, :]) / (2.0 * beam_sigma[:, None] * beam_sigma[:, None])
    )
    return (shaped / jnp.sum(shaped, axis=1, keepdims=True)).astype(jnp.bfloat16)


def make_band(beam_taps, length):
    spread = beam_taps.shape[1]
    offsets = jnp.arange(length + spread - 1)[None, :] - jnp.arange(length)[:, None]
    onehot = (offsets[:, :, None] == jnp.arange(spread)[None, None, :]).astype(jnp.float32)
    return jnp.einsum("ijk,ck->cij", onehot, beam_taps.astype(jnp.float32)).astype(jnp.bfloat16)


def inverse_root(matrix):
    frob_norm = jnp.sqrt(jnp.sum(matrix * matrix) + 1e-06)
    current = matrix / frob_norm
    unit_matrix = jnp.eye(matrix.shape[0], dtype=jnp.float32)
    inverse = unit_matrix
    for iteration in range(NS_STEPS):
        correction = 0.5 * (
            3.0 * unit_matrix - jnp.dot(inverse, current, precision=lax.Precision.HIGHEST)
        )
        current = jnp.dot(current, correction, precision=lax.Precision.HIGHEST)
        inverse = jnp.dot(correction, inverse, precision=lax.Precision.HIGHEST)
    return inverse / jnp.sqrt(frob_norm)


def pixel_moments(coarse, whitened):
    outputs = jnp.dot(coarse, whitened, preferred_element_type=jnp.float32)
    cubed = (outputs * outputs * outputs).astype(jnp.bfloat16)
    return lax.dot_general(
        cubed, whitened, (((1,), (1,)), ((), ())), preferred_element_type=jnp.float32
    )


def shards(sky_maps, beam_sigma, whitening, unmix_init):
    beam_taps = make_taps(beam_sigma)
    channels, height, breadth = sky_maps.shape
    band_rows = make_band(beam_taps, height)
    band_cols = make_band(beam_taps, breadth)
    padded = with_halo(sky_maps, (("row", 1),), HALF)
    rowwise = jnp.einsum(
        "cik,ckj->cij", band_rows, padded, preferred_element_type=jnp.float32
    ).astype(jnp.bfloat16)
    widened = with_halo(rowwise, (("col", 2),), HALF)
    smoothed = jnp.einsum(
        "cim,cjm->cij", widened, band_cols, preferred_element_type=jnp.float32
    ).astype(jnp.bfloat16)
    plane_sums = lax.psum(jnp.sum(smoothed, axis=(1, 2), dtype=jnp.float32), ("row", "col"))
    flattened = smoothed.reshape(channels, height * breadth)
    spectra = lax.all_to_all(flattened, "freq", split_axis=1, concat_axis=0, tiled=True)
    devices = lax.axis_size("freq") * lax.axis_size("row") * lax.axis_size("col")
    total_pixels = spectra.shape[1] * devices
    channel_sums = lax.all_gather(plane_sums, "freq", axis=0, tiled=True)
    means = channel_sums / total_pixels
    shift = jnp.dot(whitening.astype(jnp.float32), means, precision=lax.Precision.HIGHEST)
    whitened = (
        jnp.dot(whitening, spectra, preferred_element_type=jnp.float32) - shift[:, None]
    ).astype(jnp.bfloat16)
    unmixing = unmix_init
    for iteration in range(ITERS):
        moments = pixel_moments(unmixing.astype(jnp.bfloat16), whitened)
        moments = lax.psum(moments, ("freq", "row", "col"))
        updated = moments / total_pixels - 3.0 * unmixing
        gram = jnp.dot(updated, updated.T, precision=lax.Precision.HIGHEST)
        unmixing = jnp.dot(inverse_root(gram), updated, precision=lax.Precision.HIGHEST)
    sources = jnp.dot(
        unmixing.astype(jnp.bfloat16), whitened, preferred_element_type=jnp.float32
    ).astype(jnp.bfloat16)
    return (unmixing, sources)


def solution(mesh):
    return jax.shard_map(
        shards,
        mesh=mesh,
        in_specs=(P("freq", "row", "col"), P("freq"), P(), P()),
        out_specs=(P(), P(None, ("freq", "row", "col"))),
        check_vma=False,
    )
```

profile of v0, /device:TPU:0, one launch (start us, length us, event | category | flops | bytes accessed | tf_op | source)
XLA Modules:
  0.0 394.4 jit_solution(6294452238984527691)
XLA Ops:
  7.2 1.3 fusion.76
  8.5 5.0 %collective-permute-start = (bf16[256,8,128]{2,1,0:T(8,128)(2,1)S(1)}, bf16[256,8,128]{2,1,0:T(8,128)(2,1)S(1)}, u32[]{:S(2)}, u32[]{:S(2)}) collective-permute-start(bf16[256,8,128]{2,1,0:T(8,128)(2,1)S(1)} %get-tuple-element.4), channel_id=1, source_target_pairs={{0,4},{4,8},{8,12},{1,5},{5,9},{9,13},{2,6},{6,10},{10,14},{3,7},{... | collective-permute-start | bytes 1572872 | tf_op jit(solution)/shard_map/ppermute | solution.py:19
  13.5 1.3 collective-permute-start.1
  15.0 0.4 convolution_convert_fusion.2
  15.4 3.8 copy.7
  19.2 5.4 %collective-permute-done = bf16[256,8,128]{2,1,0:T(8,128)(2,1)S(1)} collective-permute-done((bf16[256,8,128]{2,1,0:T(8,128)(2,1)S(1)}, bf16[256,8,128]{2,1,0:T(8,128)(2,1)S(1)}, u32[]{:S(2)}, u32[]{:S(2)}) %collective-permute-start) | collective-permute-done | bytes 524320 | tf_op jit(solution)/shard_map/ppermute | solution.py:19
  24.6 4.3 %collective-permute-done.1 = bf16[256,8,128]{2,1,0:T(8,128)(2,1)} collective-permute-done((bf16[256,8,128]{2,1,0:T(8,128)(2,1)S(1)}, bf16[256,8,128]{2,1,0:T(8,128)(2,1)}, u32[]{:S(2)}, u32[]{:S(2)}) %collective-permute-start.1) | collective-permute-done | bytes 524320 | tf_op jit(solution)/shard_map/ppermute | solution.py:21
  28.9 3.3 fusion.13
  32.2 2.9 fusion.75
  35.1 2.7 copy.8
  37.8 2.7 copy.9
  40.5 1.3 collective-permute-start.3
  41.8 3.0 collective-permute-start.2
  44.9 5.2 %convolution_convert_fusion = bf16[256,128,144]{1,0,2:T(8,128)(2,1)} fusion(s32[128,144]{0,1:T(8,128)S(1)} %iota_subtract_fusion, f32[256]{0:T(256)S(1)} %fusion.55, f32[256]{0:T(256)S(1)} %multiply_multiply_fusion.2, f32[17]{0:T(128)S(1)} %multiply_negate_fusion), kind=kOutput, calls=%fused_computation.2 | convolution fusion | flops 165477120 | bytes 9513028 | tf_op jit(solution)/shard_map/ijk,ck->cij/dot_general | solution.py:40
  50.1 3.7 copy.10
  53.8 3.7 copy.11
  57.5 17.0 %convert_reduce_fusion = (f32[256]{0:T(256)S(1)}, bf16[256,32,128]{2,1,0:T(8,128)(2,1)}) fusion(bf16[256,128,144]{1,0,2:T(8,128)(2,1)} %convolution_convert_fusion, bf16[256,32,8]{2,1,0:T(8,128)(2,1)} %copy.11, bf16[256,32,128]{2,1,0:T(8,128)(2,1)S(1)} %fusion.13, bf16[256,32,8]{2,1,0:T(8,128)(2,1)} %copy.10), kind=kOutput, calls=%fused_computation.9 | convolution fusion | flops 312213248 | bytes 13894656 | tf_op jit(solution)/shard_map/cim,cjm->cij/dot_general | solution.py:75
  74.4 2.5 all_to_all.14
  77.0 2.2 copy.13
  79.2 3.8 all-to-all-start
  83.0 30.9 %psum.21 = f32[256]{0:T(256)S(1)} all-reduce(f32[256]{0:T(256)S(1)} %get-tuple-element.6), channel_id=1, replica_groups=mesh['freq'=2,'row'=4,'col'=4] {'row','col'}, use_global_device_ids=true, to_apply=%region_2.0 | all-reduce | flops 256 | bytes 2048 | tf_op jit(solution)/shard_map/psum | solution.py:78
  113.9 4.5 %all-gather = f32[2,1,256]{2,1,0:T(1,128)S(1)} all-gather(f32[1,1,256]{2,1,0:T(1,128)S(1)} %bitcast.82), channel_id=1, replica_groups=mesh['freq'=2,'row'=4,'col'=4] {'freq'}, dimensions={0}, use_global_device_ids=true | all-gather | bytes 3072 | tf_op jit(solution)/shard_map/all_gather | solution.py:83
  118.3 0.5 fusion.77
  118.8 1.3 copy-done.2
  120.2 2.9 subtract_convert_fusion
  123.2 1.9 fusion.22
  125.1 122.5 %all-reduce.3.cloned.1.call-done = f32[128,512]{1,0:T(8,128)} async-done(((f32[128,512]{1,0:T(8,128)}), f32[128,512]{1,0:T(8,128)}) %all-reduce.3.cloned.1.call-update) | async-done | bytes 262160 | tf_op jit(solution)/shard_map/psum | solution.py:92
  247.6 2.1 multiply_reduce_fusion.1
  253.8 1.8 fusion.35
  255.6 124.1 %all-reduce.5.cloned.1.call-done = f32[128,512]{1,0:T(8,128)} async-done(((f32[128,512]{1,0:T(8,128)}), f32[128,512]{1,0:T(8,128)}) %all-reduce.5.cloned.1.call-update) | async-done | bytes 262160 | tf_op jit(solution)/shard_map/psum | solution.py:92
  379.7 2.1 multiply_reduce_fusion
  385.9 1.6 convolution_convert_fusion.1
  (56 shorter events, 6.7 us)
Async XLA Ops:
  7.2 111.2 %copy-start = (bf16[512,512]{1,0:T(8,128)(2,1)S(1)}, bf16[512,512]{1,0:T(8,128)(2,1)}, u32[]{:S(2)}) copy-start(bf16[512,512]{1,0:T(8,128)(2,1)} %param.6) | copy-start | bytes 1572868
  7.2 7.6 %copy-start.6 = (f32[256]{0:T(256)S(1)}, f32[256]{0:T(256)}, u32[]{:S(2)}) copy-start(f32[256]{0:T(256)} %param.5) | copy-start | bytes 3076
  8.5 16.1 %collective-permute-start = (bf16[256,8,128]{2,1,0:T(8,128)(2,1)S(1)}, bf16[256,8,128]{2,1,0:T(8,128)(2,1)S(1)}, u32[]{:S(2)}, u32[]{:S(2)}) collective-permute-start(bf16[256,8,128]{2,1,0:T(8,128)(2,1)S(1)} %get-tuple-element.4), channel_id=1, source_target_pairs={{0,4},{4,8},{8,12},{1,5},{5,9},{9,13},{2,6},{6,10},{10,14},{3,7},{... | collective-permute-start | bytes 1572872 | tf_op jit(solution)/shard_map/ppermute | solution.py:19
  13.5 15.4 %collective-permute-start.1 = (bf16[256,8,128]{2,1,0:T(8,128)(2,1)S(1)}, bf16[256,8,128]{2,1,0:T(8,128)(2,1)}, u32[]{:S(2)}, u32[]{:S(2)}) collective-permute-start(bf16[256,8,128]{2,1,0:T(8,128)(2,1)S(1)} %get-tuple-element.5), channel_id=1, source_target_pairs={{4,0},{8,4},{12,8},{5,1},{9,5},{13,9},{6,2},{10,6},{14,10},{7,3},{... | collective-permute-start | bytes 1572872 | tf_op jit(solution)/shard_map/ppermute | solution.py:21
  40.5 13.3 %collective-permute-start.3 = (bf16[256,32,8]{0,2,1:T(8,128)(2,1)S(1)}, bf16[256,32,8]{0,2,1:T(8,128)(2,1)S(1)}, u32[]{:S(2)}, u32[]{:S(2)}) collective-permute-start(bf16[256,32,8]{0,2,1:T(8,128)(2,1)S(1)} %copy.9), channel_id=1, source_target_pairs={{1,0},{2,1},{3,2},{5,4},{6,5},{7,6},{9,8},{10,9},{11,10},{13,12},{... | collective-permute-start | bytes 393224 | tf_op jit(solution)/shard_map/ppermute | solution.py:21
  41.8 8.2 %collective-permute-start.2 = (bf16[256,32,8]{0,2,1:T(8,128)(2,1)S(1)}, bf16[256,32,8]{0,2,1:T(8,128)(2,1)S(1)}, u32[]{:S(2)}, u32[]{:S(2)}) collective-permute-start(bf16[256,32,8]{0,2,1:T(8,128)(2,1)S(1)} %copy.8), channel_id=1, source_target_pairs={{0,1},{1,2},{2,3},{4,5},{5,6},{6,7},{8,9},{9,10},{10,11},{12,13},{... | collective-permute-start | bytes 393224 | tf_op jit(solution)/shard_map/ppermute | solution.py:19
  79.2 39.6 %all-to-all-start = ((bf16[256,2,2048]{2,0,1:T(8,128)(2,1)}), bf16[256,2,2048]{2,0,1:T(8,128)(2,1)S(1)}, u32[]{:S(2)}, u32[]{:S(2)}) async-start(bf16[256,2,2048]{2,0,1:T(8,128)(2,1)} %copy.13), calls=%async_computation | async-start | bytes 4194304 | tf_op jit(solution)/shard_map/all_to_all | solution.py:80
  83.0 164.6 %all-reduce.3.cloned.1.call-start = ((), (), s32[]{:S(2)}) async-start(), calls=%async_computation.1 | async-start | bytes 524288 | tf_op jit(solution)/shard_map/psum | solution.py:92
  118.8 1.4 copy-start.2
  120.2 3.0 copy-start.1
  125.1 254.7 %all-reduce.5.cloned.1.call-start = ((), (), s32[]{:S(2)}) async-start(), calls=%async_computation.2 | async-start | bytes 524288 | tf_op jit(solution)/shard_map/psum | solution.py:92
  247.6 5.8 %copy-start.3 = (f32[128,512]{1,0:T(8,128)S(1)}, f32[128,512]{1,0:T(8,128)}, u32[]{:S(2)}) copy-start(f32[128,512]{1,0:T(8,128)} %all-reduce.3.cloned.1.call-done) | copy-start | bytes 786436
  379.7 5.8 %copy-start.4 = (f32[128,512]{1,0:T(8,128)S(1)}, f32[128,512]{1,0:T(8,128)}, u32[]{:S(2)}) copy-start(f32[128,512]{1,0:T(8,128)} %all-reduce.5.cloned.1.call-done) | copy-start | bytes 786436
  385.9 1.6 copy-start.5
Sparse Core Ops, SparseCore 0:
  125.2 122.3 all-reduce.2
  255.7 123.9 all-reduce.4
where the time goes:
time: 395 us; the launch traced here: 394 us
  waiting for transfers between devices  256 us (65%)
  matrix products  45.3 us (11%)
  blocking collectives  35.3 us (9%)
  local copies, waits for them, and re-layouts  27 us (7%)
  between operations  15.9 us (4%)
  starting transfers between devices  14.4 us (4%)
    psum x2, waiting for transfers between devices, shards(): moments = lax.psum(moments, ('freq', 'row', 'col'))  247 us
    psum x1, blocking collectives, shards(): lax.psum(jnp.sum(smoothed, axis=(1, 2), dtype=jnp.float32), ('row', 'col'))  30.9 us
    dot_general x1, matrix products, shards(): jnp.einsum('cim,cjm->cij', widened, band_cols, preferred_element_type=jnp...  17 us
    ppermute x2, starting transfers between devices, with_halo(): lax.ppermute(tail, axis, [(i, (i + 1) % count) for i in range(ends)])  8 us
  transfers between devices with their start and end apart: 7, of which 4 were waited for; matrix products, arithmetic and copies ran while one was open for 3% of the time, Pallas kernels for 0%

commit v1 on v0

--- a/solution.py
+++ b/solution.py
@@ -62,6 +62,27 @@
     )
 
 
+def total_sum(partial, axes):
+    count = 1
+    for axis in axes:
+        count *= lax.axis_size(axis)
+    flat = partial.reshape(count, partial.size // count)
+    pieces = lax.all_to_all(flat, axes, 0, 0, tiled=True)
+    piece = jnp.sum(pieces, axis=0)
+    spread = jnp.broadcast_to(piece[None], (count,) + piece.shape)
+    gathered = lax.all_to_all(spread, axes, 0, 0, tiled=True)
+    return gathered.reshape(partial.shape)
+
+
+def gathered_sum(partial, axes):
+    count = 1
+    for axis in axes:
+        count *= lax.axis_size(axis)
+    spread = jnp.broadcast_to(partial[None], (count,) + partial.shape)
+    gathered = lax.all_to_all(spread, axes, 0, 0, tiled=True)
+    return jnp.sum(gathered, axis=0)
+
+
 def shards(sky_maps, beam_sigma, whitening, unmix_init):
     beam_taps = make_taps(beam_sigma)
     channels, height, breadth = sky_maps.shape
@@ -75,12 +96,11 @@
     smoothed = jnp.einsum(
         "cim,cjm->cij", widened, band_cols, preferred_element_type=jnp.float32
     ).astype(jnp.bfloat16)
-    plane_sums = lax.psum(jnp.sum(smoothed, axis=(1, 2), dtype=jnp.float32), ("row", "col"))
     flattened = smoothed.reshape(channels, height * breadth)
     spectra = lax.all_to_all(flattened, "freq", split_axis=1, concat_axis=0, tiled=True)
     devices = lax.axis_size("freq") * lax.axis_size("row") * lax.axis_size("col")
     total_pixels = spectra.shape[1] * devices
-    channel_sums = lax.all_gather(plane_sums, "freq", axis=0, tiled=True)
+    channel_sums = gathered_sum(jnp.sum(spectra, axis=1, dtype=jnp.float32), ("freq", "row", "col"))
     means = channel_sums / total_pixels
     shift = jnp.dot(whitening.astype(jnp.float32), means, precision=lax.Precision.HIGHEST)
     whitened = (
@@ -89,7 +109,7 @@
     unmixing = unmix_init
     for iteration in range(ITERS):
         moments = pixel_moments(unmixing.astype(jnp.bfloat16), whitened)
-        moments = lax.psum(moments, ("freq", "row", "col"))
+        moments = total_sum(moments, ("freq", "row", "col"))
         updated = moments / total_pixels - 3.0 * unmixing
         gram = jnp.dot(updated, updated.T, precision=lax.Precision.HIGHEST)
         unmixing = jnp.dot(inverse_root(gram), updated, precision=lax.Precision.HIGHEST)

time: 395 us -> 180 us (0.46)
  waiting for transfers between devices: 256 us -> 9.66 us
  blocking collectives: 35.3 us -> 88.6 us
  between operations: 15.9 us -> 2.59 us
  matrix products: 45.3 us -> 40.9 us
    psum x2 -> x0, waiting for transfers between devices: 247 us -> none  [shards(): moments = lax.psum(moments, ('freq', 'row', 'col'))]
    all_to_all x0 -> x6, blocking collectives: none -> 88.6 us  [the longest x1 28.6 us: shards(): lax.all_to_all(flattened, 'freq', split_axis=1, concat_axis=0, tiled=True)]
    psum x1 -> x0, blocking collectives: 30.9 us -> none  [shards(): lax.psum(jnp.sum(smoothed, axis=(1, 2), dtype=jnp.float32), ('row', 'col'))]
    all_gather x1 -> x0, blocking collectives: 4.45 us -> none  [shards(): channel_sums = lax.all_gather(plane_sums, 'freq', axis=0, tiled=True)]
  transfers between devices with their start and end apart: 7 -> 4, of which waited for: 4 -> 2; matrix products, arithmetic and copies ran while one was open for 3% -> 7% of each run, Pallas kernels for 0% -> 0%
where the time goes in v1:
time: 180 us
  blocking collectives  88.6 us (49%)
  matrix products  40.9 us (23%)
  local copies, waits for them, and re-layouts  25.4 us (14%)
  starting transfers between devices  10.6 us (6%)
  waiting for transfers between devices  9.66 us (5%)
  between operations  2.59 us (1%)
  other arithmetic  2.29 us (1%)
    all_to_all x1, blocking collectives, shards(): lax.all_to_all(flattened, 'freq', split_axis=1, concat_axis=0, tiled=True)  28.6 us
    all_to_all x2, blocking collectives, total_sum(): gathered = lax.all_to_all(spread, axes, 0, 0, tiled=True)  25.2 us
    all_to_all x2, blocking collectives, total_sum(): pieces = lax.all_to_all(flat, axes, 0, 0, tiled=True)  24.6 us
    dot_general x1, matrix products, shards(): jnp.einsum('cim,cjm->cij', widened, band_cols, preferred_element_type=jnp...  16.2 us
    all_to_all x1, blocking collectives, gathered_sum(): gathered = lax.all_to_all(spread, axes, 0, 0, tiled=True)  10.1 us
    ppermute x2, starting transfers between devices, with_halo(): lax.ppermute(tail, axis, [(i, (i + 1) % count) for i in range(ends)])  8 us
    slice x3, local copies, waits for them, and re-layouts, with_halo(): lax.slice_in_dim(cells, cells.shape[dim] - width, cells.shape[dim], axis=...  6.9 us
    dot_general x2, matrix products, make_band(): jnp.einsum('ijk,ck->cij', onehot, beam_taps.astype(jnp.float32))  5.63 us
  transfers between devices with their start and end apart: 4, of which 2 were waited for; matrix products, arithmetic and copies ran while one was open for 7% of the time, Pallas kernels for 0%

profile of v1, /device:TPU:0, one launch (start us, length us, event | category | flops | bytes accessed | tf_op | source)
XLA Modules:
  0.0 179.9 jit_solution(13576758231059365937)
XLA Ops:
  0.7 1.3 fusion.72
  2.0 5.0 %collective-permute-start = (bf16[256,8,128]{2,1,0:T(8,128)(2,1)S(1)}, bf16[256,8,128]{2,1,0:T(8,128)(2,1)S(1)}, u32[]{:S(2)}, u32[]{:S(2)}) collective-permute-start(bf16[256,8,128]{2,1,0:T(8,128)(2,1)S(1)} %get-tuple-element.4), channel_id=1, source_target_pairs={{0,4},{4,8},{8,12},{1,5},{5,9},{9,13},{2,6},{6,10},{10,14},{3,7},{... | collective-permute-start | bytes 1572872 | tf_op jit(solution)/shard_map/ppermute | solution.py:19
  7.0 1.3 collective-permute-start.1
  8.9 3.8 %copy.25 = bf16[256,32,48]{2,1,0:T(8,128)(2,1)} copy(bf16[256,32,48]{0,2,1:T(8,128)(2,1)S(1)} %convolution_convert_fusion.2) | data formatting | bytes 1572864 | tf_op jit(solution)/shard_map/convert_element_type | solution.py:40
  12.7 5.4 %collective-permute-done = bf16[256,8,128]{2,1,0:T(8,128)(2,1)S(1)} collective-permute-done((bf16[256,8,128]{2,1,0:T(8,128)(2,1)S(1)}, bf16[256,8,128]{2,1,0:T(8,128)(2,1)S(1)}, u32[]{:S(2)}, u32[]{:S(2)}) %collective-permute-start) | collective-permute-done | bytes 524320 | tf_op jit(solution)/shard_map/ppermute | solution.py:19
  18.1 4.3 %collective-permute-done.1 = bf16[256,8,128]{2,1,0:T(8,128)(2,1)} collective-permute-done((bf16[256,8,128]{2,1,0:T(8,128)(2,1)S(1)}, bf16[256,8,128]{2,1,0:T(8,128)(2,1)}, u32[]{:S(2)}, u32[]{:S(2)}) %collective-permute-start.1) | collective-permute-done | bytes 524320 | tf_op jit(solution)/shard_map/ppermute | solution.py:21
  22.4 3.3 %fusion.13 = bf16[256,32,128]{2,1,0:T(8,128)(2,1)S(1)} fusion(bf16[256,32,48]{2,1,0:T(8,128)(2,1)} %copy.25, bf16[256,8,128]{2,1,0:T(8,128)(2,1)} %collective-permute-done.1, bf16[256,32,128]{2,1,0:T(8,128)(2,1)} %param.4, bf16[256,8,128]{2,1,0:T(8,128)(2,1)S(1)} %collective-permute-done), kind=kOutput, calls=%fused_computation.18 | convolution fusion | flops 111149056 | bytes 6029312 | tf_op jit(solution)/shard_map/cik,ckj->cij/dot_general | solution.py:92
  25.7 2.9 %fusion.71 = (bf16[256,32,8]{2,1,0:T(8,128)(2,1)}, bf16[256,32,8]{2,1,0:T(8,128)(2,1)}) fusion(bf16[256,32,128]{2,1,0:T(8,128)(2,1)S(1)} %fusion.13), kind=kLoop, calls=%fused_computation.95 | loop fusion | bytes 524288 | tf_op jit(solution)/shard_map/slice | solution.py:16
  28.6 2.7 %copy.26 = bf16[256,32,8]{0,2,1:T(8,128)(2,1)S(1)} copy(bf16[256,32,8]{2,1,0:T(8,128)(2,1)} %get-tuple-element.2) | data formatting | bytes 262144 | tf_op jit(solution)/shard_map/slice | solution.py:16
  31.3 2.7 %copy.27 = bf16[256,32,8]{0,2,1:T(8,128)(2,1)S(1)} copy(bf16[256,32,8]{2,1,0:T(8,128)(2,1)} %get-tuple-element.3) | data formatting | bytes 262144 | tf_op jit(solution)/shard_map/slice | solution.py:15
  34.0 1.3 collective-permute-start.3
  35.3 3.0 %collective-permute-start.2 = (bf16[256,32,8]{0,2,1:T(8,128)(2,1)S(1)}, bf16[256,32,8]{0,2,1:T(8,128)(2,1)S(1)}, u32[]{:S(2)}, u32[]{:S(2)}) collective-permute-start(bf16[256,32,8]{0,2,1:T(8,128)(2,1)S(1)} %copy.26), channel_id=1, source_target_pairs={{0,1},{1,2},{2,3},{4,5},{5,6},{6,7},{8,9},{9,10},{10,11},{12,13},{... | collective-permute-start | bytes 393224 | tf_op jit(solution)/shard_map/ppermute | solution.py:19
  38.3 5.2 %convolution_convert_fusion = bf16[256,128,144]{1,0,2:T(8,128)(2,1)} fusion(s32[128,144]{0,1:T(8,128)S(1)} %iota_subtract_fusion, f32[256]{0:T(256)S(1)} %fusion.55, f32[256]{0:T(256)S(1)} %multiply_multiply_fusion.2, f32[17]{0:T(128)S(1)} %multiply_negate_fusion), kind=kOutput, calls=%fused_computation.2 | convolution fusion | flops 165477120 | bytes 9513028 | tf_op jit(solution)/shard_map/ijk,ck->cij/dot_general | solution.py:40
  43.5 3.7 %copy.28 = bf16[256,32,8]{2,1,0:T(8,128)(2,1)} copy(bf16[256,32,8]{0,2,1:T(8,128)(2,1)S(1)} %collective-permute-done.2) | data formatting | bytes 262144 | tf_op jit(solution)/shard_map/ppermute | solution.py:19
  47.2 3.7 %copy.29 = bf16[256,32,8]{2,1,0:T(8,128)(2,1)} copy(bf16[256,32,8]{0,2,1:T(8,128)(2,1)S(1)} %collective-permute-done.3) | data formatting | bytes 262144 | tf_op jit(solution)/shard_map/ppermute | solution.py:21
  50.9 16.2 %fusion.16 = bf16[256,32,128]{2,1,0:T(8,128)(2,1)} fusion(bf16[256,128,144]{1,0,2:T(8,128)(2,1)} %convolution_convert_fusion, bf16[256,32,8]{2,1,0:T(8,128)(2,1)} %copy.29, bf16[256,32,128]{2,1,0:T(8,128)(2,1)S(1)} %fusion.13, bf16[256,32,8]{2,1,0:T(8,128)(2,1)} %copy.28), kind=kOutput, calls=%fused_computation.19 | convolution fusion | flops 310116352 | bytes 13893632 | tf_op jit(solution)/shard_map/cim,cjm->cij/dot_general | solution.py:96
  67.1 2.5 %all_to_all.38 = bf16[256,2,2048]{2,1,0:T(2,128)(2,1)S(1)} reshape(bf16[256,32,128]{2,1,0:T(8,128)(2,1)} %fusion.16) | data formatting | bytes 4194304 | tf_op jit(solution)/shard_map/all_to_all | solution.py:100
  69.7 0.9 copy.31
  70.6 28.6 %all_to_all.57 = bf16[256,2,2048]{2,0,1:T(8,128)(2,1)S(1)} all-to-all(bf16[256,2,2048]{2,0,1:T(8,128)(2,1)S(1)} %copy.31), channel_id=1, replica_groups=mesh['freq'=2,'row'=4,'col'=4] {'freq'}, dimensions={1} | all-to-all | bytes 4194304 | tf_op jit(solution)/shard_map/all_to_all | solution.py:100
  99.6 10.1 %all_to_all.58 = f32[32,1,512]{2,1,0:T(1,128)S(1)} all-to-all(f32[32,1,512]{2,1,0:T(1,128)S(1)} %broadcast_in_dim.9), channel_id=1, replica_groups=mesh['freq'=2,'row'=4,'col'=4] {'freq','row','col'}, dimensions={0} | all-to-all | bytes 131072 | tf_op jit(solution)/shard_map/all_to_all | solution.py:82
  110.3 3.0 %subtract_convert_fusion = bf16[2048,512]{1,0:T(8,128)(2,1)S(1)} fusion(bf16[512,2048]{1,0:T(8,128)(2,1)} %bitcast.80, bf16[512,512]{1,0:T(8,128)(2,1)S(1)} %copy-done, f32[512]{0:T(512)S(1)} %bitcast.84), kind=kOutput, calls=%fused_computation.8 | convolution fusion | flops 1075838976 | bytes 4720640 | tf_op jit(solution)/shard_map/dot_general | solution.py:107
  113.3 1.2 fusion.22
  114.8 12.0 %all_to_all.59 = f32[32,1,2048]{2,1,0:T(1,128)S(1)} all-to-all(f32[32,1,2048]{2,1,0:T(1,128)S(1)} %all_to_all.49), channel_id=1, replica_groups=mesh['freq'=2,'row'=4,'col'=4] {'freq','row','col'}, dimensions={0} | all-to-all | bytes 524288 | tf_op jit(solution)/shard_map/all_to_all | solution.py:70
  127.1 12.5 %all_to_all.60 = f32[32,1,2048]{2,1,0:T(1,128)S(1)} all-to-all(f32[32,1,2048]{2,1,0:T(1,128)S(1)} %broadcast_in_dim.10), channel_id=1, replica_groups=mesh['freq'=2,'row'=4,'col'=4] {'freq','row','col'}, dimensions={0} | all-to-all | bytes 524288 | tf_op jit(solution)/shard_map/all_to_all | solution.py:73
  139.7 0.7 multiply_reduce_fusion.1
  140.4 1.0 multiply_reduce_fusion.3
  145.5 1.1 fusion.35
  146.9 12.6 %all_to_all.61 = f32[32,1,2048]{2,1,0:T(1,128)S(1)} all-to-all(f32[32,1,2048]{2,1,0:T(1,128)S(1)} %all_to_all.50), channel_id=1, replica_groups=mesh['freq'=2,'row'=4,'col'=4] {'freq','row','col'}, dimensions={0} | all-to-all | bytes 524288 | tf_op jit(solution)/shard_map/all_to_all | solution.py:70
  159.8 12.6 %all_to_all.62 = f32[32,1,2048]{2,1,0:T(1,128)S(1)} all-to-all(f32[32,1,2048]{2,1,0:T(1,128)S(1)} %broadcast_in_dim.11), channel_id=1, replica_groups=mesh['freq'=2,'row'=4,'col'=4] {'freq','row','col'}, dimensions={0} | all-to-all | bytes 524288 | tf_op jit(solution)/shard_map/all_to_all | solution.py:73
  172.5 0.7 multiply_reduce_fusion
  173.3 1.0 multiply_reduce_fusion.2
  178.3 1.6 convolution_convert_fusion.1
  (62 shorter events, 9.3 us)
Async XLA Ops:
  0.6 109.2 %copy-start = (bf16[512,512]{1,0:T(8,128)(2,1)S(1)}, bf16[512,512]{1,0:T(8,128)(2,1)}, u32[]{:S(2)}) copy-start(bf16[512,512]{1,0:T(8,128)(2,1)} %param.6) | copy-start | bytes 1572868
  0.6 7.6 %copy-start.4 = (f32[256]{0:T(256)S(1)}, f32[256]{0:T(256)}, u32[]{:S(2)}) copy-start(f32[256]{0:T(256)} %param.5) | copy-start | bytes 3076
  2.0 16.1 %collective-permute-start = (bf16[256,8,128]{2,1,0:T(8,128)(2,1)S(1)}, bf16[256,8,128]{2,1,0:T(8,128)(2,1)S(1)}, u32[]{:S(2)}, u32[]{:S(2)}) collective-permute-start(bf16[256,8,128]{2,1,0:T(8,128)(2,1)S(1)} %get-tuple-element.4), channel_id=1, source_target_pairs={{0,4},{4,8},{8,12},{1,5},{5,9},{9,13},{2,6},{6,10},{10,14},{3,7},{... | collective-permute-start | bytes 1572872 | tf_op jit(solution)/shard_map/ppermute | solution.py:19
  7.0 15.4 %collective-permute-start.1 = (bf16[256,8,128]{2,1,0:T(8,128)(2,1)S(1)}, bf16[256,8,128]{2,1,0:T(8,128)(2,1)}, u32[]{:S(2)}, u32[]{:S(2)}) collective-permute-start(bf16[256,8,128]{2,1,0:T(8,128)(2,1)S(1)} %get-tuple-element.5), channel_id=1, source_target_pairs={{4,0},{8,4},{12,8},{5,1},{9,5},{13,9},{6,2},{10,6},{14,10},{7,3},{... | collective-permute-start | bytes 1572872 | tf_op jit(solution)/shard_map/ppermute | solution.py:21
  34.0 13.3 %collective-permute-start.3 = (bf16[256,32,8]{0,2,1:T(8,128)(2,1)S(1)}, bf16[256,32,8]{0,2,1:T(8,128)(2,1)S(1)}, u32[]{:S(2)}, u32[]{:S(2)}) collective-permute-start(bf16[256,32,8]{0,2,1:T(8,128)(2,1)S(1)} %copy.27), channel_id=1, source_target_pairs={{1,0},{2,1},{3,2},{5,4},{6,5},{7,6},{9,8},{10,9},{11,10},{13,12},{... | collective-permute-start | bytes 393224 | tf_op jit(solution)/shard_map/ppermute | solution.py:21
  35.3 8.2 %collective-permute-start.2 = (bf16[256,32,8]{0,2,1:T(8,128)(2,1)S(1)}, bf16[256,32,8]{0,2,1:T(8,128)(2,1)S(1)}, u32[]{:S(2)}, u32[]{:S(2)}) collective-permute-start(bf16[256,32,8]{0,2,1:T(8,128)(2,1)S(1)} %copy.26), channel_id=1, source_target_pairs={{0,1},{1,2},{2,3},{4,5},{5,6},{6,7},{8,9},{9,10},{10,11},{12,13},{... | collective-permute-start | bytes 393224 | tf_op jit(solution)/shard_map/ppermute | solution.py:19
  99.2 11.1 %copy-start.1 = (bf16[256,2,2048]{2,0,1:T(8,128)(2,1)}, bf16[256,2,2048]{2,0,1:T(8,128)(2,1)S(1)}, u32[]{:S(2)}) copy-start(bf16[256,2,2048]{2,0,1:T(8,128)(2,1)S(1)} %all_to_all.57) | copy-start | bytes 6291460
  110.3 3.0 %copy-start.2 = (f32[128,512]{1,0:T(8,128)S(1)}, f32[128,512]{1,0:T(8,128)}, u32[]{:S(2)}) copy-start(f32[128,512]{1,0:T(8,128)} %param.7) | copy-start | bytes 786436
  178.3 1.6 copy-start.3

commit v2 on v1

--- a/solution.py
+++ b/solution.py
@@ -97,15 +97,33 @@
         "cim,cjm->cij", widened, band_cols, preferred_element_type=jnp.float32
     ).astype(jnp.bfloat16)
     flattened = smoothed.reshape(channels, height * breadth)
-    spectra = lax.all_to_all(flattened, "freq", split_axis=1, concat_axis=0, tiled=True)
-    devices = lax.axis_size("freq") * lax.axis_size("row") * lax.axis_size("col")
-    total_pixels = spectra.shape[1] * devices
-    channel_sums = gathered_sum(jnp.sum(spectra, axis=1, dtype=jnp.float32), ("freq", "row", "col"))
-    means = channel_sums / total_pixels
-    shift = jnp.dot(whitening.astype(jnp.float32), means, precision=lax.Precision.HIGHEST)
-    whitened = (
-        jnp.dot(whitening, spectra, preferred_element_type=jnp.float32) - shift[:, None]
-    ).astype(jnp.bfloat16)
+    parts = lax.axis_size("freq")
+    devices = parts * lax.axis_size("row") * lax.axis_size("col")
+    block = height * breadth // parts
+    total_pixels = block * devices
+    if parts == 2:
+        side = lax.axis_index("freq")
+        outgoing = lax.dynamic_slice_in_dim(flattened, (1 - side) * block, block, axis=1)
+        incoming = lax.ppermute(outgoing, "freq", [(0, 1), (1, 0)])
+        local = lax.dynamic_slice_in_dim(flattened, side * block, block, axis=1)
+        plane_sums = jnp.sum(flattened, axis=1, dtype=jnp.float32)
+        placed = jnp.zeros((parts * channels,), jnp.float32)
+        placed = lax.dynamic_update_slice_in_dim(placed, plane_sums, side * channels, axis=0)
+        channel_sums = gathered_sum(placed, ("freq", "row", "col"))
+        means = channel_sums / total_pixels
+        shift = jnp.dot(whitening.astype(jnp.float32), means, precision=lax.Precision.HIGHEST)
+        mine = lax.dynamic_slice_in_dim(whitening, side * channels, channels, axis=1)
+        theirs = lax.dynamic_slice_in_dim(whitening, (1 - side) * channels, channels, axis=1)
+        mixed = jnp.dot(mine, local, preferred_element_type=jnp.float32) + jnp.dot(
+            theirs, incoming, preferred_element_type=jnp.float32
+        )
+    else:
+        spectra = lax.all_to_all(flattened, "freq", split_axis=1, concat_axis=0, tiled=True)
+        channel_sums = gathered_sum(jnp.sum(spectra, axis=1, dtype=jnp.float32), ("freq", "row", "col"))
+        means = channel_sums / total_pixels
+        shift = jnp.dot(whitening.astype(jnp.float32), means, precision=lax.Precision.HIGHEST)
+        mixed = jnp.dot(whitening, spectra, preferred_element_type=jnp.float32)
+    whitened = (mixed - shift[:, None]).astype(jnp.bfloat16)
     unmixing = unmix_init
     for iteration in range(ITERS):
         moments = pixel_moments(unmixing.astype(jnp.bfloat16), whitened)

time: 180 us -> 169 us (0.939)
  blocking collectives: 88.6 us -> 51.9 us
  waiting for transfers between devices: 9.66 us -> 26.1 us
  starting transfers between devices: 10.6 us -> 17.2 us
  matrix products: 40.9 us -> 44.1 us
    all_to_all x2 -> x0, blocking collectives: 38.8 us -> none  [the longest x1 28.6 us: shards(): lax.all_to_all(flattened, 'freq', split_axis=1, concat_axis=0, tiled=True)]
    all_to_all x0 -> x1, waiting for transfers between devices: none -> 16.6 us  [gathered_sum(): gathered = lax.all_to_all(spread, axes, 0, 0, tiled=True)]
    all_to_all x0 -> x1, starting transfers between devices: none -> 6.86 us  [gathered_sum(): gathered = lax.all_to_all(spread, axes, 0, 0, tiled=True)]
    all_to_all x2 -> x0, local copies, waits for them, and re-layouts: 3.43 us -> none  [shards(): lax.all_to_all(flattened, 'freq', split_axis=1, concat_axis=0, tiled=True)]
    dot_general x1 -> x2, matrix products: 2.96 us -> 5.99 us  [the longest x1 3.34 us: shards(): jnp.dot(theirs, incoming, preferred_element_type=jnp.float32)]
    all_to_all x2, blocking collectives: 24.6 us -> 26.6 us  [total_sum(): pieces = lax.all_to_all(flat, axes, 0, 0, tiled=True)]
  transfers between devices with their start and end apart: 4 -> 6, of which waited for: 2 -> 3; matrix products, arithmetic and copies ran while one was open for 7% -> 12% of each run, Pallas kernels for 0% -> 0%
where the time goes in v2:
time: 169 us
  blocking collectives  51.9 us (31%)
  matrix products  44.1 us (26%)
  waiting for transfers between devices  26.1 us (15%)
  local copies, waits for them, and re-layouts  25 us (15%)
  starting transfers between devices  17.2 us (10%)
  between operations  2.6 us (2%)
  other arithmetic  2.1 us (1%)
    all_to_all x2, blocking collectives, total_sum(): pieces = lax.all_to_all(flat, axes, 0, 0, tiled=True)  26.6 us
    all_to_all x2, blocking collectives, total_sum(): gathered = lax.all_to_all(spread, axes, 0, 0, tiled=True)  25.3 us
    all_to_all x1, waiting for transfers between devices, gathered_sum(): gathered = lax.all_to_all(spread, axes, 0, 0, tiled=True)  16.6 us
    dot_general x1, matrix products, shards(): jnp.einsum('cim,cjm->cij', widened, band_cols, preferred_element_type=jnp...  15.8 us
    slice x3, local copies, waits for them, and re-layouts, with_halo(): lax.slice_in_dim(cells, cells.shape[dim] - width, cells.shape[dim], axis=...  6.9 us
    all_to_all x1, starting transfers between devices, gathered_sum(): gathered = lax.all_to_all(spread, axes, 0, 0, tiled=True)  6.86 us
    ppermute x2, starting transfers between devices, with_halo(): lax.ppermute(tail, axis, [(i, (i + 1) % count) for i in range(ends)])  6.26 us
    dot_general x2, matrix products, make_band(): jnp.einsum('ijk,ck->cij', onehot, beam_taps.astype(jnp.float32))  5.63 us
  transfers between devices with their start and end apart: 6, of which 3 were waited for; matrix products, arithmetic and copies ran while one was open for 12% of the time, Pallas kernels for 0%

profile of v2, /device:TPU:0, one launch (start us, length us, event | category | flops | bytes accessed | tf_op | source)
XLA Modules:
  0.0 168.8 jit_solution(9429865616960918272)
XLA Ops:
  0.7 1.3 fusion.78
  2.0 5.0 %collective-permute-start = (bf16[256,8,128]{2,1,0:T(8,128)(2,1)S(1)}, bf16[256,8,128]{2,1,0:T(8,128)(2,1)S(1)}, u32[]{:S(2)}, u32[]{:S(2)}) collective-permute-start(bf16[256,8,128]{2,1,0:T(8,128)(2,1)S(1)} %get-tuple-element.4), channel_id=1, source_target_pairs={{0,4},{4,8},{8,12},{1,5},{5,9},{9,13},{2,6},{6,10},{10,14},{3,7},{... | collective-permute-start | bytes 1572872 | tf_op jit(solution)/shard_map/ppermute | solution.py:19
  7.0 1.3 collective-permute-start.1
  8.9 3.8 %copy.21 = bf16[256,32,48]{2,1,0:T(8,128)(2,1)} copy(bf16[256,32,48]{0,2,1:T(8,128)(2,1)S(1)} %convolution_convert_fusion.2) | data formatting | bytes 1572864 | tf_op jit(solution)/shard_map/convert_element_type | solution.py:40
  12.9 5.2 %collective-permute-done = bf16[256,8,128]{2,1,0:T(8,128)(2,1)S(1)} collective-permute-done((bf16[256,8,128]{2,1,0:T(8,128)(2,1)S(1)}, bf16[256,8,128]{2,1,0:T(8,128)(2,1)S(1)}, u32[]{:S(2)}, u32[]{:S(2)}) %collective-permute-start) | collective-permute-done | bytes 524320 | tf_op jit(solution)/shard_map/ppermute | solution.py:19
  18.1 4.3 %collective-permute-done.1 = bf16[256,8,128]{2,1,0:T(8,128)(2,1)} collective-permute-done((bf16[256,8,128]{2,1,0:T(8,128)(2,1)S(1)}, bf16[256,8,128]{2,1,0:T(8,128)(2,1)}, u32[]{:S(2)}, u32[]{:S(2)}) %collective-permute-start.1) | collective-permute-done | bytes 524320 | tf_op jit(solution)/shard_map/ppermute | solution.py:21
  22.4 3.3 %fusion.13 = bf16[256,32,128]{2,1,0:T(8,128)(2,1)S(1)} fusion(bf16[256,32,48]{2,1,0:T(8,128)(2,1)} %copy.21, bf16[256,8,128]{2,1,0:T(8,128)(2,1)} %collective-permute-done.1, bf16[256,32,128]{2,1,0:T(8,128)(2,1)} %param.4, bf16[256,8,128]{2,1,0:T(8,128)(2,1)S(1)} %collective-permute-done), kind=kOutput, calls=%fused_computation.19 | convolution fusion | flops 111149056 | bytes 6029312 | tf_op jit(solution)/shard_map/cik,ckj->cij/dot_general | solution.py:92
  25.7 2.9 %fusion.77 = (bf16[256,32,8]{2,1,0:T(8,128)(2,1)}, bf16[256,32,8]{2,1,0:T(8,128)(2,1)}) fusion(bf16[256,32,128]{2,1,0:T(8,128)(2,1)S(1)} %fusion.13), kind=kLoop, calls=%fused_computation.103 | loop fusion | bytes 524288 | tf_op jit(solution)/shard_map/slice | solution.py:16
  28.6 2.7 %copy.22 = bf16[256,32,8]{0,2,1:T(8,128)(2,1)S(1)} copy(bf16[256,32,8]{2,1,0:T(8,128)(2,1)} %get-tuple-element.2) | data formatting | bytes 262144 | tf_op jit(solution)/shard_map/slice | solution.py:16
  31.3 1.3 collective-permute-start.2
  32.6 2.7 %copy.23 = bf16[256,32,8]{0,2,1:T(8,128)(2,1)S(1)} copy(bf16[256,32,8]{2,1,0:T(8,128)(2,1)} %get-tuple-element.3) | data formatting | bytes 262144 | tf_op jit(solution)/shard_map/slice | solution.py:15
  35.3 1.3 collective-permute-start.3
  36.6 5.2 %convolution_convert_fusion = bf16[256,128,144]{1,0,2:T(8,128)(2,1)} fusion(pred[128,144,17]{0,1,2:T(8,128)(4,1)S(1)} %iota_compare_fusion, f32[256]{0:T(256)S(1)} %fusion.59, f32[256]{0:T(256)S(1)} %multiply_multiply_fusion.2, f32[17]{0:T(128)S(1)} %multiply_negate_fusion), kind=kOutput, calls=%fused_computation.2 | convolution fusion | flops 165163776 | bytes 9752644 | tf_op jit(solution)/shard_map/ijk,ck->cij/dot_general | solution.py:40
  41.8 3.7 %copy.24 = bf16[256,32,8]{2,1,0:T(8,128)(2,1)} copy(bf16[256,32,8]{0,2,1:T(8,128)(2,1)S(1)} %collective-permute-done.2) | data formatting | bytes 262144 | tf_op jit(solution)/shard_map/ppermute | solution.py:19
  45.5 3.7 %copy.25 = bf16[256,32,8]{2,1,0:T(8,128)(2,1)} copy(bf16[256,32,8]{0,2,1:T(8,128)(2,1)S(1)} %collective-permute-done.3) | data formatting | bytes 262144 | tf_op jit(solution)/shard_map/ppermute | solution.py:21
  49.2 15.8 %convert_reduce_fusion = (f32[256]{0:T(256)S(1)}, bf16[256,32,128]{2,1,0:T(8,128)(2,1)S(1)}) fusion(bf16[256,128,144]{1,0,2:T(8,128)(2,1)} %convolution_convert_fusion, bf16[256,32,8]{2,1,0:T(8,128)(2,1)} %copy.25, bf16[256,32,128]{2,1,0:T(8,128)(2,1)S(1)} %fusion.13, bf16[256,32,8]{2,1,0:T(8,128)(2,1)} %copy.24), kind=kOutput, calls=%fused_computation.9 | convolution fusion | flops 312213248 | bytes 13894656 | tf_op jit(solution)/shard_map/cim,cjm->cij/dot_general | solution.py:96
  65.0 1.0 copy.42
  66.0 1.1 constant_dynamic-slice_fusion
  67.0 1.5 collective-permute-start.4
  69.5 6.9 %all-to-all-start = ((f32[32,1,512]{2,1,0:T(1,128)}), f32[32,1,512]{2,1,0:T(1,128)S(1)}, u32[]{:S(2)}, u32[]{:S(2)}) async-start(f32[32,1,512]{2,1,0:T(1,128)} %broadcast_in_dim.6), calls=%async_computation | async-start | bytes 131072 | tf_op jit(solution)/shard_map/all_to_all | solution.py:82
  76.4 2.7 %fusion.35 = f32[512,2048]{1,0:T(8,128)} fusion(bf16[256,4096]{1,0:T(8,128)(2,1)S(1)} %bitcast.78, s32[]{:T(128)S(6)} %select_n.14, bf16[512,512]{1,0:T(8,128)(2,1)S(1)} %copy-done, s32[]{:T(128)S(6)} %select_n.13), kind=kOutput, calls=%fused_computation.51 | convolution fusion | flops 536870912 | bytes 5505032 | tf_op jit(solution)/shard_map/dot_general | solution.py:117
  79.1 16.6 %all-to-all-done = f32[32,1,512]{2,1,0:T(1,128)S(1)} async-done(((f32[32,1,512]{2,1,0:T(1,128)}), f32[32,1,512]{2,1,0:T(1,128)S(1)}, u32[]{:S(2)}, u32[]{:S(2)}) %all-to-all-start) | async-done | bytes 65568 | tf_op jit(solution)/shard_map/all_to_all | solution.py:82
  96.2 3.3 %subtract_convert_fusion = bf16[512,2048]{1,0:T(8,128)(2,1)S(1)} fusion(f32[512,2048]{1,0:T(8,128)} %fusion.35, bf16[256,2048]{1,0:T(8,128)(2,1)} %collective-permute-done.4, f32[512]{0:T(512)S(1)} %bitcast.80, bf16[512,512]{1,0:T(8,128)(2,1)S(1)} %copy-done, s32[]{:T(128)S(6)} %select_n.15), kind=kOutput, calls=%fused_computation.8 | convolution fusion | flops 540016640 | bytes 7604228 | tf_op jit(solution)/shard_map/dot_general | solution.py:117
  99.6 2.1 %fusion.23 = f32[128,512]{1,0:T(8,128)S(1)} fusion(bf16[512,2048]{1,0:T(8,128)(2,1)S(1)} %subtract_convert_fusion, f32[128,512]{1,0:T(8,128)S(1)} %copy-done.1), kind=kOutput, calls=%fused_computation.27 | convolution fusion | flops 537722880 | bytes 2621440 | tf_op jit(solution)/shard_map/dot_general | solution.py:60
  102.0 14.0 %all_to_all.38 = f32[32,1,2048]{2,1,0:T(1,128)S(1)} all-to-all(f32[32,1,2048]{2,1,0:T(1,128)S(1)} %all_to_all.31), channel_id=1, replica_groups=mesh['freq'=2,'row'=4,'col'=4] {'freq','row','col'}, dimensions={0} | all-to-all | bytes 524288 | tf_op jit(solution)/shard_map/all_to_all | solution.py:70
  116.3 12.6 %all_to_all.39 = f32[32,1,2048]{2,1,0:T(1,128)S(1)} all-to-all(f32[32,1,2048]{2,1,0:T(1,128)S(1)} %broadcast_in_dim.7), channel_id=1, replica_groups=mesh['freq'=2,'row'=4,'col'=4] {'freq','row','col'}, dimensions={0} | all-to-all | bytes 524288 | tf_op jit(solution)/shard_map/all_to_all | solution.py:73
  129.7 1.0 multiply_reduce_fusion.3
  134.7 1.1 fusion.37
  136.2 12.6 %all_to_all.40 = f32[32,1,2048]{2,1,0:T(1,128)S(1)} all-to-all(f32[32,1,2048]{2,1,0:T(1,128)S(1)} %all_to_all.32), channel_id=1, replica_groups=mesh['freq'=2,'row'=4,'col'=4] {'freq','row','col'}, dimensions={0} | all-to-all | bytes 524288 | tf_op jit(solution)/shard_map/all_to_all | solution.py:70
  149.1 12.6 %all_to_all.41 = f32[32,1,2048]{2,1,0:T(1,128)S(1)} all-to-all(f32[32,1,2048]{2,1,0:T(1,128)S(1)} %broadcast_in_dim.8), channel_id=1, replica_groups=mesh['freq'=2,'row'=4,'col'=4] {'freq','row','col'}, dimensions={0} | all-to-all | bytes 524288 | tf_op jit(solution)/shard_map/all_to_all | solution.py:73
  162.5 1.0 multiply_reduce_fusion.2
  167.6 1.2 convolution_convert_fusion.1
  (64 shorter events, 11.5 us)
Async XLA Ops:
  0.6 75.8 %copy-start = (bf16[512,512]{1,0:T(8,128)(2,1)S(1)}, bf16[512,512]{1,0:T(8,128)(2,1)}, u32[]{:S(2)}) copy-start(bf16[512,512]{1,0:T(8,128)(2,1)} %param.6) | copy-start | bytes 1572868
  0.6 7.7 %copy-start.3 = (f32[256]{0:T(256)S(1)}, f32[256]{0:T(256)}, u32[]{:S(2)}) copy-start(f32[256]{0:T(256)} %param.5) | copy-start | bytes 3076
  2.0 16.1 %collective-permute-start = (bf16[256,8,128]{2,1,0:T(8,128)(2,1)S(1)}, bf16[256,8,128]{2,1,0:T(8,128)(2,1)S(1)}, u32[]{:S(2)}, u32[]{:S(2)}) collective-permute-start(bf16[256,8,128]{2,1,0:T(8,128)(2,1)S(1)} %get-tuple-element.4), channel_id=1, source_target_pairs={{0,4},{4,8},{8,12},{1,5},{5,9},{9,13},{2,6},{6,10},{10,14},{3,7},{... | collective-permute-start | bytes 1572872 | tf_op jit(solution)/shard_map/ppermute | solution.py:19
  7.0 15.4 %collective-permute-start.1 = (bf16[256,8,128]{2,1,0:T(8,128)(2,1)S(1)}, bf16[256,8,128]{2,1,0:T(8,128)(2,1)}, u32[]{:S(2)}, u32[]{:S(2)}) collective-permute-start(bf16[256,8,128]{2,1,0:T(8,128)(2,1)S(1)} %get-tuple-element.5), channel_id=1, source_target_pairs={{4,0},{8,4},{12,8},{5,1},{9,5},{13,9},{6,2},{10,6},{14,10},{7,3},{... | collective-permute-start | bytes 1572872 | tf_op jit(solution)/shard_map/ppermute | solution.py:21
  31.3 10.5 %collective-permute-start.2 = (bf16[256,32,8]{0,2,1:T(8,128)(2,1)S(1)}, bf16[256,32,8]{0,2,1:T(8,128)(2,1)S(1)}, u32[]{:S(2)}, u32[]{:S(2)}) collective-permute-start(bf16[256,32,8]{0,2,1:T(8,128)(2,1)S(1)} %copy.22), channel_id=1, source_target_pairs={{0,1},{1,2},{2,3},{4,5},{5,6},{6,7},{8,9},{9,10},{10,11},{12,13},{... | collective-permute-start | bytes 393224 | tf_op jit(solution)/shard_map/ppermute | solution.py:19
  35.3 10.2 %collective-permute-start.3 = (bf16[256,32,8]{0,2,1:T(8,128)(2,1)S(1)}, bf16[256,32,8]{0,2,1:T(8,128)(2,1)S(1)}, u32[]{:S(2)}, u32[]{:S(2)}) collective-permute-start(bf16[256,32,8]{0,2,1:T(8,128)(2,1)S(1)} %copy.23), channel_id=1, source_target_pairs={{1,0},{2,1},{3,2},{5,4},{6,5},{7,6},{9,8},{10,9},{11,10},{13,12},{... | collective-permute-start | bytes 393224 | tf_op jit(solution)/shard_map/ppermute | solution.py:21
  67.0 29.2 %collective-permute-start.4 = (bf16[256,2048]{1,0:T(8,128)(2,1)}, bf16[256,2048]{1,0:T(8,128)(2,1)}, u32[]{:S(2)}, u32[]{:S(2)}) collective-permute-start(bf16[256,2048]{1,0:T(8,128)(2,1)} %constant_dynamic-slice_fusion), channel_id=1, source_target_pairs={{0,16},{16,0},{1,17},{17,1},{2,18},{18,2},{3,19},{19,3},{4,20},{20... | collective-permute-start | bytes 3145736 | tf_op jit(solution)/shard_map/ppermute | solution.py:107
  69.5 26.1 %all-to-all-start = ((f32[32,1,512]{2,1,0:T(1,128)}), f32[32,1,512]{2,1,0:T(1,128)S(1)}, u32[]{:S(2)}, u32[]{:S(2)}) async-start(f32[32,1,512]{2,1,0:T(1,128)} %broadcast_in_dim.6), calls=%async_computation | async-start | bytes 131072 | tf_op jit(solution)/shard_map/all_to_all | solution.py:82
  96.2 3.4 %copy-start.1 = (f32[128,512]{1,0:T(8,128)S(1)}, f32[128,512]{1,0:T(8,128)}, u32[]{:S(2)}) copy-start(f32[128,512]{1,0:T(8,128)} %param.7) | copy-start | bytes 786436
  167.6 1.3 copy-start.2

commit v3 on v2

--- a/solution.py
+++ b/solution.py
@@ -23,6 +23,32 @@
             axis=dim,
         )
     return cells
+
+
+def corner(cells, rows, cols, step_row, step_col):
+    tall = lax.axis_size("row")
+    wide = lax.axis_size("col")
+    pairs = []
+    for a in range(tall):
+        for b in range(wide):
+            if 0 <= a + step_row < tall and 0 <= b + step_col < wide:
+                pairs.append((a * wide + b, (a + step_row) * wide + b + step_col))
+    return lax.ppermute(cells[:, rows, cols], ("row", "col"), pairs)
+
+
+def with_frame(cells, width):
+    height, breadth = cells.shape[1], cells.shape[2]
+    top, bottom = slice(0, width), slice(height - width, height)
+    left, right = slice(0, width), slice(breadth - width, breadth)
+    rows = with_halo(cells, (("row", 1),), width)
+    sides = with_halo(cells, (("col", 2),), width)
+    upper = jnp.concatenate(
+        [corner(cells, bottom, right, 1, 1), rows[:, :width], corner(cells, bottom, left, 1, -1)], axis=2
+    )
+    lower = jnp.concatenate(
+        [corner(cells, top, right, -1, 1), rows[:, -width:], corner(cells, top, left, -1, -1)], axis=2
+    )
+    return jnp.concatenate([upper, sides, lower], axis=1)
 
 
 def make_taps(beam_sigma):
@@ -88,11 +114,10 @@
     channels, height, breadth = sky_maps.shape
     band_rows = make_band(beam_taps, height)
     band_cols = make_band(beam_taps, breadth)
-    padded = with_halo(sky_maps, (("row", 1),), HALF)
-    rowwise = jnp.einsum(
-        "cik,ckj->cij", band_rows, padded, preferred_element_type=jnp.float32
+    framed = with_frame(sky_maps, HALF)
+    widened = jnp.einsum(
+        "cik,ckj->cij", band_rows, framed, preferred_element_type=jnp.float32
     ).astype(jnp.bfloat16)
-    widened = with_halo(rowwise, (("col", 2),), HALF)
     smoothed = jnp.einsum(
         "cim,cjm->cij", widened, band_cols, preferred_element_type=jnp.float32
     ).astype(jnp.bfloat16)

time: 169 us -> 187 us (1.11)
  starting transfers between devices: 17.2 us -> 23.4 us
  local copies, waits for them, and re-layouts: 25 us -> 30.5 us
  waiting for transfers between devices: 26.1 us -> 30.1 us
  matrix products: 44.1 us -> 47.2 us
    ppermute x0 -> x4, waiting for transfers between devices: none -> 11 us  [corner(): return lax.ppermute(cells[:, rows, cols], ('row', 'col'), pairs)]
    ppermute x0 -> x4, starting transfers between devices: none -> 9.57 us  [corner(): return lax.ppermute(cells[:, rows, cols], ('row', 'col'), pairs)]
    unnamed x9 -> x17, local copies, waits for them, and re-layouts: 1.02 us -> 9.29 us
    dot_general x1, matrix products: 15.8 us -> 22.3 us  [shards(): jnp.einsum('cim,cjm->cij', widened, band_cols, preferred_element_type=jnp...]
    ppermute x2, waiting for transfers between devices: 5.23 us -> 0.01 us  [with_halo(): lax.ppermute(tail, axis, [(i, (i + 1) % count) for i in range(ends)])]
    ppermute x2, waiting for transfers between devices: 4.25 us -> 0.01 us  [with_halo(): lax.ppermute(head, axis, [((i + 1) % count, i) for i in range(ends)])]
    all_to_all x1, starting transfers between devices: 6.86 us -> 2.79 us  [gathered_sum(): gathered = lax.all_to_all(spread, axes, 0, 0, tiled=True)]
    dot_general x1 -> x0, matrix products: 3.32 us -> none  [shards(): jnp.einsum('cik,ckj->cij', band_rows, padded, preferred_element_type=jnp....]
  transfers between devices with their start and end apart: 6 -> 10, of which waited for: 3 -> 2; matrix products, arithmetic and copies ran while one was open for 12% -> 17% of each run, Pallas kernels for 0% -> 0%
where the time goes in v3:
time: 187 us
  blocking collectives  50.6 us (27%)
  matrix products  47.2 us (25%)
  local copies, waits for them, and re-layouts  30.5 us (16%)
  waiting for transfers between devices  30.1 us (16%)
  starting transfers between devices  23.4 us (13%)
  between operations  2.59 us (1%)
  other arithmetic  2.1 us (1%)
    all_to_all x2, blocking collectives, total_sum(): pieces = lax.all_to_all(flat, axes, 0, 0, tiled=True)  25.4 us
    all_to_all x2, blocking collectives, total_sum(): gathered = lax.all_to_all(spread, axes, 0, 0, tiled=True)  25.3 us
    dot_general x1, matrix products, shards(): jnp.einsum('cim,cjm->cij', widened, band_cols, preferred_element_type=jnp...  22.3 us
    all_to_all x1, waiting for transfers between devices, gathered_sum(): gathered = lax.all_to_all(spread, axes, 0, 0, tiled=True)  19.1 us
    ppermute x4, waiting for transfers between devices, corner(): return lax.ppermute(cells[:, rows, cols], ('row', 'col'), pairs)  11 us
    ppermute x4, starting transfers between devices, corner(): return lax.ppermute(cells[:, rows, cols], ('row', 'col'), pairs)  9.57 us
    unnamed x17, local copies, waits for them, and re-layouts  9.29 us
    ppermute x2, starting transfers between devices, with_halo(): lax.ppermute(tail, axis, [(i, (i + 1) % count) for i in range(ends)])  7.01 us
  transfers between devices with their start and end apart: 10, of which 2 were waited for; matrix products, arithmetic and copies ran while one was open for 17% of the time, Pallas kernels for 0%

profile of v3, /device:TPU:0, one launch (start us, length us, event | category | flops | bytes accessed | tf_op | source)
XLA Modules:
  0.0 186.6 jit_solution(16613095350194418964)
XLA Ops:
  0.7 3.2 %fusion.86 = (bf16[256,8,8]{2,1,0:T(8,128)(2,1)S(1)}, bf16[256,8,8]{2,1,0:T(8,128)(2,1)}, bf16[256,8,8]{2,1,0:T(8,128)(2,1)}, bf16[256,8,8]{2,1,0:T(8,128)(2,1)}) fusion(bf16[256,32,128]{2,1,0:T(8,128)(2,1)} %param.4), kind=kLoop, calls=%fused_computation.109 | loop fusion | bytes 262144 | tf_op jit(solution)/shard_map/slice | solution.py:36
  3.8 5.2 %collective-permute-start = (bf16[256,8,8]{2,1,0:T(8,128)(2,1)S(1)}, bf16[256,8,8]{2,1,0:T(8,128)(2,1)}, u32[]{:S(2)}, u32[]{:S(2)}) collective-permute-start(bf16[256,8,8]{2,1,0:T(8,128)(2,1)S(1)} %get-tuple-element.2), channel_id=1, source_target_pairs={{0,5},{1,6},{2,7},{4,9},{5,10},{6,11},{8,13},{9,14},{10,15},{16,21... | collective-permute-start | bytes 98312 | tf_op jit(solution)/shard_map/ppermute | solution.py:36
  9.0 2.9 %fusion.88 = (bf16[256,32,8]{2,1,0:T(8,128)(2,1)}, bf16[256,32,8]{2,1,0:T(8,128)(2,1)}) fusion(bf16[256,32,128]{2,1,0:T(8,128)(2,1)S(1)} %copy-done.1), kind=kLoop, calls=%fused_computation.111 | loop fusion | bytes 524288 | tf_op jit(solution)/shard_map/slice | solution.py:16
  11.9 3.3 %copy.32 = bf16[256,32,8]{0,2,1:T(8,128)(2,1)} copy(bf16[256,32,8]{2,1,0:T(8,128)(2,1)} %get-tuple-element.8) | data formatting | bytes 262144
  15.2 3.5 %collective-permute-start.3 = (bf16[256,32,8]{0,2,1:T(8,128)(2,1)}, bf16[256,32,8]{0,2,1:T(8,128)(2,1)S(1)}, u32[]{:S(2)}, u32[]{:S(2)}) collective-permute-start(bf16[256,32,8]{0,2,1:T(8,128)(2,1)} %copy.32), channel_id=1, source_target_pairs={{0,1},{1,2},{2,3},{4,5},{5,6},{6,7},{8,9},{9,10},{10,11},{12,13},{... | collective-permute-start | bytes 393224 | tf_op jit(solution)/shard_map/ppermute | solution.py:19
  18.8 2.7 %copy.33 = bf16[256,32,8]{0,2,1:T(8,128)(2,1)S(1)} copy(bf16[256,32,8]{2,1,0:T(8,128)(2,1)} %get-tuple-element.9) | data formatting | bytes 262144
  21.5 1.3 collective-permute-start.4
  22.8 1.1 fusion.87
  23.8 3.5 %collective-permute-start.1 = (bf16[256,8,128]{2,1,0:T(8,128)(2,1)}, bf16[256,8,128]{2,1,0:T(8,128)(2,1)}, u32[]{:S(2)}, u32[]{:S(2)}) collective-permute-start(bf16[256,8,128]{2,1,0:T(8,128)(2,1)} %get-tuple-element.6), channel_id=1, source_target_pairs={{0,4},{4,8},{8,12},{1,5},{5,9},{9,13},{2,6},{6,10},{10,14},{3,7},{... | collective-permute-start | bytes 1572872 | tf_op jit(solution)/shard_map/ppermute | solution.py:19
  27.3 1.3 collective-permute-start.6
  28.9 5.2 %convolution_convert_fusion = bf16[256,128,144]{1,0,2:T(8,128)(2,1)} fusion(pred[128,144,17]{0,1,2:T(8,128)(4,1)S(1)} %iota_compare_fusion, f32[256]{0:T(256)S(1)} %fusion.68, f32[256]{0:T(256)S(1)} %multiply_multiply_fusion.2, f32[17]{0:T(128)S(1)} %multiply_negate_fusion), kind=kOutput, calls=%fused_computation.2 | convolution fusion | flops 165163776 | bytes 9752644 | tf_op jit(solution)/shard_map/ijk,ck->cij/dot_general | solution.py:66
  34.1 1.4 collective-permute-start.2
  35.6 1.5 collective-permute-start.5
  37.7 1.5 collective-permute-start.7
  39.6 3.8 %copy.25 = bf16[256,32,48]{2,1,0:T(8,128)(2,1)} copy(bf16[256,32,48]{0,2,1:T(8,128)(2,1)S(1)} %convolution_convert_fusion.2) | data formatting | bytes 1572864 | tf_op jit(solution)/shard_map/convert_element_type | solution.py:66
  43.4 3.7 %copy.23 = bf16[256,32,8]{2,1,0:T(8,128)(2,1)} copy(bf16[256,32,8]{0,2,1:T(8,128)(2,1)S(1)} %collective-permute-done.3) | data formatting | bytes 262144 | tf_op jit(solution)/shard_map/ppermute | solution.py:19
  47.1 3.7 %copy.24 = bf16[256,32,8]{2,1,0:T(8,128)(2,1)} copy(bf16[256,32,8]{0,2,1:T(8,128)(2,1)S(1)} %copy-done.5) | data formatting | bytes 262144 | tf_op jit(solution)/shard_map/ppermute | solution.py:21
  50.8 11.0 %collective-permute-done.7 = bf16[256,8,8]{2,1,0:T(8,128)(2,1)} collective-permute-done((bf16[256,8,8]{2,1,0:T(8,128)(2,1)}, bf16[256,8,8]{2,1,0:T(8,128)(2,1)}, u32[]{:S(2)}, u32[]{:S(2)}) %collective-permute-start.7) | collective-permute-done | bytes 32800 | tf_op jit(solution)/shard_map/ppermute | solution.py:36
  61.8 22.3 %convert_reduce_fusion = (f32[256]{0:T(256)S(1)}, bf16[256,32,128]{2,1,0:T(8,128)(2,1)}) fusion(bf16[256,128,144]{1,0,2:T(8,128)(2,1)} %convolution_convert_fusion, bf16[256,32,48]{2,1,0:T(8,128)(2,1)} %copy.25, bf16[256,8,8]{2,1,0:T(8,128)(2,1)} %collective-permute-done.7, bf16[256,8,128]{2,1,0:T(8,128)(2,1)} %collective-permute-done.6, ...), kind=kOutput, calls=%fused_computation.22 | convolution fusion | flops 451411712 | bytes 15860736 | tf_op jit(solution)/shard_map/cim,cjm->cij/dot_general | solution.py:121
  84.1 2.6 %copy.44 = bf16[32,8,32,128]{3,1,2,0:T(8,128)(2,1)S(1)} copy(bf16[32,8,32,128]{3,2,1,0:T(8,128)(2,1)} %bitcast.79) | data formatting | bytes 4194304
  87.7 1.5 collective-permute-start.8
  90.0 2.8 %all-to-all-start = ((f32[32,1,512]{2,1,0:T(1,128)}), f32[32,1,512]{2,1,0:T(1,128)S(1)}, u32[]{:S(2)}, u32[]{:S(2)}) async-start(f32[32,1,512]{2,1,0:T(1,128)} %broadcast_in_dim.6), calls=%async_computation | async-start | bytes 131072 | tf_op jit(solution)/shard_map/all_to_all | solution.py:108
  92.8 2.7 %fusion.44 = f32[512,2048]{1,0:T(8,128)} fusion(bf16[256,4096]{1,0:T(8,128)(2,1)S(1)} %bitcast.78, s32[]{:T(128)S(6)} %select_n.14, bf16[512,512]{1,0:T(8,128)(2,1)S(1)} %copy-done, s32[]{:T(128)S(6)} %select_n.13), kind=kOutput, calls=%fused_computation.58 | convolution fusion | flops 536870912 | bytes 5505032 | tf_op jit(solution)/shard_map/dot_general | solution.py:142
  95.5 19.1 %all-to-all-done = f32[32,1,512]{2,1,0:T(1,128)S(1)} async-done(((f32[32,1,512]{2,1,0:T(1,128)}), f32[32,1,512]{2,1,0:T(1,128)S(1)}, u32[]{:S(2)}, u32[]{:S(2)}) %all-to-all-start) | async-done | bytes 65568 | tf_op jit(solution)/shard_map/all_to_all | solution.py:108
  115.2 3.4 %subtract_convert_fusion = bf16[512,2048]{1,0:T(8,128)(2,1)S(1)} fusion(f32[512,2048]{1,0:T(8,128)} %fusion.44, bf16[256,2048]{1,0:T(8,128)(2,1)} %collective-permute-done.8, f32[512]{0:T(512)S(1)} %bitcast.80, bf16[512,512]{1,0:T(8,128)(2,1)S(1)} %copy-done, s32[]{:T(128)S(6)} %select_n.15), kind=kOutput, calls=%fused_computation.21 | convolution fusion | flops 540016640 | bytes 7604228 | tf_op jit(solution)/shard_map/dot_general | solution.py:142
  118.5 2.1 %fusion.32 = f32[128,512]{1,0:T(8,128)S(1)} fusion(bf16[512,2048]{1,0:T(8,128)(2,1)S(1)} %subtract_convert_fusion, f32[128,512]{1,0:T(8,128)S(1)} %copy-done.2), kind=kOutput, calls=%fused_computation.34 | convolution fusion | flops 537722880 | bytes 2621440 | tf_op jit(solution)/shard_map/dot_general | solution.py:86
  121.0 12.8 %all_to_all.38 = f32[32,1,2048]{2,1,0:T(1,128)S(1)} all-to-all(f32[32,1,2048]{2,1,0:T(1,128)S(1)} %all_to_all.31), channel_id=1, replica_groups=mesh['freq'=2,'row'=4,'col'=4] {'freq','row','col'}, dimensions={0} | all-to-all | bytes 524288 | tf_op jit(solution)/shard_map/all_to_all | solution.py:96
  134.0 12.6 %all_to_all.39 = f32[32,1,2048]{2,1,0:T(1,128)S(1)} all-to-all(f32[32,1,2048]{2,1,0:T(1,128)S(1)} %broadcast_in_dim.7), channel_id=1, replica_groups=mesh['freq'=2,'row'=4,'col'=4] {'freq','row','col'}, dimensions={0} | all-to-all | bytes 524288 | tf_op jit(solution)/shard_map/all_to_all | solution.py:99
  152.5 1.1 fusion.46
  153.9 12.6 %all_to_all.40 = f32[32,1,2048]{2,1,0:T(1,128)S(1)} all-to-all(f32[32,1,2048]{2,1,0:T(1,128)S(1)} %all_to_all.32), channel_id=1, replica_groups=mesh['freq'=2,'row'=4,'col'=4] {'freq','row','col'}, dimensions={0} | all-to-all | bytes 524288 | tf_op jit(solution)/shard_map/all_to_all | solution.py:96
  166.9 12.6 %all_to_all.41 = f32[32,1,2048]{2,1,0:T(1,128)S(1)} all-to-all(f32[32,1,2048]{2,1,0:T(1,128)S(1)} %broadcast_in_dim.8), channel_id=1, replica_groups=mesh['freq'=2,'row'=4,'col'=4] {'freq','row','col'}, dimensions={0} | all-to-all | bytes 524288 | tf_op jit(solution)/shard_map/all_to_all | solution.py:99
  185.3 1.2 convolution_convert_fusion.1
  (78 shorter events, 15.0 us)
Async XLA Ops:
  0.6 92.2 %copy-start = (bf16[512,512]{1,0:T(8,128)(2,1)S(1)}, bf16[512,512]{1,0:T(8,128)(2,1)}, u32[]{:S(2)}) copy-start(bf16[512,512]{1,0:T(8,128)(2,1)} %param.6) | copy-start | bytes 1572868
  0.6 8.4 %copy-start.1 = (bf16[256,32,128]{2,1,0:T(8,128)(2,1)S(1)}, bf16[256,32,128]{2,1,0:T(8,128)(2,1)}, u32[]{:S(2)}) copy-start(bf16[256,32,128]{2,1,0:T(8,128)(2,1)} %param.4) | copy-start | bytes 6291460
  3.8 30.3 %collective-permute-start = (bf16[256,8,8]{2,1,0:T(8,128)(2,1)S(1)}, bf16[256,8,8]{2,1,0:T(8,128)(2,1)}, u32[]{:S(2)}, u32[]{:S(2)}) collective-permute-start(bf16[256,8,8]{2,1,0:T(8,128)(2,1)S(1)} %get-tuple-element.2), channel_id=1, source_target_pairs={{0,5},{1,6},{2,7},{4,9},{5,10},{6,11},{8,13},{9,14},{10,15},{16,21... | collective-permute-start | bytes 98312 | tf_op jit(solution)/shard_map/ppermute | solution.py:36
  15.2 20.4 %collective-permute-start.3 = (bf16[256,32,8]{0,2,1:T(8,128)(2,1)}, bf16[256,32,8]{0,2,1:T(8,128)(2,1)S(1)}, u32[]{:S(2)}, u32[]{:S(2)}) collective-permute-start(bf16[256,32,8]{0,2,1:T(8,128)(2,1)} %copy.32), channel_id=1, source_target_pairs={{0,1},{1,2},{2,3},{4,5},{5,6},{6,7},{8,9},{9,10},{10,11},{12,13},{... | collective-permute-start | bytes 393224 | tf_op jit(solution)/shard_map/ppermute | solution.py:19
  18.7 9.9 %copy-start.6 = (f32[256]{0:T(256)S(1)}, f32[256]{0:T(256)}, u32[]{:S(2)}) copy-start(f32[256]{0:T(256)} %param.5) | copy-start | bytes 3076
  21.5 15.6 %collective-permute-start.4 = (bf16[256,32,8]{0,2,1:T(8,128)(2,1)S(1)}, bf16[256,32,8]{0,2,1:T(8,128)(2,1)S(1)}, u32[]{:S(2)}, u32[]{:S(2)}) collective-permute-start(bf16[256,32,8]{0,2,1:T(8,128)(2,1)S(1)} %copy.33), channel_id=1, source_target_pairs={{1,0},{2,1},{3,2},{5,4},{6,5},{7,6},{9,8},{10,9},{11,10},{13,12},{... | collective-permute-start | bytes 393224 | tf_op jit(solution)/shard_map/ppermute | solution.py:21
  23.8 38.0 %collective-permute-start.1 = (bf16[256,8,128]{2,1,0:T(8,128)(2,1)}, bf16[256,8,128]{2,1,0:T(8,128)(2,1)}, u32[]{:S(2)}, u32[]{:S(2)}) collective-permute-start(bf16[256,8,128]{2,1,0:T(8,128)(2,1)} %get-tuple-element.6), channel_id=1, source_target_pairs={{0,4},{4,8},{8,12},{1,5},{5,9},{9,13},{2,6},{6,10},{10,14},{3,7},{... | collective-permute-start | bytes 1572872 | tf_op jit(solution)/shard_map/ppermute | solution.py:19
  27.3 34.5 %collective-permute-start.6 = (bf16[256,8,128]{2,1,0:T(8,128)(2,1)}, bf16[256,8,128]{2,1,0:T(8,128)(2,1)}, u32[]{:S(2)}, u32[]{:S(2)}) collective-permute-start(bf16[256,8,128]{2,1,0:T(8,128)(2,1)} %get-tuple-element.7), channel_id=1, source_target_pairs={{4,0},{8,4},{12,8},{5,1},{9,5},{13,9},{6,2},{10,6},{14,10},{7,3},{... | collective-permute-start | bytes 1572872 | tf_op jit(solution)/shard_map/ppermute | solution.py:21
  34.1 16.7 %collective-permute-start.2 = (bf16[256,8,8]{2,1,0:T(8,128)(2,1)}, bf16[256,8,8]{2,1,0:T(8,128)(2,1)}, u32[]{:S(2)}, u32[]{:S(2)}) collective-permute-start(bf16[256,8,8]{2,1,0:T(8,128)(2,1)} %get-tuple-element.4), channel_id=1, source_target_pairs={{1,4},{2,5},{3,6},{5,8},{6,9},{7,10},{9,12},{10,13},{11,14},{17,20... | collective-permute-start | bytes 98312 | tf_op jit(solution)/shard_map/ppermute | solution.py:36
  35.6 15.2 %collective-permute-start.5 = (bf16[256,8,8]{2,1,0:T(8,128)(2,1)}, bf16[256,8,8]{2,1,0:T(8,128)(2,1)}, u32[]{:S(2)}, u32[]{:S(2)}) collective-permute-start(bf16[256,8,8]{2,1,0:T(8,128)(2,1)} %get-tuple-element.3), channel_id=1, source_target_pairs={{4,1},{5,2},{6,3},{8,5},{9,6},{10,7},{12,9},{13,10},{14,11},{20,17... | collective-permute-start | bytes 98312 | tf_op jit(solution)/shard_map/ppermute | solution.py:36
  37.1 0.7 copy-start.4
  37.7 24.1 %collective-permute-start.7 = (bf16[256,8,8]{2,1,0:T(8,128)(2,1)}, bf16[256,8,8]{2,1,0:T(8,128)(2,1)}, u32[]{:S(2)}, u32[]{:S(2)}) collective-permute-start(bf16[256,8,8]{2,1,0:T(8,128)(2,1)} %get-tuple-element.5), channel_id=1, source_target_pairs={{5,0},{6,1},{7,2},{9,4},{10,5},{11,6},{13,8},{14,9},{15,10},{21,16... | collective-permute-start | bytes 98312 | tf_op jit(solution)/shard_map/ppermute | solution.py:36
  43.4 3.7 %copy-start.5 = (bf16[256,32,8]{0,2,1:T(8,128)(2,1)S(1)}, bf16[256,32,8]{0,2,1:T(8,128)(2,1)}, u32[]{:S(2)}) copy-start(bf16[256,32,8]{0,2,1:T(8,128)(2,1)} %copy-done.4) | copy-start | bytes 393220
  87.7 27.5 %collective-permute-start.8 = (bf16[256,2048]{1,0:T(8,128)(2,1)}, bf16[256,2048]{1,0:T(8,128)(2,1)}, u32[]{:S(2)}, u32[]{:S(2)}) collective-permute-start(bf16[256,2048]{1,0:T(8,128)(2,1)} %constant_dynamic-slice_fusion), channel_id=1, source_target_pairs={{0,16},{16,0},{1,17},{17,1},{2,18},{18,2},{3,19},{19,3},{4,20},{20... | collective-permute-start | bytes 3145736 | tf_op jit(solution)/shard_map/ppermute | solution.py:132
  90.0 24.6 %all-to-all-start = ((f32[32,1,512]{2,1,0:T(1,128)}), f32[32,1,512]{2,1,0:T(1,128)S(1)}, u32[]{:S(2)}, u32[]{:S(2)}) async-start(f32[32,1,512]{2,1,0:T(1,128)} %broadcast_in_dim.6), calls=%async_computation | async-start | bytes 131072 | tf_op jit(solution)/shard_map/all_to_all | solution.py:108
  115.2 3.4 %copy-start.2 = (f32[128,512]{1,0:T(8,128)S(1)}, f32[128,512]{1,0:T(8,128)}, u32[]{:S(2)}) copy-start(f32[128,512]{1,0:T(8,128)} %param.7) | copy-start | bytes 786436
  185.3 1.3 copy-start.3

commit v4 on v2

--- a/solution.py
+++ b/solution.py
@@ -38,6 +38,19 @@
     offsets = jnp.arange(length + spread - 1)[None, :] - jnp.arange(length)[:, None]
     onehot = (offsets[:, :, None] == jnp.arange(spread)[None, None, :]).astype(jnp.float32)
     return jnp.einsum("ijk,ck->cij", onehot, beam_taps.astype(jnp.float32)).astype(jnp.bfloat16)
+
+
+def depthwise(cells, kernel):
+    out = lax.conv_general_dilated(
+        cells[None],
+        kernel,
+        window_strides=(1, 1),
+        padding="VALID",
+        dimension_numbers=("NCHW", "OIHW", "NCHW"),
+        feature_group_count=cells.shape[0],
+        preferred_element_type=jnp.float32,
+    )
+    return out[0].astype(jnp.bfloat16)
 
 
 def inverse_root(matrix):
@@ -84,18 +97,12 @@
 
 
 def shards(sky_maps, beam_sigma, whitening, unmix_init):
-    beam_taps = make_taps(beam_sigma)
+    beam_taps = lax.optimization_barrier(make_taps(beam_sigma))
     channels, height, breadth = sky_maps.shape
-    band_rows = make_band(beam_taps, height)
-    band_cols = make_band(beam_taps, breadth)
     padded = with_halo(sky_maps, (("row", 1),), HALF)
-    rowwise = jnp.einsum(
-        "cik,ckj->cij", band_rows, padded, preferred_element_type=jnp.float32
-    ).astype(jnp.bfloat16)
+    rowwise = depthwise(padded, beam_taps[:, None, :, None])
     widened = with_halo(rowwise, (("col", 2),), HALF)
-    smoothed = jnp.einsum(
-        "cim,cjm->cij", widened, band_cols, preferred_element_type=jnp.float32
-    ).astype(jnp.bfloat16)
+    smoothed = depthwise(widened, beam_taps[:, None, None, :])
     flattened = smoothed.reshape(channels, height * breadth)
     parts = lax.axis_size("freq")
     devices = parts * lax.axis_size("row") * lax.axis_size("col")
@@ -106,7 +113,7 @@
         outgoing = lax.dynamic_slice_in_dim(flattened, (1 - side) * block, block, axis=1)
         incoming = lax.ppermute(outgoing, "freq", [(0, 1), (1, 0)])
         local = lax.dynamic_slice_in_dim(flattened, side * block, block, axis=1)
-        plane_sums = jnp.sum(flattened, axis=1, dtype=jnp.float32)
+        plane_sums = jnp.sum(lax.optimization_barrier(flattened), axis=1, dtype=jnp.float32)
         placed = jnp.zeros((parts * channels,), jnp.float32)
         placed = lax.dynamic_update_slice_in_dim(placed, plane_sums, side * channels, axis=0)
         channel_sums = gathered_sum(placed, ("freq", "row", "col"))

time: 169 us -> 152 us (0.90)
  local copies, waits for them, and re-layouts: 25 us -> 11.9 us
  matrix products: 44.1 us -> 32.2 us
  waiting for transfers between devices: 26.1 us -> 32.7 us
    dot_general x4 -> x0, matrix products: 24.7 us -> none  [the longest x1 15.8 us: shards(): jnp.einsum('cim,cjm->cij', widened, band_cols, preferred_element_type=jnp...]
    conv_general_dilated x0 -> x2, matrix products: none -> 12.8 us  [depthwise(): lax.conv_general_dilated(cells[None], kernel, window_strides=(1, 1), padd...]
    ppermute x2 -> x0, local copies, waits for them, and re-layouts: 7.4 us -> none  [the longest x1 3.74 us: with_halo(): lax.ppermute(tail, axis, [(i, (i + 1) % count) for i in range(ends)])]
    slice x3 -> x2, local copies, waits for them, and re-layouts: 6.9 us -> 0.11 us  [with_halo(): lax.slice_in_dim(cells, cells.shape[dim] - width, cells.shape[dim], axis=...]
    ppermute x2, waiting for transfers between devices: 5.23 us -> 9.62 us  [with_halo(): lax.ppermute(tail, axis, [(i, (i + 1) % count) for i in range(ends)])]
    ppermute x2, waiting for transfers between devices: 4.25 us -> 7.82 us  [with_halo(): lax.ppermute(head, axis, [((i + 1) % count, i) for i in range(ends)])]
    slice x1 -> x0, local copies, waits for them, and re-layouts: 2.71 us -> none  [with_halo(): head = lax.slice_in_dim(cells, 0, width, axis=dim)]
    unnamed x9 -> x11, local copies, waits for them, and re-layouts: 1.02 us -> 3.17 us
  transfers between devices with their start and end apart: 6 -> 6, of which waited for: 3 -> 4; matrix products, arithmetic and copies ran while one was open for 12% -> 3% of each run, Pallas kernels for 0% -> 0%
where the time goes in v4:
time: 152 us
  blocking collectives  52.7 us (35%)
  waiting for transfers between devices  32.7 us (22%)
  matrix products  32.2 us (21%)
  starting transfers between devices  16.3 us (11%)
  local copies, waits for them, and re-layouts  11.9 us (8%)
  other arithmetic  3.13 us (2%)
  between operations  2.65 us (2%)
    all_to_all x2, blocking collectives, total_sum(): pieces = lax.all_to_all(flat, axes, 0, 0, tiled=True)  27.4 us
    all_to_all x2, blocking collectives, total_sum(): gathered = lax.all_to_all(spread, axes, 0, 0, tiled=True)  25.3 us
    all_to_all x1, waiting for transfers between devices, gathered_sum(): gathered = lax.all_to_all(spread, axes, 0, 0, tiled=True)  15.3 us
    conv_general_dilated x2, matrix products, depthwise(): lax.conv_general_dilated(cells[None], kernel, window_strides=(1, 1), padd...  12.8 us
    ppermute x2, waiting for transfers between devices, with_halo(): lax.ppermute(tail, axis, [(i, (i + 1) % count) for i in range(ends)])  9.62 us
    ppermute x2, waiting for transfers between devices, with_halo(): lax.ppermute(head, axis, [((i + 1) % count, i) for i in range(ends)])  7.82 us
    ppermute x2, starting transfers between devices, with_halo(): lax.ppermute(tail, axis, [(i, (i + 1) % count) for i in range(ends)])  6.26 us
    all_to_all x1, starting transfers between devices, gathered_sum(): gathered = lax.all_to_all(spread, axes, 0, 0, tiled=True)  5.97 us
  transfers between devices with their start and end apart: 6, of which 4 were waited for; matrix products, arithmetic and copies ran while one was open for 3% of the time, Pallas kernels for 0%

profile of v4, /device:TPU:0, one launch (start us, length us, event | category | flops | bytes accessed | tf_op | source)
XLA Modules:
  0.0 151.6 jit_solution(17120462605794994789)
XLA Ops:
  0.7 3.1 %copy.58 = bf16[256,32,128]{0,2,1:T(8,128)(2,1)S(1)} copy(bf16[256,32,128]{2,1,0:T(8,128)(2,1)} %param.4) | data formatting | bytes 4194304 | tf_op args[0]
  3.8 5.0 %collective-permute-start = (bf16[256,8,128]{0,2,1:T(8,128)(2,1)S(1)}, bf16[256,8,128]{0,2,1:T(8,128)(2,1)S(1)}, u32[]{:S(2)}, u32[]{:S(2)}) collective-permute-start(bf16[256,8,128]{0,2,1:T(8,128)(2,1)S(1)} %get-tuple-element.4), channel_id=1, source_target_pairs={{0,4},{4,8},{8,12},{1,5},{5,9},{9,13},{2,6},{6,10},{10,14},{3,7},{... | collective-permute-start | bytes 1572872 | tf_op jit(solution)/shard_map/ppermute | solution.py:19
  8.8 1.3 collective-permute-start.1
  10.3 9.6 %collective-permute-done = bf16[256,8,128]{0,2,1:T(8,128)(2,1)S(1)} collective-permute-done((bf16[256,8,128]{0,2,1:T(8,128)(2,1)S(1)}, bf16[256,8,128]{0,2,1:T(8,128)(2,1)S(1)}, u32[]{:S(2)}, u32[]{:S(2)}) %collective-permute-start) | collective-permute-done | bytes 524320 | tf_op jit(solution)/shard_map/ppermute | solution.py:19
  19.9 4.1 %collective-permute-done.1 = bf16[256,8,128]{0,2,1:T(8,128)(2,1)S(1)} collective-permute-done((bf16[256,8,128]{0,2,1:T(8,128)(2,1)S(1)}, bf16[256,8,128]{0,2,1:T(8,128)(2,1)S(1)}, u32[]{:S(2)}, u32[]{:S(2)}) %collective-permute-start.1) | collective-permute-done | bytes 524320 | tf_op jit(solution)/shard_map/ppermute | solution.py:21
  24.5 6.9 %fusion.11 = bf16[32,8,16,256]{3,1,2,0:T(8,128)(2,1)S(1)} fusion(bf16[256,48,8,16]{0,3,2,1:T(8,128)(2,1)S(1)} %bitcast.93, bf16[256,1,17,1]{0,2,3,1:T(8,128)(2,1)S(1)} %bitcast.94), kind=kOutput, calls=%fused_computation.19 | convolution fusion | flops 36700160 | bytes 5251584 | tf_op jit(solution)/shard_map/conv_general_dilated | solution.py:44
  32.1 1.3 collective-permute-start.2
  33.4 1.3 collective-permute-start.3
  34.7 3.7 %collective-permute-done.3 = bf16[256,32,8]{0,2,1:T(8,128)(2,1)S(1)} collective-permute-done((bf16[256,32,8]{0,2,1:T(8,128)(2,1)S(1)}, bf16[256,32,8]{0,2,1:T(8,128)(2,1)S(1)}, u32[]{:S(2)}, u32[]{:S(2)}) %collective-permute-start.3) | collective-permute-done | bytes 131104 | tf_op jit(solution)/shard_map/ppermute | solution.py:21
  38.5 0.9 copy.64
  39.4 1.3 copy.66
  41.4 5.9 %select_convert_fusion = bf16[32,8,18,256]{3,1,2,0:T(8,128)(2,1)S(1)} fusion(pred[8,18]{0,1:T(8,128)(4,1)S(1)} %copy-done.4, bf16[256,32,1,7,16]{0,3,4,1,2:T(8,128)(2,1)S(1)} %slice.23, bf16[256,32,1,8,18]{0,3,4,1,2:T(8,128)(2,1)S(1)} %copy.66, bf16[256,1,1,17]{0,3,2,1:T(8,128)(2,1)S(1)} %bitcast.95), kind=kOutput, calls=%fused_computation.2 | convolution fusion | flops 55836672 | bytes 6562448 | tf_op jit(solution)/shard_map/conv_general_dilated | solution.py:44
  47.3 0.9 copy.68
  48.4 1.2 copy.69
  49.6 1.1 constant_dynamic-slice_fusion
  50.6 1.5 collective-permute-start.4
  52.9 0.7 broadcast_in_dim.18
  53.6 6.0 %all-to-all-start = ((f32[32,1,512]{2,1,0:T(1,128)}), f32[32,1,512]{2,1,0:T(1,128)S(1)}, u32[]{:S(2)}, u32[]{:S(2)}) async-start(f32[32,1,512]{2,1,0:T(1,128)} %broadcast_in_dim.18), calls=%async_computation | async-start | bytes 131072 | tf_op jit(solution)/shard_map/all_to_all | solution.py:95
  59.6 2.7 %fusion.29 = f32[512,2048]{1,0:T(8,128)} fusion(bf16[256,4096]{0,1:T(8,128)(2,1)S(1)} %bitcast.88, s32[]{:T(128)S(6)} %select_n.14, bf16[512,512]{1,0:T(8,128)(2,1)S(1)} %copy-done, s32[]{:T(128)S(6)} %select_n.13), kind=kOutput, calls=%fused_computation.47 | convolution fusion | flops 536870912 | bytes 5505032 | tf_op jit(solution)/shard_map/dot_general | solution.py:124
  62.3 15.3 %all-to-all-done = f32[32,1,512]{2,1,0:T(1,128)S(1)} async-done(((f32[32,1,512]{2,1,0:T(1,128)}), f32[32,1,512]{2,1,0:T(1,128)S(1)}, u32[]{:S(2)}, u32[]{:S(2)}) %all-to-all-start) | async-done | bytes 65568 | tf_op jit(solution)/shard_map/all_to_all | solution.py:95
  78.1 3.4 %subtract_convert_fusion = bf16[512,2048]{1,0:T(8,128)(2,1)S(1)} fusion(f32[512,2048]{1,0:T(8,128)} %fusion.29, bf16[256,2048]{0,1:T(8,128)(2,1)} %collective-permute-done.4, f32[512]{0:T(512)S(1)} %bitcast.96, bf16[512,512]{1,0:T(8,128)(2,1)S(1)} %copy-done, s32[]{:T(128)S(6)} %select_n.15), kind=kOutput, calls=%fused_computation.9 | convolution fusion | flops 540016640 | bytes 7604228 | tf_op jit(solution)/shard_map/dot_general | solution.py:124
  81.5 2.1 %fusion.17 = f32[128,512]{1,0:T(8,128)S(1)} fusion(bf16[512,2048]{1,0:T(8,128)(2,1)S(1)} %subtract_convert_fusion, f32[128,512]{1,0:T(8,128)S(1)} %copy-done.1), kind=kOutput, calls=%fused_computation.23 | convolution fusion | flops 537722880 | bytes 2621440 | tf_op jit(solution)/shard_map/dot_general | solution.py:73
  83.9 14.8 %all_to_all.38 = f32[32,1,2048]{2,1,0:T(1,128)S(1)} all-to-all(f32[32,1,2048]{2,1,0:T(1,128)S(1)} %all_to_all.31), channel_id=1, replica_groups=mesh['freq'=2,'row'=4,'col'=4] {'freq','row','col'}, dimensions={0} | all-to-all | bytes 524288 | tf_op jit(solution)/shard_map/all_to_all | solution.py:83
  99.0 12.6 %all_to_all.39 = f32[32,1,2048]{2,1,0:T(1,128)S(1)} all-to-all(f32[32,1,2048]{2,1,0:T(1,128)S(1)} %broadcast_in_dim.19), channel_id=1, replica_groups=mesh['freq'=2,'row'=4,'col'=4] {'freq','row','col'}, dimensions={0} | all-to-all | bytes 524288 | tf_op jit(solution)/shard_map/all_to_all | solution.py:86
  111.6 0.7 multiply_reduce_fusion.1
  112.4 1.0 multiply_reduce_fusion.3
  117.5 1.1 fusion.31
  118.9 12.6 %all_to_all.40 = f32[32,1,2048]{2,1,0:T(1,128)S(1)} all-to-all(f32[32,1,2048]{2,1,0:T(1,128)S(1)} %all_to_all.32), channel_id=1, replica_groups=mesh['freq'=2,'row'=4,'col'=4] {'freq','row','col'}, dimensions={0} | all-to-all | bytes 524288 | tf_op jit(solution)/shard_map/all_to_all | solution.py:83
  131.8 12.6 %all_to_all.41 = f32[32,1,2048]{2,1,0:T(1,128)S(1)} all-to-all(f32[32,1,2048]{2,1,0:T(1,128)S(1)} %broadcast_in_dim.20), channel_id=1, replica_groups=mesh['freq'=2,'row'=4,'col'=4] {'freq','row','col'}, dimensions={0} | all-to-all | bytes 524288 | tf_op jit(solution)/shard_map/all_to_all | solution.py:86
  144.5 0.7 multiply_reduce_fusion
  145.3 1.0 multiply_reduce_fusion.2
  150.3 1.2 convolution_convert_fusion
  (67 shorter events, 11.5 us)
Async XLA Ops:
  0.6 59.0 %copy-start = (bf16[512,512]{1,0:T(8,128)(2,1)S(1)}, bf16[512,512]{1,0:T(8,128)(2,1)}, u32[]{:S(2)}) copy-start(bf16[512,512]{1,0:T(8,128)(2,1)} %param.6) | copy-start | bytes 1572868
  0.6 9.5 %copy-start.3 = (f32[256]{0:T(256)S(1)}, f32[256]{0:T(256)}, u32[]{:S(2)}) copy-start(f32[256]{0:T(256)} %param.5) | copy-start | bytes 3076
  3.8 16.1 %collective-permute-start = (bf16[256,8,128]{0,2,1:T(8,128)(2,1)S(1)}, bf16[256,8,128]{0,2,1:T(8,128)(2,1)S(1)}, u32[]{:S(2)}, u32[]{:S(2)}) collective-permute-start(bf16[256,8,128]{0,2,1:T(8,128)(2,1)S(1)} %get-tuple-element.4), channel_id=1, source_target_pairs={{0,4},{4,8},{8,12},{1,5},{5,9},{9,13},{2,6},{6,10},{10,14},{3,7},{... | collective-permute-start | bytes 1572872 | tf_op jit(solution)/shard_map/ppermute | solution.py:19
  8.8 15.3 %collective-permute-start.1 = (bf16[256,8,128]{0,2,1:T(8,128)(2,1)S(1)}, bf16[256,8,128]{0,2,1:T(8,128)(2,1)S(1)}, u32[]{:S(2)}, u32[]{:S(2)}) collective-permute-start(bf16[256,8,128]{0,2,1:T(8,128)(2,1)S(1)} %get-tuple-element.5), channel_id=1, source_target_pairs={{4,0},{8,4},{12,8},{5,1},{9,5},{13,9},{6,2},{10,6},{14,10},{7,3},{... | collective-permute-start | bytes 1572872 | tf_op jit(solution)/shard_map/ppermute | solution.py:21
  32.1 2.6 %collective-permute-start.2 = (bf16[256,32,8]{0,2,1:T(8,128)(2,1)S(1)}, bf16[256,32,8]{0,2,1:T(8,128)(2,1)S(1)}, u32[]{:S(2)}, u32[]{:S(2)}) collective-permute-start(bf16[256,32,8]{0,2,1:T(8,128)(2,1)S(1)} %get-tuple-element.2), channel_id=1, source_target_pairs={{0,1},{1,2},{2,3},{4,5},{5,6},{6,7},{8,9},{9,10},{10,11},{12,13},{... | collective-permute-start | bytes 393224 | tf_op jit(solution)/shard_map/ppermute | solution.py:19
  33.4 5.0 %collective-permute-start.3 = (bf16[256,32,8]{0,2,1:T(8,128)(2,1)S(1)}, bf16[256,32,8]{0,2,1:T(8,128)(2,1)S(1)}, u32[]{:S(2)}, u32[]{:S(2)}) collective-permute-start(bf16[256,32,8]{0,2,1:T(8,128)(2,1)S(1)} %get-tuple-element.3), channel_id=1, source_target_pairs={{1,0},{2,1},{3,2},{5,4},{6,5},{7,6},{9,8},{10,9},{11,10},{13,12},{... | collective-permute-start | bytes 393224 | tf_op jit(solution)/shard_map/ppermute | solution.py:21
  40.8 0.7 copy-start.4
  50.6 27.5 %collective-permute-start.4 = (bf16[256,2048]{0,1:T(8,128)(2,1)}, bf16[256,2048]{0,1:T(8,128)(2,1)}, u32[]{:S(2)}, u32[]{:S(2)}) collective-permute-start(bf16[256,2048]{0,1:T(8,128)(2,1)} %constant_dynamic-slice_fusion), channel_id=1, source_target_pairs={{0,16},{16,0},{1,17},{17,1},{2,18},{18,2},{3,19},{19,3},{4,20},{20... | collective-permute-start | bytes 3145736 | tf_op jit(solution)/shard_map/ppermute | solution.py:114
  53.6 23.9 %all-to-all-start = ((f32[32,1,512]{2,1,0:T(1,128)}), f32[32,1,512]{2,1,0:T(1,128)S(1)}, u32[]{:S(2)}, u32[]{:S(2)}) async-start(f32[32,1,512]{2,1,0:T(1,128)} %broadcast_in_dim.18), calls=%async_computation | async-start | bytes 131072 | tf_op jit(solution)/shard_map/all_to_all | solution.py:95
  78.1 3.4 %copy-start.1 = (f32[128,512]{1,0:T(8,128)S(1)}, f32[128,512]{1,0:T(8,128)}, u32[]{:S(2)}) copy-start(f32[128,512]{1,0:T(8,128)} %param.7) | copy-start | bytes 786436
  150.3 1.3 copy-start.2

commit v5 on v4

--- a/solution.py
+++ b/solution.py
@@ -53,6 +53,26 @@
     return out[0].astype(jnp.bfloat16)
 
 
+def split_pass(cells, kernel, axis, dim):
+    length = cells.shape[dim]
+    if length < 4 * HALF:
+        return depthwise(with_halo(cells, ((axis, dim),), HALF), kernel)
+    count = lax.axis_size(axis)
+    ends = count - 1
+    head = lax.slice_in_dim(cells, 0, 2 * HALF, axis=dim)
+    tail = lax.slice_in_dim(cells, length - 2 * HALF, length, axis=dim)
+    before = lax.ppermute(
+        lax.slice_in_dim(tail, HALF, 2 * HALF, axis=dim), axis, [(i, (i + 1) % count) for i in range(ends)]
+    )
+    after = lax.ppermute(
+        lax.slice_in_dim(head, 0, HALF, axis=dim), axis, [((i + 1) % count, i) for i in range(ends)]
+    )
+    middle = depthwise(cells, kernel)
+    first = depthwise(jnp.concatenate([before, head], axis=dim), kernel)
+    last = depthwise(jnp.concatenate([tail, after], axis=dim), kernel)
+    return jnp.concatenate([first, middle, last], axis=dim)
+
+
 def inverse_root(matrix):
     frob_norm = jnp.sqrt(jnp.sum(matrix * matrix) + 1e-06)
     current = matrix / frob_norm
@@ -99,10 +119,8 @@
 def shards(sky_maps, beam_sigma, whitening, unmix_init):
     beam_taps = lax.optimization_barrier(make_taps(beam_sigma))
     channels, height, breadth = sky_maps.shape
-    padded = with_halo(sky_maps, (("row", 1),), HALF)
-    rowwise = depthwise(padded, beam_taps[:, None, :, None])
-    widened = with_halo(rowwise, (("col", 2),), HALF)
-    smoothed = depthwise(widened, beam_taps[:, None, None, :])
+    rowwise = split_pass(sky_maps, beam_taps[:, None, :, None], "row", 1)
+    smoothed = split_pass(rowwise, beam_taps[:, None, None, :], "col", 2)
     flattened = smoothed.reshape(channels, height * breadth)
     parts = lax.axis_size("freq")
     devices = parts * lax.axis_size("row") * lax.axis_size("col")

time: 152 us -> 147 us (0.967)
  waiting for transfers between devices: 32.7 us -> 21.9 us
  matrix products: 32.2 us -> 35.9 us
    ppermute x4, waiting for transfers between devices: 17.4 us -> 5.97 us  [the longest x2 4.15 us: split_pass(): lax.ppermute(lax.slice_in_dim(head, 0, HALF, axis=dim), axis, [((i + 1) %...]
    conv_general_dilated x2 -> x6, matrix products: 12.8 us -> 16.5 us  [depthwise(): lax.conv_general_dilated(cells[None], kernel, window_strides=(1, 1), padd...]
    convert_element_type x4 -> x5, local copies, waits for them, and re-layouts: 2.87 us -> 3.45 us  [depthwise(): return out[0].astype(jnp.bfloat16)]
    unnamed x11 -> x15, local copies, waits for them, and re-layouts: 3.17 us -> 3.22 us
  transfers between devices with their start and end apart: 6 -> 6, of which waited for: 4 -> 3; matrix products, arithmetic and copies ran while one was open for 3% -> 15% of each run, Pallas kernels for 0% -> 0%
where the time goes in v5:
time: 147 us
  blocking collectives  51.9 us (35%)
  matrix products  35.9 us (24%)
  waiting for transfers between devices  21.9 us (15%)
  starting transfers between devices  17.4 us (12%)
  local copies, waits for them, and re-layouts  12.5 us (9%)
  other arithmetic  4.42 us (3%)
  between operations  2.74 us (2%)
    all_to_all x2, blocking collectives, total_sum(): pieces = lax.all_to_all(flat, axes, 0, 0, tiled=True)  26.6 us
    all_to_all x2, blocking collectives, total_sum(): gathered = lax.all_to_all(spread, axes, 0, 0, tiled=True)  25.3 us
    conv_general_dilated x6, matrix products, depthwise(): lax.conv_general_dilated(cells[None], kernel, window_strides=(1, 1), padd...  16.5 us
    all_to_all x1, waiting for transfers between devices, gathered_sum(): gathered = lax.all_to_all(spread, axes, 0, 0, tiled=True)  15.9 us
    all_to_all x1, starting transfers between devices, gathered_sum(): gathered = lax.all_to_all(spread, axes, 0, 0, tiled=True)  7.03 us
    ppermute x2, starting transfers between devices, split_pass(): lax.ppermute(lax.slice_in_dim(tail, HALF, 2 * HALF, axis=dim), axis, [(i,...  6.25 us
    ppermute x2, waiting for transfers between devices, split_pass(): lax.ppermute(lax.slice_in_dim(head, 0, HALF, axis=dim), axis, [((i + 1) %...  4.15 us
    convert_element_type x5, local copies, waits for them, and re-layouts, depthwise(): return out[0].astype(jnp.bfloat16)  3.45 us
  transfers between devices with their start and end apart: 6, of which 3 were waited for; matrix products, arithmetic and copies ran while one was open for 15% of the time, Pallas kernels for 0%

profile of v5, /device:TPU:0, one launch (start us, length us, event | category | flops | bytes accessed | tf_op | source)
XLA Modules:
  0.0 146.7 jit_solution(8585933321935352237)
XLA Ops:
  0.6 3.0 %copy.102 = bf16[256,32,128]{0,2,1:T(8,128)(2,1)S(1)} copy(bf16[256,32,128]{2,1,0:T(8,128)(2,1)} %param.4) | data formatting | bytes 4194304 | tf_op args[0]
  3.7 1.0 fusion.82
  4.8 4.9 %collective-permute-start = (bf16[256,8,128]{0,2,1:T(8,128)(2,1)}, bf16[256,8,128]{0,2,1:T(8,128)(2,1)S(1)}, u32[]{:S(2)}, u32[]{:S(2)}) collective-permute-start(bf16[256,8,128]{0,2,1:T(8,128)(2,1)} %get-tuple-element.6), channel_id=1, source_target_pairs={{0,4},{4,8},{8,12},{1,5},{5,9},{9,13},{2,6},{6,10},{10,14},{3,7},{... | collective-permute-start | bytes 1572872 | tf_op jit(solution)/shard_map/ppermute | solution.py:64
  9.7 1.3 collective-permute-start.1
  11.2 5.4 %fusion.16 = bf16[16,8,16,256]{3,1,2,0:T(8,128)(2,1)} fusion(bf16[256,32,8,16]{0,3,2,1:T(8,128)(2,1)S(1)} %bitcast.113, bf16[256,1,17,1]{0,2,3,1:T(8,128)(2,1)S(1)} %bitcast.123), kind=kOutput, calls=%fused_computation.28 | convolution fusion | flops 18350080 | bytes 3154432 | tf_op jit(solution)/shard_map/conv_general_dilated | solution.py:44
  16.7 2.5 %copy.110 = bf16[16,8,16,256]{3,2,1,0:T(8,128)(2,1)} copy(bf16[16,8,16,256]{3,1,2,0:T(8,128)(2,1)} %fusion.16) | data formatting | bytes 2097152 | tf_op jit(solution)/shard_map/convert_element_type | solution.py:53
  19.3 1.8 %collective-permute-done = bf16[256,8,128]{0,2,1:T(8,128)(2,1)S(1)} collective-permute-done((bf16[256,8,128]{0,2,1:T(8,128)(2,1)}, bf16[256,8,128]{0,2,1:T(8,128)(2,1)S(1)}, u32[]{:S(2)}, u32[]{:S(2)}) %collective-permute-start) | collective-permute-done | bytes 524320 | tf_op jit(solution)/shard_map/ppermute | solution.py:64
  21.2 4.1 %collective-permute-done.1 = bf16[256,8,128]{0,2,1:T(8,128)(2,1)} collective-permute-done((bf16[256,8,128]{0,2,1:T(8,128)(2,1)}, bf16[256,8,128]{0,2,1:T(8,128)(2,1)}, u32[]{:S(2)}, u32[]{:S(2)}) %collective-permute-start.1) | collective-permute-done | bytes 524320 | tf_op jit(solution)/shard_map/ppermute | solution.py:67
  25.3 1.3 pad_maximum_fusion.2
  26.6 1.7 %fusion.21 = bf16[8,8,16,256]{3,1,2,0:T(8,128)(2,1)S(1)} fusion(bf16[256,24,8,16]{0,3,2,1:T(8,128)(2,1)S(1)} %bitcast.120, bf16[256,1,17,1]{0,2,3,1:T(8,128)(2,1)S(1)} %bitcast.124), kind=kOutput, calls=%fused_computation.29 | convolution fusion | flops 9175040 | bytes 2105856 | tf_op jit(solution)/shard_map/conv_general_dilated | solution.py:44
  28.4 1.7 %fusion.24 = bf16[8,8,16,256]{3,1,2,0:T(8,128)(2,1)S(1)} fusion(bf16[256,24,8,16]{0,3,2,1:T(8,128)(2,1)S(1)} %bitcast.119, bf16[256,1,17,1]{0,2,3,1:T(8,128)(2,1)S(1)} %bitcast.125), kind=kOutput, calls=%fused_computation.30 | convolution fusion | flops 9175040 | bytes 2105856 | tf_op jit(solution)/shard_map/conv_general_dilated | solution.py:44
  30.5 1.3 collective-permute-start.2
  31.8 1.3 collective-permute-start.3
  33.1 0.9 copy.119
  34.8 5.3 %select_convert_fusion = bf16[32,8,16,256]{3,1,2,0:T(8,128)(2,1)S(1)} fusion(pred[8,16]{0,1:T(8,128)(4,1)S(1)} %copy-done.5, bf16[256,32,1,7,16]{0,3,4,1,2:T(8,128)(2,1)S(1)} %slice.47, bf16[256,32,1,8,16]{0,3,4,1,2:T(8,128)(2,1)S(1)} %copy.119, bf16[256,1,1,17]{0,3,2,1:T(8,128)(2,1)S(1)} %bitcast.126), kind=kOutput, calls=%fused_computation.8 | convolution fusion | flops 50331648 | bytes 6038144 | tf_op jit(solution)/shard_map/conv_general_dilated | solution.py:44
  40.9 1.2 convolution_convert_fusion.2
  42.2 1.2 convolution_convert_fusion.1
  43.8 1.1 constant_dynamic-slice_fusion
  44.8 1.5 %collective-permute-start.4 = (bf16[256,2048]{0,1:T(8,128)(2,1)}, bf16[256,2048]{0,1:T(8,128)(2,1)}, u32[]{:S(2)}, u32[]{:S(2)}) collective-permute-start(bf16[256,2048]{0,1:T(8,128)(2,1)} %constant_dynamic-slice_fusion), channel_id=1, source_target_pairs={{0,16},{16,0},{1,17},{17,1},{2,18},{18,2},{3,19},{19,3},{4,20},{20... | collective-permute-start | bytes 3145736 | tf_op jit(solution)/shard_map/ppermute | solution.py:132
  47.8 7.0 %all-to-all-start = ((f32[32,1,512]{2,1,0:T(1,128)}), f32[32,1,512]{2,1,0:T(1,128)S(1)}, u32[]{:S(2)}, u32[]{:S(2)}) async-start(f32[32,1,512]{2,1,0:T(1,128)} %broadcast_in_dim.57), calls=%async_computation | async-start | bytes 131072 | tf_op jit(solution)/shard_map/all_to_all | solution.py:115
  54.8 2.7 %fusion.39 = f32[512,2048]{1,0:T(8,128)} fusion(bf16[256,4096]{0,1:T(8,128)(2,1)S(1)} %bitcast.112, s32[]{:T(128)S(6)} %select_n.14, bf16[512,512]{1,0:T(8,128)(2,1)S(1)} %copy-done, s32[]{:T(128)S(6)} %select_n.13), kind=kOutput, calls=%fused_computation.57 | convolution fusion | flops 536870912 | bytes 5505032 | tf_op jit(solution)/shard_map/dot_general | solution.py:142
  57.5 15.9 %all-to-all-done = f32[32,1,512]{2,1,0:T(1,128)S(1)} async-done(((f32[32,1,512]{2,1,0:T(1,128)}), f32[32,1,512]{2,1,0:T(1,128)S(1)}, u32[]{:S(2)}, u32[]{:S(2)}) %all-to-all-start) | async-done | bytes 65568 | tf_op jit(solution)/shard_map/all_to_all | solution.py:115
  74.0 3.4 %subtract_convert_fusion = bf16[512,2048]{1,0:T(8,128)(2,1)S(1)} fusion(f32[512,2048]{1,0:T(8,128)} %fusion.39, bf16[256,2048]{0,1:T(8,128)(2,1)} %collective-permute-done.4, f32[512]{0:T(512)S(1)} %bitcast.129, bf16[512,512]{1,0:T(8,128)(2,1)S(1)} %copy-done, s32[]{:T(128)S(6)} %select_n.15), kind=kOutput, calls=%fused_computation.9 | convolution fusion | flops 540016640 | bytes 7604228 | tf_op jit(solution)/shard_map/dot_general | solution.py:142
  77.4 2.1 %fusion.27 = f32[128,512]{1,0:T(8,128)S(1)} fusion(bf16[512,2048]{1,0:T(8,128)(2,1)S(1)} %subtract_convert_fusion, f32[128,512]{1,0:T(8,128)S(1)} %copy-done.2), kind=kOutput, calls=%fused_computation.31 | convolution fusion | flops 537722880 | bytes 2621440 | tf_op jit(solution)/shard_map/dot_general | solution.py:93
  79.8 14.0 %all_to_all.38 = f32[32,1,2048]{2,1,0:T(1,128)S(1)} all-to-all(f32[32,1,2048]{2,1,0:T(1,128)S(1)} %all_to_all.31), channel_id=1, replica_groups=mesh['freq'=2,'row'=4,'col'=4] {'freq','row','col'}, dimensions={0} | all-to-all | bytes 524288 | tf_op jit(solution)/shard_map/all_to_all | solution.py:103
  94.1 12.6 %all_to_all.39 = f32[32,1,2048]{2,1,0:T(1,128)S(1)} all-to-all(f32[32,1,2048]{2,1,0:T(1,128)S(1)} %broadcast_in_dim.58), channel_id=1, replica_groups=mesh['freq'=2,'row'=4,'col'=4] {'freq','row','col'}, dimensions={0} | all-to-all | bytes 524288 | tf_op jit(solution)/shard_map/all_to_all | solution.py:106
  107.5 1.0 multiply_reduce_fusion.3
  112.6 1.1 fusion.43
  114.0 12.6 %all_to_all.40 = f32[32,1,2048]{2,1,0:T(1,128)S(1)} all-to-all(f32[32,1,2048]{2,1,0:T(1,128)S(1)} %all_to_all.32), channel_id=1, replica_groups=mesh['freq'=2,'row'=4,'col'=4] {'freq','row','col'}, dimensions={0} | all-to-all | bytes 524288 | tf_op jit(solution)/shard_map/all_to_all | solution.py:103
  126.9 12.6 %all_to_all.41 = f32[32,1,2048]{2,1,0:T(1,128)S(1)} all-to-all(f32[32,1,2048]{2,1,0:T(1,128)S(1)} %broadcast_in_dim.59), channel_id=1, replica_groups=mesh['freq'=2,'row'=4,'col'=4] {'freq','row','col'}, dimensions={0} | all-to-all | bytes 524288 | tf_op jit(solution)/shard_map/all_to_all | solution.py:106
  140.4 1.0 multiply_reduce_fusion.2
  145.4 1.2 convolution_convert_fusion
  (80 shorter events, 13.9 us)
Async XLA Ops:
  0.6 54.2 %copy-start = (bf16[512,512]{1,0:T(8,128)(2,1)S(1)}, bf16[512,512]{1,0:T(8,128)(2,1)}, u32[]{:S(2)}) copy-start(bf16[512,512]{1,0:T(8,128)(2,1)} %param.6) | copy-start | bytes 1572868
  3.7 7.3 %copy-start.4 = (f32[256]{0:T(256)S(1)}, f32[256]{0:T(256)}, u32[]{:S(2)}) copy-start(f32[256]{0:T(256)} %param.5) | copy-start | bytes 3076
  4.8 16.4 %collective-permute-start = (bf16[256,8,128]{0,2,1:T(8,128)(2,1)}, bf16[256,8,128]{0,2,1:T(8,128)(2,1)S(1)}, u32[]{:S(2)}, u32[]{:S(2)}) collective-permute-start(bf16[256,8,128]{0,2,1:T(8,128)(2,1)} %get-tuple-element.6), channel_id=1, source_target_pairs={{0,4},{4,8},{8,12},{1,5},{5,9},{9,13},{2,6},{6,10},{10,14},{3,7},{... | collective-permute-start | bytes 1572872 | tf_op jit(solution)/shard_map/ppermute | solution.py:64
  9.7 15.6 %collective-permute-start.1 = (bf16[256,8,128]{0,2,1:T(8,128)(2,1)}, bf16[256,8,128]{0,2,1:T(8,128)(2,1)}, u32[]{:S(2)}, u32[]{:S(2)}) collective-permute-start(bf16[256,8,128]{0,2,1:T(8,128)(2,1)} %get-tuple-element.7), channel_id=1, source_target_pairs={{4,0},{8,4},{12,8},{5,1},{9,5},{13,9},{6,2},{10,6},{14,10},{7,3},{... | collective-permute-start | bytes 1572872 | tf_op jit(solution)/shard_map/ppermute | solution.py:67
  28.4 1.8 %copy-start.1 = (bf16[16,8,16,256]{3,2,1,0:T(8,128)(2,1)S(1)}, bf16[16,8,16,256]{3,2,1,0:T(8,128)(2,1)}, u32[]{:S(2)}) copy-start(bf16[16,8,16,256]{3,2,1,0:T(8,128)(2,1)} %copy.110) | copy-start | bytes 3145732
  30.5 10.3 %collective-permute-start.2 = (bf16[256,32,8]{0,2,1:T(8,128)(2,1)S(1)}, bf16[256,32,8]{0,2,1:T(8,128)(2,1)S(1)}, u32[]{:S(2)}, u32[]{:S(2)}) collective-permute-start(bf16[256,32,8]{0,2,1:T(8,128)(2,1)S(1)} %get-tuple-element.2), channel_id=1, source_target_pairs={{0,1},{1,2},{2,3},{4,5},{5,6},{6,7},{8,9},{9,10},{10,11},{12,13},{... | collective-permute-start | bytes 393224 | tf_op jit(solution)/shard_map/ppermute | solution.py:64
  31.8 10.3 %collective-permute-start.3 = (bf16[256,32,8]{0,2,1:T(8,128)(2,1)S(1)}, bf16[256,32,8]{0,2,1:T(8,128)(2,1)S(1)}, u32[]{:S(2)}, u32[]{:S(2)}) collective-permute-start(bf16[256,32,8]{0,2,1:T(8,128)(2,1)S(1)} %get-tuple-element.3), channel_id=1, source_target_pairs={{1,0},{2,1},{3,2},{5,4},{6,5},{7,6},{9,8},{10,9},{11,10},{13,12},{... | collective-permute-start | bytes 393224 | tf_op jit(solution)/shard_map/ppermute | solution.py:67
  34.1 0.7 copy-start.5
  44.8 29.2 %collective-permute-start.4 = (bf16[256,2048]{0,1:T(8,128)(2,1)}, bf16[256,2048]{0,1:T(8,128)(2,1)}, u32[]{:S(2)}, u32[]{:S(2)}) collective-permute-start(bf16[256,2048]{0,1:T(8,128)(2,1)} %constant_dynamic-slice_fusion), channel_id=1, source_target_pairs={{0,16},{16,0},{1,17},{17,1},{2,18},{18,2},{3,19},{19,3},{4,20},{20... | collective-permute-start | bytes 3145736 | tf_op jit(solution)/shard_map/ppermute | solution.py:132
  47.8 25.7 %all-to-all-start = ((f32[32,1,512]{2,1,0:T(1,128)}), f32[32,1,512]{2,1,0:T(1,128)S(1)}, u32[]{:S(2)}, u32[]{:S(2)}) async-start(f32[32,1,512]{2,1,0:T(1,128)} %broadcast_in_dim.57), calls=%async_computation | async-start | bytes 131072 | tf_op jit(solution)/shard_map/all_to_all | solution.py:115
  74.0 3.4 %copy-start.2 = (f32[128,512]{1,0:T(8,128)S(1)}, f32[128,512]{1,0:T(8,128)}, u32[]{:S(2)}) copy-start(f32[128,512]{1,0:T(8,128)} %param.7) | copy-start | bytes 786436
  145.4 1.3 copy-start.3

commit v6 on v5

--- a/solution.py
+++ b/solution.py
@@ -53,24 +53,39 @@
     return out[0].astype(jnp.bfloat16)
 
 
-def split_pass(cells, kernel, axis, dim):
+def halos(cells, axis, dim):
+    length = cells.shape[dim]
+    count = lax.axis_size(axis)
+    ends = count - 1
+    before = lax.ppermute(
+        lax.slice_in_dim(cells, length - HALF, length, axis=dim), axis, [(i, (i + 1) % count) for i in range(ends)]
+    )
+    after = lax.ppermute(
+        lax.slice_in_dim(cells, 0, HALF, axis=dim), axis, [((i + 1) % count, i) for i in range(ends)]
+    )
+    return before, after
+
+
+def assemble(cells, before, after, kernel, dim):
     length = cells.shape[dim]
     if length < 4 * HALF:
-        return depthwise(with_halo(cells, ((axis, dim),), HALF), kernel)
-    count = lax.axis_size(axis)
-    ends = count - 1
+        return depthwise(jnp.concatenate([before, cells, after], axis=dim), kernel)
     head = lax.slice_in_dim(cells, 0, 2 * HALF, axis=dim)
     tail = lax.slice_in_dim(cells, length - 2 * HALF, length, axis=dim)
-    before = lax.ppermute(
-        lax.slice_in_dim(tail, HALF, 2 * HALF, axis=dim), axis, [(i, (i + 1) % count) for i in range(ends)]
-    )
-    after = lax.ppermute(
-        lax.slice_in_dim(head, 0, HALF, axis=dim), axis, [((i + 1) % count, i) for i in range(ends)]
-    )
     middle = depthwise(cells, kernel)
     first = depthwise(jnp.concatenate([before, head], axis=dim), kernel)
     last = depthwise(jnp.concatenate([tail, after], axis=dim), kernel)
     return jnp.concatenate([first, middle, last], axis=dim)
+
+
+def split_pass(cells, kernel, axis, dim):
+    before, after = halos(cells, axis, dim)
+    return assemble(cells, before, after, kernel, dim)
+
+
+def band_of_rows(cells, before, after, kernel, start, rows):
+    pick = lambda part: lax.dynamic_slice_in_dim(part, start, rows, axis=1)
+    return assemble(pick(cells), pick(before), pick(after), kernel, 2)
 
 
 def inverse_root(matrix):
@@ -120,18 +135,21 @@
     beam_taps = lax.optimization_barrier(make_taps(beam_sigma))
     channels, height, breadth = sky_maps.shape
     rowwise = split_pass(sky_maps, beam_taps[:, None, :, None], "row", 1)
-    smoothed = split_pass(rowwise, beam_taps[:, None, None, :], "col", 2)
-    flattened = smoothed.reshape(channels, height * breadth)
+    column_kernel = beam_taps[:, None, None, :]
     parts = lax.axis_size("freq")
     devices = parts * lax.axis_size("row") * lax.axis_size("col")
     block = height * breadth // parts
     total_pixels = block * devices
-    if parts == 2:
+    if parts == 2 and height % parts == 0:
         side = lax.axis_index("freq")
-        outgoing = lax.dynamic_slice_in_dim(flattened, (1 - side) * block, block, axis=1)
+        half = height // parts
+        before, after = halos(rowwise, "col", 2)
+        outgoing = band_of_rows(rowwise, before, after, column_kernel, (1 - side) * half, half)
+        outgoing = outgoing.reshape(channels, block)
         incoming = lax.ppermute(outgoing, "freq", [(0, 1), (1, 0)])
-        local = lax.dynamic_slice_in_dim(flattened, side * block, block, axis=1)
-        plane_sums = jnp.sum(lax.optimization_barrier(flattened), axis=1, dtype=jnp.float32)
+        local = band_of_rows(rowwise, before, after, column_kernel, side * half, half)
+        local = local.reshape(channels, block)
+        plane_sums = jnp.sum(outgoing, axis=1, dtype=jnp.float32) + jnp.sum(local, axis=1, dtype=jnp.float32)
         placed = jnp.zeros((parts * channels,), jnp.float32)
         placed = lax.dynamic_update_slice_in_dim(placed, plane_sums, side * channels, axis=0)
         channel_sums = gathered_sum(placed, ("freq", "row", "col"))
@@ -143,6 +161,8 @@
             theirs, incoming, preferred_element_type=jnp.float32
         )
     else:
+        smoothed = split_pass(rowwise, column_kernel, "col", 2)
+        flattened = smoothed.reshape(channels, height * breadth)
         spectra = lax.all_to_all(flattened, "freq", split_axis=1, concat_axis=0, tiled=True)
         channel_sums = gathered_sum(jnp.sum(spectra, axis=1, dtype=jnp.float32), ("freq", "row", "col"))
         means = channel_sums / total_pixels

time: 147 us -> 146 us (level)
  local copies, waits for them, and re-layouts: 12.5 us -> 11 us
    convert_element_type x5 -> x7, local copies, waits for them, and re-layouts: 3.45 us -> 3.3 us  [depthwise(): return out[0].astype(jnp.bfloat16)]
    unnamed x15 -> x17, local copies, waits for them, and re-layouts: 3.22 us -> 3.13 us
    conv_general_dilated x6 -> x9, matrix products: 16.5 us -> 16.5 us  [depthwise(): lax.conv_general_dilated(cells[None], kernel, window_strides=(1, 1), padd...]
  transfers between devices with their start and end apart: 6 -> 6, of which waited for: 3 -> 3; matrix products, arithmetic and copies ran while one was open for 15% -> 14% of each run, Pallas kernels for 0% -> 0%
where the time goes in v6:
time: 146 us
  blocking collectives  51.9 us (36%)
  matrix products  35.9 us (25%)
  waiting for transfers between devices  22.2 us (15%)
  starting transfers between devices  17.4 us (12%)
  local copies, waits for them, and re-layouts  11 us (8%)
  other arithmetic  4.54 us (3%)
  between operations  2.85 us (2%)
    all_to_all x2, blocking collectives, total_sum(): pieces = lax.all_to_all(flat, axes, 0, 0, tiled=True)  26.6 us
    all_to_all x2, blocking collectives, total_sum(): gathered = lax.all_to_all(spread, axes, 0, 0, tiled=True)  25.3 us
    conv_general_dilated x9, matrix products, depthwise(): lax.conv_general_dilated(cells[None], kernel, window_strides=(1, 1), padd...  16.5 us
    all_to_all x1, waiting for transfers between devices, gathered_sum(): gathered = lax.all_to_all(spread, axes, 0, 0, tiled=True)  16.2 us
    all_to_all x1, starting transfers between devices, gathered_sum(): gathered = lax.all_to_all(spread, axes, 0, 0, tiled=True)  6.85 us
    ppermute x2, starting transfers between devices, halos(): lax.ppermute(lax.slice_in_dim(cells, length - HALF, length, axis=dim), ax...  6.25 us
    ppermute x2, waiting for transfers between devices, halos(): lax.ppermute(lax.slice_in_dim(cells, 0, HALF, axis=dim), axis, [((i + 1)...  4.15 us
    dot_general x1, matrix products, shards(): jnp.dot(theirs, incoming, preferred_element_type=jnp.float32)  3.38 us
  transfers between devices with their start and end apart: 6, of which 3 were waited for; matrix products, arithmetic and copies ran while one was open for 14% of the time, Pallas kernels for 0%

profile of v6, /device:TPU:0, one launch (start us, length us, event | category | flops | bytes accessed | tf_op | source)
XLA Modules:
  0.0 145.7 jit_solution(11262069490210157182)
XLA Ops:
  0.6 3.0 %copy.194 = bf16[256,32,128]{0,2,1:T(8,128)(2,1)S(1)} copy(bf16[256,32,128]{2,1,0:T(8,128)(2,1)} %param.4) | data formatting | bytes 4194304 | tf_op args[0]
  3.7 1.0 fusion.99
  4.8 4.9 %collective-permute-start = (bf16[256,8,128]{0,2,1:T(8,128)(2,1)}, bf16[256,8,128]{0,2,1:T(8,128)(2,1)S(1)}, u32[]{:S(2)}, u32[]{:S(2)}) collective-permute-start(bf16[256,8,128]{0,2,1:T(8,128)(2,1)} %get-tuple-element.14), channel_id=1, source_target_pairs={{0,4},{4,8},{8,12},{1,5},{5,9},{9,13},{2,6},{6,10},{10,14},{3,7},{... | collective-permute-start | bytes 1572872 | tf_op jit(solution)/shard_map/ppermute | solution.py:60
  9.7 1.3 collective-permute-start.1
  11.2 5.4 %fusion.23 = bf16[16,8,16,256]{3,1,2,0:T(8,128)(2,1)} fusion(bf16[256,32,8,16]{0,3,2,1:T(8,128)(2,1)S(1)} %bitcast.133, bf16[256,1,17,1]{0,2,3,1:T(8,128)(2,1)S(1)} %bitcast.149), kind=kOutput, calls=%fused_computation.34 | convolution fusion | flops 18350080 | bytes 3154432 | tf_op jit(solution)/shard_map/conv_general_dilated | solution.py:44
  16.7 2.5 %copy.202 = bf16[16,8,16,256]{3,2,1,0:T(8,128)(2,1)} copy(bf16[16,8,16,256]{3,1,2,0:T(8,128)(2,1)} %fusion.23) | data formatting | bytes 2097152 | tf_op jit(solution)/shard_map/convert_element_type | solution.py:53
  19.3 1.8 %collective-permute-done = bf16[256,8,128]{0,2,1:T(8,128)(2,1)S(1)} collective-permute-done((bf16[256,8,128]{0,2,1:T(8,128)(2,1)}, bf16[256,8,128]{0,2,1:T(8,128)(2,1)S(1)}, u32[]{:S(2)}, u32[]{:S(2)}) %collective-permute-start) | collective-permute-done | bytes 524320 | tf_op jit(solution)/shard_map/ppermute | solution.py:60
  21.2 4.1 %collective-permute-done.1 = bf16[256,8,128]{0,2,1:T(8,128)(2,1)} collective-permute-done((bf16[256,8,128]{0,2,1:T(8,128)(2,1)}, bf16[256,8,128]{0,2,1:T(8,128)(2,1)}, u32[]{:S(2)}, u32[]{:S(2)}) %collective-permute-start.1) | collective-permute-done | bytes 524320 | tf_op jit(solution)/shard_map/ppermute | solution.py:63
  25.3 1.3 pad_maximum_fusion.1
  26.6 1.7 %fusion.30 = bf16[8,8,16,256]{3,1,2,0:T(8,128)(2,1)S(1)} fusion(bf16[256,24,8,16]{0,3,2,1:T(8,128)(2,1)S(1)} %bitcast.143, bf16[256,1,17,1]{0,2,3,1:T(8,128)(2,1)S(1)} %bitcast.150), kind=kOutput, calls=%fused_computation.35 | convolution fusion | flops 9175040 | bytes 2105856 | tf_op jit(solution)/shard_map/conv_general_dilated | solution.py:44
  28.4 1.7 %fusion.33 = bf16[8,8,16,256]{3,1,2,0:T(8,128)(2,1)S(1)} fusion(bf16[256,24,8,16]{0,3,2,1:T(8,128)(2,1)S(1)} %bitcast.142, bf16[256,1,17,1]{0,2,3,1:T(8,128)(2,1)S(1)} %bitcast.151), kind=kOutput, calls=%fused_computation.36 | convolution fusion | flops 9175040 | bytes 2105856 | tf_op jit(solution)/shard_map/conv_general_dilated | solution.py:44
  30.5 1.3 collective-permute-start.2
  31.8 1.5 %collective-permute-start.3 = (bf16[256,32,8]{0,2,1:T(8,128)(2,1)S(1)}, bf16[256,32,8]{0,2,1:T(8,128)(2,1)S(1)}, u32[]{:S(2)}, u32[]{:S(2)}) collective-permute-start(bf16[256,32,8]{0,2,1:T(8,128)(2,1)S(1)} %get-tuple-element.13), channel_id=1, source_target_pairs={{1,0},{2,1},{3,2},{5,4},{6,5},{7,6},{9,8},{10,9},{11,10},{13,12},{... | collective-permute-start | bytes 393224 | tf_op jit(solution)/shard_map/ppermute | solution.py:63
  34.6 2.7 %select_convert_fusion.1 = bf16[16,8,16,256]{3,1,2,0:T(8,128)(2,1)S(1)} fusion(bf16[256,16,1,7,16]{0,3,4,1,2:T(8,128)(2,1)S(1)} %slice.52, bf16[256,16,1,8,16]{0,3,4,1,2:T(8,128)(2,1)S(1)} %copy.211, pred[8,16]{0,1:T(8,128)(4,1)S(1)} %copy-done.5, bf16[256,1,1,17]{0,3,2,1:T(8,128)(2,1)S(1)} %bitcast.152), kind=kOutput, calls=%fused_computation.22 | convolution fusion | flops 25165824 | bytes 3023488 | tf_op jit(solution)/shard_map/conv_general_dilated | solution.py:44
  37.9 2.7 %select_convert_fusion = bf16[16,8,16,256]{3,1,2,0:T(8,128)(2,1)S(1)} fusion(bf16[256,16,1,7,16]{0,3,4,1,2:T(8,128)(2,1)S(1)} %slice.55, bf16[256,16,1,8,16]{0,3,4,1,2:T(8,128)(2,1)S(1)} %copy.219, pred[8,16]{0,1:T(8,128)(4,1)S(1)} %copy-done.5, bf16[256,1,1,17]{0,3,2,1:T(8,128)(2,1)S(1)} %bitcast.153), kind=kOutput, calls=%fused_computation.21 | convolution fusion | flops 25165824 | bytes 3023488 | tf_op jit(solution)/shard_map/conv_general_dilated | solution.py:44
  44.0 1.6 %collective-permute-start.4 = (bf16[256,2048]{0,1:T(8,128)(2,1)S(1)}, bf16[256,2048]{0,1:T(8,128)(2,1)}, u32[]{:S(2)}, u32[]{:S(2)}) collective-permute-start(bf16[256,2048]{0,1:T(8,128)(2,1)S(1)} %bitcast.144), channel_id=1, source_target_pairs={{0,16},{16,0},{1,17},{17,1},{2,18},{18,2},{3,19},{19,3},{4,20},{20... | collective-permute-start | bytes 3145736 | tf_op jit(solution)/shard_map/ppermute | solution.py:149
  46.0 0.7 broadcast_in_dim.69
  46.7 6.9 %all-to-all-start = ((f32[32,1,512]{2,1,0:T(1,128)}), f32[32,1,512]{2,1,0:T(1,128)S(1)}, u32[]{:S(2)}, u32[]{:S(2)}) async-start(f32[32,1,512]{2,1,0:T(1,128)} %broadcast_in_dim.69), calls=%async_computation | async-start | bytes 131072 | tf_op jit(solution)/shard_map/all_to_all | solution.py:130
  53.6 2.7 %fusion.57 = f32[512,2048]{1,0:T(8,128)} fusion(bf16[256,2048]{0,1:T(8,128)(2,1)S(1)} %bitcast.137, bf16[512,512]{1,0:T(8,128)(2,1)S(1)} %copy-done, s32[]{:T(128)S(6)} %select_n.8), kind=kOutput, calls=%fused_computation.81 | convolution fusion | flops 536870912 | bytes 5505028 | tf_op jit(solution)/shard_map/dot_general | solution.py:160
  56.2 16.2 %all-to-all-done = f32[32,1,512]{2,1,0:T(1,128)S(1)} async-done(((f32[32,1,512]{2,1,0:T(1,128)}), f32[32,1,512]{2,1,0:T(1,128)S(1)}, u32[]{:S(2)}, u32[]{:S(2)}) %all-to-all-start) | async-done | bytes 65568 | tf_op jit(solution)/shard_map/all_to_all | solution.py:130
  73.0 3.4 %subtract_convert_fusion = bf16[512,2048]{1,0:T(8,128)(2,1)S(1)} fusion(f32[512,2048]{1,0:T(8,128)} %fusion.57, bf16[256,2048]{0,1:T(8,128)(2,1)} %collective-permute-done.4, f32[512]{0:T(512)S(1)} %bitcast.158, bf16[512,512]{1,0:T(8,128)(2,1)S(1)} %copy-done, s32[]{:T(128)S(6)} %select_n.19), kind=kOutput, calls=%fused_computation.3 | convolution fusion | flops 540016640 | bytes 7604228 | tf_op jit(solution)/shard_map/dot_general | solution.py:160
  76.4 2.1 %fusion.36 = f32[128,512]{1,0:T(8,128)S(1)} fusion(bf16[512,2048]{1,0:T(8,128)(2,1)S(1)} %subtract_convert_fusion, f32[128,512]{1,0:T(8,128)S(1)} %copy-done.2), kind=kOutput, calls=%fused_computation.37 | convolution fusion | flops 537722880 | bytes 2621440 | tf_op jit(solution)/shard_map/dot_general | solution.py:108
  78.8 14.0 %all_to_all.38 = f32[32,1,2048]{2,1,0:T(1,128)S(1)} all-to-all(f32[32,1,2048]{2,1,0:T(1,128)S(1)} %all_to_all.31), channel_id=1, replica_groups=mesh['freq'=2,'row'=4,'col'=4] {'freq','row','col'}, dimensions={0} | all-to-all | bytes 524288 | tf_op jit(solution)/shard_map/all_to_all | solution.py:118
  93.1 12.6 %all_to_all.39 = f32[32,1,2048]{2,1,0:T(1,128)S(1)} all-to-all(f32[32,1,2048]{2,1,0:T(1,128)S(1)} %broadcast_in_dim.70), channel_id=1, replica_groups=mesh['freq'=2,'row'=4,'col'=4] {'freq','row','col'}, dimensions={0} | all-to-all | bytes 524288 | tf_op jit(solution)/shard_map/all_to_all | solution.py:121
  105.7 0.7 multiply_reduce_fusion.1
  106.5 1.0 multiply_reduce_fusion.3
  111.6 1.1 fusion.50
  113.0 12.6 %all_to_all.40 = f32[32,1,2048]{2,1,0:T(1,128)S(1)} all-to-all(f32[32,1,2048]{2,1,0:T(1,128)S(1)} %all_to_all.32), channel_id=1, replica_groups=mesh['freq'=2,'row'=4,'col'=4] {'freq','row','col'}, dimensions={0} | all-to-all | bytes 524288 | tf_op jit(solution)/shard_map/all_to_all | solution.py:118
  125.9 12.6 %all_to_all.41 = f32[32,1,2048]{2,1,0:T(1,128)S(1)} all-to-all(f32[32,1,2048]{2,1,0:T(1,128)S(1)} %broadcast_in_dim.71), channel_id=1, replica_groups=mesh['freq'=2,'row'=4,'col'=4] {'freq','row','col'}, dimensions={0} | all-to-all | bytes 524288 | tf_op jit(solution)/shard_map/all_to_all | solution.py:121
  138.6 0.7 multiply_reduce_fusion
  139.4 1.0 multiply_reduce_fusion.2
  144.4 1.2 convolution_convert_fusion
  (93 shorter events, 14.8 us)
Async XLA Ops:
  0.6 52.9 %copy-start = (bf16[512,512]{1,0:T(8,128)(2,1)S(1)}, bf16[512,512]{1,0:T(8,128)(2,1)}, u32[]{:S(2)}) copy-start(bf16[512,512]{1,0:T(8,128)(2,1)} %param.6) | copy-start | bytes 1572868
  3.7 7.3 %copy-start.4 = (f32[256]{0:T(256)S(1)}, f32[256]{0:T(256)}, u32[]{:S(2)}) copy-start(f32[256]{0:T(256)} %param.5) | copy-start | bytes 3076
  4.8 16.4 %collective-permute-start = (bf16[256,8,128]{0,2,1:T(8,128)(2,1)}, bf16[256,8,128]{0,2,1:T(8,128)(2,1)S(1)}, u32[]{:S(2)}, u32[]{:S(2)}) collective-permute-start(bf16[256,8,128]{0,2,1:T(8,128)(2,1)} %get-tuple-element.14), channel_id=1, source_target_pairs={{0,4},{4,8},{8,12},{1,5},{5,9},{9,13},{2,6},{6,10},{10,14},{3,7},{... | collective-permute-start | bytes 1572872 | tf_op jit(solution)/shard_map/ppermute | solution.py:60
  9.7 15.6 %collective-permute-start.1 = (bf16[256,8,128]{0,2,1:T(8,128)(2,1)}, bf16[256,8,128]{0,2,1:T(8,128)(2,1)}, u32[]{:S(2)}, u32[]{:S(2)}) collective-permute-start(bf16[256,8,128]{0,2,1:T(8,128)(2,1)} %get-tuple-element.15), channel_id=1, source_target_pairs={{4,0},{8,4},{12,8},{5,1},{9,5},{13,9},{6,2},{10,6},{14,10},{7,3},{... | collective-permute-start | bytes 1572872 | tf_op jit(solution)/shard_map/ppermute | solution.py:63
  28.4 1.8 %copy-start.1 = (bf16[16,8,16,256]{3,2,1,0:T(8,128)(2,1)S(1)}, bf16[16,8,16,256]{3,2,1,0:T(8,128)(2,1)}, u32[]{:S(2)}) copy-start(bf16[16,8,16,256]{3,2,1,0:T(8,128)(2,1)} %copy.202) | copy-start | bytes 3145732
  30.5 10.4 %collective-permute-start.2 = (bf16[256,32,8]{0,2,1:T(8,128)(2,1)S(1)}, bf16[256,32,8]{0,2,1:T(8,128)(2,1)S(1)}, u32[]{:S(2)}, u32[]{:S(2)}) collective-permute-start(bf16[256,32,8]{0,2,1:T(8,128)(2,1)S(1)} %get-tuple-element.12), channel_id=1, source_target_pairs={{0,1},{1,2},{2,3},{4,5},{5,6},{6,7},{8,9},{9,10},{10,11},{12,13},{... | collective-permute-start | bytes 393224 | tf_op jit(solution)/shard_map/ppermute | solution.py:60
  31.8 9.7 %collective-permute-start.3 = (bf16[256,32,8]{0,2,1:T(8,128)(2,1)S(1)}, bf16[256,32,8]{0,2,1:T(8,128)(2,1)S(1)}, u32[]{:S(2)}, u32[]{:S(2)}) collective-permute-start(bf16[256,32,8]{0,2,1:T(8,128)(2,1)S(1)} %get-tuple-element.13), channel_id=1, source_target_pairs={{1,0},{2,1},{3,2},{5,4},{6,5},{7,6},{9,8},{10,9},{11,10},{13,12},{... | collective-permute-start | bytes 393224 | tf_op jit(solution)/shard_map/ppermute | solution.py:63
  33.9 0.7 copy-start.5
  44.0 29.1 %collective-permute-start.4 = (bf16[256,2048]{0,1:T(8,128)(2,1)S(1)}, bf16[256,2048]{0,1:T(8,128)(2,1)}, u32[]{:S(2)}, u32[]{:S(2)}) collective-permute-start(bf16[256,2048]{0,1:T(8,128)(2,1)S(1)} %bitcast.144), channel_id=1, source_target_pairs={{0,16},{16,0},{1,17},{17,1},{2,18},{18,2},{3,19},{19,3},{4,20},{20... | collective-permute-start | bytes 3145736 | tf_op jit(solution)/shard_map/ppermute | solution.py:149
  46.7 25.7 %all-to-all-start = ((f32[32,1,512]{2,1,0:T(1,128)}), f32[32,1,512]{2,1,0:T(1,128)S(1)}, u32[]{:S(2)}, u32[]{:S(2)}) async-start(f32[32,1,512]{2,1,0:T(1,128)} %broadcast_in_dim.69), calls=%async_computation | async-start | bytes 131072 | tf_op jit(solution)/shard_map/all_to_all | solution.py:130
  73.0 3.4 %copy-start.2 = (f32[128,512]{1,0:T(8,128)S(1)}, f32[128,512]{1,0:T(8,128)}, u32[]{:S(2)}) copy-start(f32[128,512]{1,0:T(8,128)} %param.7) | copy-start | bytes 786436
  144.4 1.3 copy-start.3

commit v7 on v6

--- a/solution.py
+++ b/solution.py
@@ -147,6 +147,7 @@
         outgoing = band_of_rows(rowwise, before, after, column_kernel, (1 - side) * half, half)
         outgoing = outgoing.reshape(channels, block)
         incoming = lax.ppermute(outgoing, "freq", [(0, 1), (1, 0)])
+        outgoing, rowwise, before, after = lax.optimization_barrier((outgoing, rowwise, before, after))
         local = band_of_rows(rowwise, before, after, column_kernel, side * half, half)
         local = local.reshape(channels, block)
         plane_sums = jnp.sum(outgoing, axis=1, dtype=jnp.float32) + jnp.sum(local, axis=1, dtype=jnp.float32)

time: 146 us -> 141 us (0.966)
  waiting for transfers between devices: 22.2 us -> 16.9 us
    all_to_all x1, waiting for transfers between devices: 16.2 us -> 10.9 us  [gathered_sum(): gathered = lax.all_to_all(spread, axes, 0, 0, tiled=True)]
  transfers between devices with their start and end apart: 6 -> 6, of which waited for: 3 -> 3; matrix products, arithmetic and copies ran while one was open for 14% -> 16% of each run, Pallas kernels for 0% -> 0%
where the time goes in v7:
time: 141 us; the launch traced here: 140 us
  blocking collectives  51.9 us (37%)
  matrix products  35.9 us (25%)
  starting transfers between devices  17.4 us (12%)
  waiting for transfers between devices  16.9 us (12%)
  local copies, waits for them, and re-layouts  11 us (8%)
  other arithmetic  4.52 us (3%)
  between operations  2.89 us (2%)
    all_to_all x2, blocking collectives, total_sum(): pieces = lax.all_to_all(flat, axes, 0, 0, tiled=True)  26.6 us
    all_to_all x2, blocking collectives, total_sum(): gathered = lax.all_to_all(spread, axes, 0, 0, tiled=True)  25.3 us
    conv_general_dilated x9, matrix products, depthwise(): lax.conv_general_dilated(cells[None], kernel, window_strides=(1, 1), padd...  16.5 us
    all_to_all x1, waiting for transfers between devices, gathered_sum(): gathered = lax.all_to_all(spread, axes, 0, 0, tiled=True)  10.9 us
    all_to_all x1, starting transfers between devices, gathered_sum(): gathered = lax.all_to_all(spread, axes, 0, 0, tiled=True)  6.85 us
    ppermute x2, starting transfers between devices, halos(): lax.ppermute(lax.slice_in_dim(cells, length - HALF, length, axis=dim), ax...  6.25 us
    ppermute x2, waiting for transfers between devices, halos(): lax.ppermute(lax.slice_in_dim(cells, 0, HALF, axis=dim), axis, [((i + 1)...  4.15 us
    dot_general x1, matrix products, shards(): jnp.dot(theirs, incoming, preferred_element_type=jnp.float32)  3.38 us
  transfers between devices with their start and end apart: 6, of which 3 were waited for; matrix products, arithmetic and copies ran while one was open for 16% of the time, Pallas kernels for 0%

profile of v7, /device:TPU:0, one launch (start us, length us, event | category | flops | bytes accessed | tf_op | source)
XLA Modules:
  0.0 140.5 jit_solution(15621838177361308889)
XLA Ops:
  0.6 3.0 %copy.194 = bf16[256,32,128]{0,2,1:T(8,128)(2,1)S(1)} copy(bf16[256,32,128]{2,1,0:T(8,128)(2,1)} %param.4) | data formatting | bytes 4194304 | tf_op args[0]
  3.7 1.0 fusion.99
  4.8 4.9 %collective-permute-start = (bf16[256,8,128]{0,2,1:T(8,128)(2,1)}, bf16[256,8,128]{0,2,1:T(8,128)(2,1)S(1)}, u32[]{:S(2)}, u32[]{:S(2)}) collective-permute-start(bf16[256,8,128]{0,2,1:T(8,128)(2,1)} %get-tuple-element.18), channel_id=1, source_target_pairs={{0,4},{4,8},{8,12},{1,5},{5,9},{9,13},{2,6},{6,10},{10,14},{3,7},{... | collective-permute-start | bytes 1572872 | tf_op jit(solution)/shard_map/ppermute | solution.py:60
  9.7 1.3 collective-permute-start.1
  11.2 5.4 %fusion.23 = bf16[16,8,16,256]{3,1,2,0:T(8,128)(2,1)} fusion(bf16[256,32,8,16]{0,3,2,1:T(8,128)(2,1)S(1)} %bitcast.133, bf16[256,1,17,1]{0,2,3,1:T(8,128)(2,1)S(1)} %bitcast.150), kind=kOutput, calls=%fused_computation.34 | convolution fusion | flops 18350080 | bytes 3154432 | tf_op jit(solution)/shard_map/conv_general_dilated | solution.py:44
  16.7 2.5 %copy.202 = bf16[16,8,16,256]{3,2,1,0:T(8,128)(2,1)} copy(bf16[16,8,16,256]{3,1,2,0:T(8,128)(2,1)} %fusion.23) | data formatting | bytes 2097152 | tf_op jit(solution)/shard_map/convert_element_type | solution.py:53
  19.3 1.8 %collective-permute-done = bf16[256,8,128]{0,2,1:T(8,128)(2,1)S(1)} collective-permute-done((bf16[256,8,128]{0,2,1:T(8,128)(2,1)}, bf16[256,8,128]{0,2,1:T(8,128)(2,1)S(1)}, u32[]{:S(2)}, u32[]{:S(2)}) %collective-permute-start) | collective-permute-done | bytes 524320 | tf_op jit(solution)/shard_map/ppermute | solution.py:60
  21.2 4.1 %collective-permute-done.1 = bf16[256,8,128]{0,2,1:T(8,128)(2,1)} collective-permute-done((bf16[256,8,128]{0,2,1:T(8,128)(2,1)}, bf16[256,8,128]{0,2,1:T(8,128)(2,1)}, u32[]{:S(2)}, u32[]{:S(2)}) %collective-permute-start.1) | collective-permute-done | bytes 524320 | tf_op jit(solution)/shard_map/ppermute | solution.py:63
  25.3 1.3 pad_maximum_fusion.1
  26.6 1.7 %fusion.30 = bf16[8,8,16,256]{3,1,2,0:T(8,128)(2,1)S(1)} fusion(bf16[256,24,8,16]{0,3,2,1:T(8,128)(2,1)S(1)} %bitcast.145, bf16[256,1,17,1]{0,2,3,1:T(8,128)(2,1)S(1)} %bitcast.151), kind=kOutput, calls=%fused_computation.35 | convolution fusion | flops 9175040 | bytes 2105856 | tf_op jit(solution)/shard_map/conv_general_dilated | solution.py:44
  28.4 1.7 %fusion.33 = bf16[8,8,16,256]{3,1,2,0:T(8,128)(2,1)S(1)} fusion(bf16[256,24,8,16]{0,3,2,1:T(8,128)(2,1)S(1)} %bitcast.144, bf16[256,1,17,1]{0,2,3,1:T(8,128)(2,1)S(1)} %bitcast.152), kind=kOutput, calls=%fused_computation.36 | convolution fusion | flops 9175040 | bytes 2105856 | tf_op jit(solution)/shard_map/conv_general_dilated | solution.py:44
  30.5 1.3 collective-permute-start.2
  31.8 1.5 %collective-permute-start.3 = (bf16[256,32,8]{0,2,1:T(8,128)(2,1)S(1)}, bf16[256,32,8]{0,2,1:T(8,128)(2,1)S(1)}, u32[]{:S(2)}, u32[]{:S(2)}) collective-permute-start(bf16[256,32,8]{0,2,1:T(8,128)(2,1)S(1)} %get-tuple-element.15), channel_id=1, source_target_pairs={{1,0},{2,1},{3,2},{5,4},{6,5},{7,6},{9,8},{10,9},{11,10},{13,12},{... | collective-permute-start | bytes 393224 | tf_op jit(solution)/shard_map/ppermute | solution.py:63
  34.1 2.7 %select_convert_fusion.1 = bf16[16,8,16,256]{3,1,2,0:T(8,128)(2,1)S(1)} fusion(bf16[256,16,1,7,16]{0,3,4,1,2:T(8,128)(2,1)S(1)} %slice.52, bf16[256,16,1,8,16]{0,3,4,1,2:T(8,128)(2,1)S(1)} %copy.211, pred[8,16]{0,1:T(8,128)(4,1)S(1)} %copy-done.5, bf16[256,1,1,17]{0,3,2,1:T(8,128)(2,1)S(1)} %bitcast.153), kind=kOutput, calls=%fused_computation.22 | convolution fusion | flops 25165824 | bytes 3023488 | tf_op jit(solution)/shard_map/conv_general_dilated | solution.py:44
  38.8 1.6 %collective-permute-start.4 = (bf16[256,2048]{0,1:T(8,128)(2,1)S(1)}, bf16[256,2048]{0,1:T(8,128)(2,1)}, u32[]{:S(2)}, u32[]{:S(2)}) collective-permute-start(bf16[256,2048]{0,1:T(8,128)(2,1)S(1)} %bitcast.136), channel_id=1, source_target_pairs={{0,16},{16,0},{1,17},{17,1},{2,18},{18,2},{3,19},{19,3},{4,20},{20... | collective-permute-start | bytes 3145736 | tf_op jit(solution)/shard_map/ppermute | solution.py:149
  42.6 2.7 %select_convert_fusion = bf16[16,8,16,256]{3,1,2,0:T(8,128)(2,1)S(1)} fusion(bf16[256,16,1,7,16]{0,3,4,1,2:T(8,128)(2,1)S(1)} %slice.55, bf16[256,16,1,8,16]{0,3,4,1,2:T(8,128)(2,1)S(1)} %copy.219, pred[8,16]{0,1:T(8,128)(4,1)S(1)} %copy-done.5, bf16[256,1,1,17]{0,3,2,1:T(8,128)(2,1)S(1)} %bitcast.158), kind=kOutput, calls=%fused_computation.21 | convolution fusion | flops 25165824 | bytes 3023488 | tf_op jit(solution)/shard_map/conv_general_dilated | solution.py:44
  46.1 0.7 broadcast_in_dim.69
  46.8 6.9 %all-to-all-start = ((f32[32,1,512]{2,1,0:T(1,128)}), f32[32,1,512]{2,1,0:T(1,128)S(1)}, u32[]{:S(2)}, u32[]{:S(2)}) async-start(f32[32,1,512]{2,1,0:T(1,128)} %broadcast_in_dim.69), calls=%async_computation | async-start | bytes 131072 | tf_op jit(solution)/shard_map/all_to_all | solution.py:130
  53.6 2.7 %fusion.57 = f32[512,2048]{1,0:T(8,128)} fusion(bf16[256,2048]{0,1:T(8,128)(2,1)S(1)} %bitcast.139, bf16[512,512]{1,0:T(8,128)(2,1)S(1)} %copy-done, s32[]{:T(128)S(6)} %select_n.8), kind=kOutput, calls=%fused_computation.81 | convolution fusion | flops 536870912 | bytes 5505028 | tf_op jit(solution)/shard_map/dot_general | solution.py:161
  56.3 10.9 %all-to-all-done = f32[32,1,512]{2,1,0:T(1,128)S(1)} async-done(((f32[32,1,512]{2,1,0:T(1,128)}), f32[32,1,512]{2,1,0:T(1,128)S(1)}, u32[]{:S(2)}, u32[]{:S(2)}) %all-to-all-start) | async-done | bytes 65568 | tf_op jit(solution)/shard_map/all_to_all | solution.py:130
  67.8 3.4 %subtract_convert_fusion = bf16[512,2048]{1,0:T(8,128)(2,1)S(1)} fusion(f32[512,2048]{1,0:T(8,128)} %fusion.57, bf16[256,2048]{0,1:T(8,128)(2,1)} %collective-permute-done.4, f32[512]{0:T(512)S(1)} %bitcast.159, bf16[512,512]{1,0:T(8,128)(2,1)S(1)} %copy-done, s32[]{:T(128)S(6)} %select_n.20), kind=kOutput, calls=%fused_computation.3 | convolution fusion | flops 540016640 | bytes 7604228 | tf_op jit(solution)/shard_map/dot_general | solution.py:161
  71.2 2.1 %fusion.36 = f32[128,512]{1,0:T(8,128)S(1)} fusion(bf16[512,2048]{1,0:T(8,128)(2,1)S(1)} %subtract_convert_fusion, f32[128,512]{1,0:T(8,128)S(1)} %copy-done.2), kind=kOutput, calls=%fused_computation.37 | convolution fusion | flops 537722880 | bytes 2621440 | tf_op jit(solution)/shard_map/dot_general | solution.py:108
  73.6 14.0 %all_to_all.38 = f32[32,1,2048]{2,1,0:T(1,128)S(1)} all-to-all(f32[32,1,2048]{2,1,0:T(1,128)S(1)} %all_to_all.31), channel_id=1, replica_groups=mesh['freq'=2,'row'=4,'col'=4] {'freq','row','col'}, dimensions={0} | all-to-all | bytes 524288 | tf_op jit(solution)/shard_map/all_to_all | solution.py:118
  87.9 12.6 %all_to_all.39 = f32[32,1,2048]{2,1,0:T(1,128)S(1)} all-to-all(f32[32,1,2048]{2,1,0:T(1,128)S(1)} %broadcast_in_dim.70), channel_id=1, replica_groups=mesh['freq'=2,'row'=4,'col'=4] {'freq','row','col'}, dimensions={0} | all-to-all | bytes 524288 | tf_op jit(solution)/shard_map/all_to_all | solution.py:121
  100.5 0.7 multiply_reduce_fusion.1
  101.3 1.0 multiply_reduce_fusion.3
  106.4 1.1 fusion.50
  107.8 12.6 %all_to_all.40 = f32[32,1,2048]{2,1,0:T(1,128)S(1)} all-to-all(f32[32,1,2048]{2,1,0:T(1,128)S(1)} %all_to_all.32), channel_id=1, replica_groups=mesh['freq'=2,'row'=4,'col'=4] {'freq','row','col'}, dimensions={0} | all-to-all | bytes 524288 | tf_op jit(solution)/shard_map/all_to_all | solution.py:118
  120.8 12.6 %all_to_all.41 = f32[32,1,2048]{2,1,0:T(1,128)S(1)} all-to-all(f32[32,1,2048]{2,1,0:T(1,128)S(1)} %broadcast_in_dim.71), channel_id=1, replica_groups=mesh['freq'=2,'row'=4,'col'=4] {'freq','row','col'}, dimensions={0} | all-to-all | bytes 524288 | tf_op jit(solution)/shard_map/all_to_all | solution.py:121
  133.4 0.7 multiply_reduce_fusion
  134.2 1.0 multiply_reduce_fusion.2
  139.2 1.2 convolution_convert_fusion
  (98 shorter events, 14.9 us)
Async XLA Ops:
  0.6 53.0 %copy-start = (bf16[512,512]{1,0:T(8,128)(2,1)S(1)}, bf16[512,512]{1,0:T(8,128)(2,1)}, u32[]{:S(2)}) copy-start(bf16[512,512]{1,0:T(8,128)(2,1)} %param.6) | copy-start | bytes 1572868
  3.7 7.3 %copy-start.4 = (f32[256]{0:T(256)S(1)}, f32[256]{0:T(256)}, u32[]{:S(2)}) copy-start(f32[256]{0:T(256)} %param.5) | copy-start | bytes 3076
  4.8 16.4 %collective-permute-start = (bf16[256,8,128]{0,2,1:T(8,128)(2,1)}, bf16[256,8,128]{0,2,1:T(8,128)(2,1)S(1)}, u32[]{:S(2)}, u32[]{:S(2)}) collective-permute-start(bf16[256,8,128]{0,2,1:T(8,128)(2,1)} %get-tuple-element.18), channel_id=1, source_target_pairs={{0,4},{4,8},{8,12},{1,5},{5,9},{9,13},{2,6},{6,10},{10,14},{3,7},{... | collective-permute-start | bytes 1572872 | tf_op jit(solution)/shard_map/ppermute | solution.py:60
  9.7 15.6 %collective-permute-start.1 = (bf16[256,8,128]{0,2,1:T(8,128)(2,1)}, bf16[256,8,128]{0,2,1:T(8,128)(2,1)}, u32[]{:S(2)}, u32[]{:S(2)}) collective-permute-start(bf16[256,8,128]{0,2,1:T(8,128)(2,1)} %get-tuple-element.19), channel_id=1, source_target_pairs={{4,0},{8,4},{12,8},{5,1},{9,5},{13,9},{6,2},{10,6},{14,10},{7,3},{... | collective-permute-start | bytes 1572872 | tf_op jit(solution)/shard_map/ppermute | solution.py:63
  28.4 1.8 %copy-start.1 = (bf16[16,8,16,256]{3,2,1,0:T(8,128)(2,1)S(1)}, bf16[16,8,16,256]{3,2,1,0:T(8,128)(2,1)}, u32[]{:S(2)}) copy-start(bf16[16,8,16,256]{3,2,1,0:T(8,128)(2,1)} %copy.202) | copy-start | bytes 3145732
  30.5 6.6 %collective-permute-start.2 = (bf16[256,32,8]{0,2,1:T(8,128)(2,1)S(1)}, bf16[256,32,8]{0,2,1:T(8,128)(2,1)S(1)}, u32[]{:S(2)}, u32[]{:S(2)}) collective-permute-start(bf16[256,32,8]{0,2,1:T(8,128)(2,1)S(1)} %get-tuple-element.14), channel_id=1, source_target_pairs={{0,1},{1,2},{2,3},{4,5},{5,6},{6,7},{8,9},{9,10},{10,11},{12,13},{... | collective-permute-start | bytes 393224 | tf_op jit(solution)/shard_map/ppermute | solution.py:60
  31.8 6.0 %collective-permute-start.3 = (bf16[256,32,8]{0,2,1:T(8,128)(2,1)S(1)}, bf16[256,32,8]{0,2,1:T(8,128)(2,1)S(1)}, u32[]{:S(2)}, u32[]{:S(2)}) collective-permute-start(bf16[256,32,8]{0,2,1:T(8,128)(2,1)S(1)} %get-tuple-element.15), channel_id=1, source_target_pairs={{1,0},{2,1},{3,2},{5,4},{6,5},{7,6},{9,8},{10,9},{11,10},{13,12},{... | collective-permute-start | bytes 393224 | tf_op jit(solution)/shard_map/ppermute | solution.py:63
  33.4 0.7 copy-start.5
  38.8 29.1 %collective-permute-start.4 = (bf16[256,2048]{0,1:T(8,128)(2,1)S(1)}, bf16[256,2048]{0,1:T(8,128)(2,1)}, u32[]{:S(2)}, u32[]{:S(2)}) collective-permute-start(bf16[256,2048]{0,1:T(8,128)(2,1)S(1)} %bitcast.136), channel_id=1, source_target_pairs={{0,16},{16,0},{1,17},{17,1},{2,18},{18,2},{3,19},{19,3},{4,20},{20... | collective-permute-start | bytes 3145736 | tf_op jit(solution)/shard_map/ppermute | solution.py:149
  46.8 20.5 %all-to-all-start = ((f32[32,1,512]{2,1,0:T(1,128)}), f32[32,1,512]{2,1,0:T(1,128)S(1)}, u32[]{:S(2)}, u32[]{:S(2)}) async-start(f32[32,1,512]{2,1,0:T(1,128)} %broadcast_in_dim.69), calls=%async_computation | async-start | bytes 131072 | tf_op jit(solution)/shard_map/all_to_all | solution.py:130
  67.8 3.4 %copy-start.2 = (f32[128,512]{1,0:T(8,128)S(1)}, f32[128,512]{1,0:T(8,128)}, u32[]{:S(2)}) copy-start(f32[128,512]{1,0:T(8,128)} %param.7) | copy-start | bytes 786436
  139.2 1.3 copy-start.3

commit v8 on v6

--- a/solution.py
+++ b/solution.py
@@ -53,15 +53,22 @@
     return out[0].astype(jnp.bfloat16)
 
 
+def flat_permute(cells, axis, pairs, dim):
+    if dim != 1:
+        return lax.ppermute(cells, axis, pairs)
+    flat = cells.reshape(cells.shape[0], cells.shape[1] * cells.shape[2])
+    return lax.ppermute(flat, axis, pairs).reshape(cells.shape)
+
+
 def halos(cells, axis, dim):
     length = cells.shape[dim]
     count = lax.axis_size(axis)
     ends = count - 1
-    before = lax.ppermute(
-        lax.slice_in_dim(cells, length - HALF, length, axis=dim), axis, [(i, (i + 1) % count) for i in range(ends)]
-    )
-    after = lax.ppermute(
-        lax.slice_in_dim(cells, 0, HALF, axis=dim), axis, [((i + 1) % count, i) for i in range(ends)]
+    before = flat_permute(
+        lax.slice_in_dim(cells, length - HALF, length, axis=dim), axis, [(i, (i + 1) % count) for i in range(ends)], dim
+    )
+    after = flat_permute(
+        lax.slice_in_dim(cells, 0, HALF, axis=dim), axis, [((i + 1) % count, i) for i in range(ends)], dim
     )
     return before, after
 
@@ -143,12 +150,28 @@
     if parts == 2 and height % parts == 0:
         side = lax.axis_index("freq")
         half = height // parts
-        before, after = halos(rowwise, "col", 2)
-        outgoing = band_of_rows(rowwise, before, after, column_kernel, (1 - side) * half, half)
-        outgoing = outgoing.reshape(channels, block)
-        incoming = lax.ppermute(outgoing, "freq", [(0, 1), (1, 0)])
-        local = band_of_rows(rowwise, before, after, column_kernel, side * half, half)
-        local = local.reshape(channels, block)
+        width = channels // 2 if channels % 2 == 0 else channels
+        spans = [(low, min(low + width, channels)) for low in range(0, channels, width)]
+        theirs = lax.dynamic_slice_in_dim(whitening, (1 - side) * channels, channels, axis=1)
+        sends, frames, partial = [], [], None
+        for low, high in spans:
+            rows = rowwise[low:high]
+            before, after = halos(rows, "col", 2)
+            outgoing = band_of_rows(rows, before, after, column_kernel[low:high], (1 - side) * half, half)
+            outgoing = outgoing.reshape(high - low, block)
+            incoming = lax.ppermute(outgoing, "freq", [(0, 1), (1, 0)])
+            outgoing, rowwise, before, after = lax.optimization_barrier((outgoing, rowwise, before, after))
+            sends.append(outgoing)
+            frames.append((before, after))
+            term = jnp.dot(theirs[:, low:high], incoming, preferred_element_type=jnp.float32)
+            partial = term if partial is None else partial + term
+        local = jnp.concatenate(
+            [
+                band_of_rows(rowwise[low:high], before, after, column_kernel[low:high], side * half, half)
+                for (low, high), (before, after) in zip(spans, frames)
+            ]
+        ).reshape(channels, block)
+        outgoing = jnp.concatenate(sends)
         plane_sums = jnp.sum(outgoing, axis=1, dtype=jnp.float32) + jnp.sum(local, axis=1, dtype=jnp.float32)
         placed = jnp.zeros((parts * channels,), jnp.float32)
         placed = lax.dynamic_update_slice_in_dim(placed, plane_sums, side * channels, axis=0)
@@ -156,10 +179,7 @@
         means = channel_sums / total_pixels
         shift = jnp.dot(whitening.astype(jnp.float32), means, precision=lax.Precision.HIGHEST)
         mine = lax.dynamic_slice_in_dim(whitening, side * channels, channels, axis=1)
-        theirs = lax.dynamic_slice_in_dim(whitening, (1 - side) * channels, channels, axis=1)
-        mixed = jnp.dot(mine, local, preferred_element_type=jnp.float32) + jnp.dot(
-            theirs, incoming, preferred_element_type=jnp.float32
-        )
+        mixed = jnp.dot(mine, local, preferred_element_type=jnp.float32) + partial
     else:
         smoothed = split_pass(rowwise, column_kernel, "col", 2)
         flattened = smoothed.reshape(channels, height * breadth)

time: 146 us -> 140 us (0.959)
  waiting for transfers between devices: 22.2 us -> 8.12 us
  starting transfers between devices: 17.4 us -> 26.6 us
  local copies, waits for them, and re-layouts: 11 us -> 13.7 us
  blocking collectives: 51.9 us -> 49.8 us
  matrix products: 35.9 us -> 33.9 us
    all_to_all x1, waiting for transfers between devices: 16.2 us -> 4.71 us  [gathered_sum(): gathered = lax.all_to_all(spread, axes, 0, 0, tiled=True)]
    ppermute x4 -> x6, starting transfers between devices: 9.01 us -> 16.3 us  [the longest x4 8.62 us: flat_permute(): return lax.ppermute(cells, axis, pairs)]
    ppermute x4 -> x6, waiting for transfers between devices: 5.97 us -> 3.4 us  [the longest x2 1.93 us: flat_permute(): return lax.ppermute(flat, axis, pairs).reshape(cells.shape)]
    reshape x0 -> x2, local copies, waits for them, and re-layouts: none -> 2.26 us  [flat_permute(): flat = cells.reshape(cells.shape[0], cells.shape[1] * cells.shape[2])]
    all_to_all x2, blocking collectives: 26.6 us -> 24.6 us  [total_sum(): pieces = lax.all_to_all(flat, axes, 0, 0, tiled=True)]
    conv_general_dilated x9 -> x15, matrix products: 16.5 us -> 15.2 us  [depthwise(): lax.conv_general_dilated(cells[None], kernel, window_strides=(1, 1), padd...]
    convert_element_type x7 -> x11, local copies, waits for them, and re-layouts: 3.3 us -> 2.05 us  [depthwise(): return out[0].astype(jnp.bfloat16)]
    dot_general x2 -> x3, matrix products: 6.05 us -> 5.36 us  [the longest x1 2.68 us: shards(): mixed = jnp.dot(mine, local, preferred_element_type=jnp.float32) + partial]
  transfers between devices with their start and end apart: 6 -> 9, of which waited for: 3 -> 3; matrix products, arithmetic and copies ran while one was open for 14% -> 19% of each run, Pallas kernels for 0% -> 0%
where the time goes in v8:
time: 140 us
  blocking collectives  49.8 us (36%)
  matrix products  33.9 us (24%)
  starting transfers between devices  26.6 us (19%)
  local copies, waits for them, and re-layouts  13.7 us (10%)
  waiting for transfers between devices  8.12 us (6%)
  other arithmetic  4.56 us (3%)
  between operations  3.13 us (2%)
    all_to_all x2, blocking collectives, total_sum(): gathered = lax.all_to_all(spread, axes, 0, 0, tiled=True)  25.2 us
    all_to_all x2, blocking collectives, total_sum(): pieces = lax.all_to_all(flat, axes, 0, 0, tiled=True)  24.6 us
    conv_general_dilated x15, matrix products, depthwise(): lax.conv_general_dilated(cells[None], kernel, window_strides=(1, 1), padd...  15.2 us
    ppermute x4, starting transfers between devices, flat_permute(): return lax.ppermute(cells, axis, pairs)  8.62 us
    all_to_all x1, starting transfers between devices, gathered_sum(): gathered = lax.all_to_all(spread, axes, 0, 0, tiled=True)  8.19 us
    ppermute x2, starting transfers between devices, flat_permute(): return lax.ppermute(flat, axis, pairs).reshape(cells.shape)  7.64 us
    all_to_all x1, waiting for transfers between devices, gathered_sum(): gathered = lax.all_to_all(spread, axes, 0, 0, tiled=True)  4.71 us
    unnamed x23, local copies, waits for them, and re-layouts  3.7 us
  transfers between devices with their start and end apart: 9, of which 3 were waited for; matrix products, arithmetic and copies ran while one was open for 19% of the time, Pallas kernels for 0%

profile of v8, /device:TPU:0, one launch (start us, length us, event | category | flops | bytes accessed | tf_op | source)
XLA Modules:
  0.0 139.8 jit_solution(16353364715916409074)
XLA Ops:
  0.6 1.3 fusion.134
  2.0 1.1 copy.524
  3.1 1.3 collective-permute-start.1
  4.4 1.1 copy.523
  5.5 6.4 %collective-permute-start = (bf16[256,1024]{0,1:T(8,128)(2,1)}, bf16[256,1024]{0,1:T(8,128)(2,1)}, u32[]{:S(2)}, u32[]{:S(2)}) collective-permute-start(bf16[256,1024]{0,1:T(8,128)(2,1)} %bitcast), channel_id=1, source_target_pairs={{0,4},{4,8},{8,12},{1,5},{5,9},{9,13},{2,6},{6,10},{10,14},{3,7},{... | collective-permute-start | bytes 1572872 | tf_op jit(solution)/shard_map/ppermute | solution.py:60
  11.9 3.0 %copy.475 = bf16[256,32,128]{0,2,1:T(8,128)(2,1)S(1)} copy(bf16[256,32,128]{2,1,0:T(8,128)(2,1)} %param.4) | data formatting | bytes 4194304 | tf_op args[0]
  15.1 4.1 %fusion.11 = bf16[16,8,16,256]{3,1,2,0:T(8,128)(2,1)S(1)} fusion(bf16[256,32,8,16]{0,3,2,1:T(8,128)(2,1)S(1)} %bitcast.176, bf16[256,1,17,1]{0,2,3,1:T(8,128)(2,1)S(1)} %bitcast.204), kind=kOutput, calls=%fused_computation.22 | convolution fusion | flops 18350080 | bytes 3154432 | tf_op jit(solution)/shard_map/conv_general_dilated | solution.py:44
  19.3 1.2 copy.482
  20.6 1.9 %collective-permute-done = bf16[256,1024]{0,1:T(8,128)(2,1)} collective-permute-done((bf16[256,1024]{0,1:T(8,128)(2,1)}, bf16[256,1024]{0,1:T(8,128)(2,1)}, u32[]{:S(2)}, u32[]{:S(2)}) %collective-permute-start) | collective-permute-done | bytes 524320 | tf_op jit(solution)/shard_map/ppermute | solution.py:60
  22.6 1.3 pad_maximum_fusion.1
  23.9 1.7 %fusion.14 = bf16[8,8,16,256]{3,1,2,0:T(8,128)(2,1)S(1)} fusion(bf16[256,24,8,16]{0,3,2,1:T(8,128)(2,1)S(1)} %bitcast.194, bf16[256,1,17,1]{0,2,3,1:T(8,128)(2,1)S(1)} %bitcast.205), kind=kOutput, calls=%fused_computation.23 | convolution fusion | flops 9175040 | bytes 2105856 | tf_op jit(solution)/shard_map/conv_general_dilated | solution.py:44
  25.7 1.7 %fusion.17 = bf16[8,8,16,256]{3,1,2,0:T(8,128)(2,1)S(1)} fusion(bf16[256,24,8,16]{0,3,2,1:T(8,128)(2,1)S(1)} %bitcast.193, bf16[256,1,17,1]{0,2,3,1:T(8,128)(2,1)S(1)} %bitcast.206), kind=kOutput, calls=%fused_computation.24 | convolution fusion | flops 9175040 | bytes 2105856 | tf_op jit(solution)/shard_map/conv_general_dilated | solution.py:44
  28.0 1.3 collective-permute-start.2
  29.3 1.3 collective-permute-start.3
  31.0 1.4 fusion.23
  32.9 1.5 %collective-permute-done.3 = bf16[128,32,8]{0,2,1:T(8,128)(2,1)S(1)} collective-permute-done((bf16[128,32,8]{0,2,1:T(8,128)(2,1)S(1)}, bf16[128,32,8]{0,2,1:T(8,128)(2,1)S(1)}, u32[]{:S(2)}, u32[]{:S(2)}) %collective-permute-start.3) | collective-permute-done | bytes 65568 | tf_op jit(solution)/shard_map/ppermute | solution.py:58
  34.8 1.6 %collective-permute-start.6 = (bf16[128,2048]{0,1:T(8,128)(2,1)S(1)}, bf16[128,2048]{0,1:T(8,128)(2,1)S(1)}, u32[]{:S(2)}, u32[]{:S(2)}) collective-permute-start(bf16[128,2048]{0,1:T(8,128)(2,1)S(1)} %bitcast.179), channel_id=1, source_target_pairs={{0,16},{16,0},{1,17},{17,1},{2,18},{18,2},{3,19},{19,3},{4,20},{20... | collective-permute-start | bytes 1572872 | tf_op jit(solution)/shard_map/ppermute | solution.py:162
  36.6 4.6 %collective-permute-start.4 = (bf16[128,32,8]{0,2,1:T(8,128)(2,1)S(1)}, bf16[128,32,8]{0,2,1:T(8,128)(2,1)S(1)}, u32[]{:S(2)}, u32[]{:S(2)}) collective-permute-start(bf16[128,32,8]{0,2,1:T(8,128)(2,1)S(1)} %get-tuple-element.22), channel_id=1, source_target_pairs={{0,1},{1,2},{2,3},{4,5},{5,6},{6,7},{8,9},{9,10},{10,11},{12,13},{... | collective-permute-start | bytes 196616 | tf_op jit(solution)/shard_map/ppermute | solution.py:58
  41.2 1.5 %collective-permute-start.5 = (bf16[128,32,8]{0,2,1:T(8,128)(2,1)S(1)}, bf16[128,32,8]{0,2,1:T(8,128)(2,1)S(1)}, u32[]{:S(2)}, u32[]{:S(2)}) collective-permute-start(bf16[128,32,8]{0,2,1:T(8,128)(2,1)S(1)} %get-tuple-element.23), channel_id=1, source_target_pairs={{1,0},{2,1},{3,2},{5,4},{6,5},{7,6},{9,8},{10,9},{11,10},{13,12},{... | collective-permute-start | bytes 196616 | tf_op jit(solution)/shard_map/ppermute | solution.py:58
  43.0 1.4 fusion.22
  48.4 1.4 fusion.20
  50.1 1.4 fusion.21
  53.2 8.2 %all-to-all-start = ((f32[32,1,512]{2,1,0:T(1,128)}), f32[32,1,512]{2,1,0:T(1,128)S(1)}, u32[]{:S(2)}, u32[]{:S(2)}) async-start(f32[32,1,512]{2,1,0:T(1,128)} %broadcast_in_dim.90), calls=%async_computation | async-start | bytes 131072 | tf_op jit(solution)/shard_map/all_to_all | solution.py:137
  61.4 2.7 %fusion.66 = f32[512,2048]{1,0:T(8,128)} fusion(bf16[256,2048]{0,1:T(8,128)(2,1)S(1)} %bitcast.178, bf16[512,512]{1,0:T(8,128)(2,1)S(1)} %copy-done, s32[]{:T(128)S(6)} %select_n.8), kind=kOutput, calls=%fused_computation.101 | convolution fusion | flops 536870912 | bytes 5505028 | tf_op jit(solution)/shard_map/dot_general | solution.py:182
  64.0 4.7 %all-to-all-done = f32[32,1,512]{2,1,0:T(1,128)S(1)} async-done(((f32[32,1,512]{2,1,0:T(1,128)}), f32[32,1,512]{2,1,0:T(1,128)S(1)}, u32[]{:S(2)}, u32[]{:S(2)}) %all-to-all-start) | async-done | bytes 65568 | tf_op jit(solution)/shard_map/all_to_all | solution.py:137
  69.3 1.9 %fusion.76 = f32[512,2048]{1,0:T(8,128)S(1)} fusion(bf16[128,2048]{0,1:T(8,128)(2,1)} %collective-permute-done.7, bf16[512,512]{1,0:T(8,128)(2,1)S(1)} %copy-done, s32[]{:T(128)S(6)} %add.62), kind=kOutput, calls=%fused_computation.111 | convolution fusion | flops 268435456 | bytes 4849668 | tf_op jit(solution)/shard_map/dot_general | solution.py:166
  72.7 2.1 %fusion.24 = f32[128,512]{1,0:T(8,128)S(1)} fusion(bf16[512,2048]{1,0:T(8,128)(2,1)S(1)} %subtract_convert_fusion, f32[128,512]{1,0:T(8,128)S(1)} %copy-done.3), kind=kOutput, calls=%fused_computation.33 | convolution fusion | flops 537722880 | bytes 2621440 | tf_op jit(solution)/shard_map/dot_general | solution.py:115
  75.1 12.0 %all_to_all.38 = f32[32,1,2048]{2,1,0:T(1,128)S(1)} all-to-all(f32[32,1,2048]{2,1,0:T(1,128)S(1)} %all_to_all.31), channel_id=1, replica_groups=mesh['freq'=2,'row'=4,'col'=4] {'freq','row','col'}, dimensions={0} | all-to-all | bytes 524288 | tf_op jit(solution)/shard_map/all_to_all | solution.py:125
  87.4 12.5 %all_to_all.39 = f32[32,1,2048]{2,1,0:T(1,128)S(1)} all-to-all(f32[32,1,2048]{2,1,0:T(1,128)S(1)} %broadcast_in_dim.91), channel_id=1, replica_groups=mesh['freq'=2,'row'=4,'col'=4] {'freq','row','col'}, dimensions={0} | all-to-all | bytes 524288 | tf_op jit(solution)/shard_map/all_to_all | solution.py:128
  107.2 12.6 %all_to_all.40 = f32[32,1,2048]{2,1,0:T(1,128)S(1)} all-to-all(f32[32,1,2048]{2,1,0:T(1,128)S(1)} %all_to_all.32), channel_id=1, replica_groups=mesh['freq'=2,'row'=4,'col'=4] {'freq','row','col'}, dimensions={0} | all-to-all | bytes 524288 | tf_op jit(solution)/shard_map/all_to_all | solution.py:125
  120.1 12.6 %all_to_all.41 = f32[32,1,2048]{2,1,0:T(1,128)S(1)} all-to-all(f32[32,1,2048]{2,1,0:T(1,128)S(1)} %broadcast_in_dim.92), channel_id=1, replica_groups=mesh['freq'=2,'row'=4,'col'=4] {'freq','row','col'}, dimensions={0} | all-to-all | bytes 524288 | tf_op jit(solution)/shard_map/all_to_all | solution.py:128
  138.6 1.2 convolution_convert_fusion
  (145 shorter events, 22.8 us)
Async XLA Ops:
  0.6 60.7 %copy-start = (bf16[512,512]{1,0:T(8,128)(2,1)S(1)}, bf16[512,512]{1,0:T(8,128)(2,1)}, u32[]{:S(2)}) copy-start(bf16[512,512]{1,0:T(8,128)(2,1)} %param.6) | copy-start | bytes 1572868
  3.1 17.5 %collective-permute-start.1 = (bf16[256,1024]{0,1:T(8,128)(2,1)}, bf16[256,1024]{0,1:T(8,128)(2,1)S(1)}, u32[]{:S(2)}, u32[]{:S(2)}) collective-permute-start(bf16[256,1024]{0,1:T(8,128)(2,1)} %bitcast.11), channel_id=1, source_target_pairs={{4,0},{8,4},{12,8},{5,1},{9,5},{13,9},{6,2},{10,6},{14,10},{7,3},{... | collective-permute-start | bytes 1572872 | tf_op jit(solution)/shard_map/ppermute | solution.py:60
  5.5 17.0 %collective-permute-start = (bf16[256,1024]{0,1:T(8,128)(2,1)}, bf16[256,1024]{0,1:T(8,128)(2,1)}, u32[]{:S(2)}, u32[]{:S(2)}) collective-permute-start(bf16[256,1024]{0,1:T(8,128)(2,1)} %bitcast), channel_id=1, source_target_pairs={{0,4},{4,8},{8,12},{1,5},{5,9},{9,13},{2,6},{6,10},{10,14},{3,7},{... | collective-permute-start | bytes 1572872 | tf_op jit(solution)/shard_map/ppermute | solution.py:60
  11.9 3.0 %copy-start.5 = (f32[256]{0:T(256)S(1)}, f32[256]{0:T(256)}, u32[]{:S(2)}) copy-start(f32[256]{0:T(256)} %param.5) | copy-start | bytes 3076
  25.7 1.8 %copy-start.2 = (bf16[16,8,16,256]{3,2,1,0:T(8,128)(2,1)S(1)}, bf16[16,8,16,256]{3,2,1,0:T(8,128)(2,1)}, u32[]{:S(2)}) copy-start(bf16[16,8,16,256]{3,2,1,0:T(8,128)(2,1)} %copy.482) | copy-start | bytes 3145732
  28.0 3.0 %copy-start.6 = (pred[8,16]{0,1:T(8,128)(4,1)S(1)}, pred[8,16]{0,1:T(8,128)(4,1)}, u32[]{:S(2)}) copy-start(pred[8,16]{0,1:T(8,128)(4,1)} %constant.98) | copy-start | bytes 388
  28.0 4.5 %collective-permute-start.2 = (bf16[128,32,8]{0,2,1:T(8,128)(2,1)S(1)}, bf16[128,32,8]{0,2,1:T(8,128)(2,1)S(1)}, u32[]{:S(2)}, u32[]{:S(2)}) collective-permute-start(bf16[128,32,8]{0,2,1:T(8,128)(2,1)S(1)} %get-tuple-element.24), channel_id=1, source_target_pairs={{0,1},{1,2},{2,3},{4,5},{5,6},{6,7},{8,9},{9,10},{10,11},{12,13},{... | collective-permute-start | bytes 196616 | tf_op jit(solution)/shard_map/ppermute | solution.py:58
  29.3 5.1 %collective-permute-start.3 = (bf16[128,32,8]{0,2,1:T(8,128)(2,1)S(1)}, bf16[128,32,8]{0,2,1:T(8,128)(2,1)S(1)}, u32[]{:S(2)}, u32[]{:S(2)}) collective-permute-start(bf16[128,32,8]{0,2,1:T(8,128)(2,1)S(1)} %get-tuple-element.25), channel_id=1, source_target_pairs={{1,0},{2,1},{3,2},{5,4},{6,5},{7,6},{9,8},{10,9},{11,10},{13,12},{... | collective-permute-start | bytes 196616 | tf_op jit(solution)/shard_map/ppermute | solution.py:58
  34.8 36.5 %collective-permute-start.6 = (bf16[128,2048]{0,1:T(8,128)(2,1)S(1)}, bf16[128,2048]{0,1:T(8,128)(2,1)S(1)}, u32[]{:S(2)}, u32[]{:S(2)}) collective-permute-start(bf16[128,2048]{0,1:T(8,128)(2,1)S(1)} %bitcast.179), channel_id=1, source_target_pairs={{0,16},{16,0},{1,17},{17,1},{2,18},{18,2},{3,19},{19,3},{4,20},{20... | collective-permute-start | bytes 1572872 | tf_op jit(solution)/shard_map/ppermute | solution.py:162
  36.6 7.9 %collective-permute-start.4 = (bf16[128,32,8]{0,2,1:T(8,128)(2,1)S(1)}, bf16[128,32,8]{0,2,1:T(8,128)(2,1)S(1)}, u32[]{:S(2)}, u32[]{:S(2)}) collective-permute-start(bf16[128,32,8]{0,2,1:T(8,128)(2,1)S(1)} %get-tuple-element.22), channel_id=1, source_target_pairs={{0,1},{1,2},{2,3},{4,5},{5,6},{6,7},{8,9},{9,10},{10,11},{12,13},{... | collective-permute-start | bytes 196616 | tf_op jit(solution)/shard_map/ppermute | solution.py:58
  41.2 3.7 %collective-permute-start.5 = (bf16[128,32,8]{0,2,1:T(8,128)(2,1)S(1)}, bf16[128,32,8]{0,2,1:T(8,128)(2,1)S(1)}, u32[]{:S(2)}, u32[]{:S(2)}) collective-permute-start(bf16[128,32,8]{0,2,1:T(8,128)(2,1)S(1)} %get-tuple-element.23), channel_id=1, source_target_pairs={{1,0},{2,1},{3,2},{5,4},{6,5},{7,6},{9,8},{10,9},{11,10},{13,12},{... | collective-permute-start | bytes 196616 | tf_op jit(solution)/shard_map/ppermute | solution.py:58
  46.1 23.2 %collective-permute-start.7 = (bf16[128,2048]{0,1:T(8,128)(2,1)S(1)}, bf16[128,2048]{0,1:T(8,128)(2,1)}, u32[]{:S(2)}, u32[]{:S(2)}) collective-permute-start(bf16[128,2048]{0,1:T(8,128)(2,1)S(1)} %bitcast.181), channel_id=1, source_target_pairs={{0,16},{16,0},{1,17},{17,1},{2,18},{18,2},{3,19},{19,3},{4,20},{20... | collective-permute-start | bytes 1572872 | tf_op jit(solution)/shard_map/ppermute | solution.py:162
  53.2 15.6 %all-to-all-start = ((f32[32,1,512]{2,1,0:T(1,128)}), f32[32,1,512]{2,1,0:T(1,128)S(1)}, u32[]{:S(2)}, u32[]{:S(2)}) async-start(f32[32,1,512]{2,1,0:T(1,128)} %broadcast_in_dim.90), calls=%async_computation | async-start | bytes 131072 | tf_op jit(solution)/shard_map/all_to_all | solution.py:137
  69.3 2.4 %copy-start.1 = (f32[512,2048]{1,0:T(8,128)S(1)}, f32[512,2048]{1,0:T(8,128)}, u32[]{:S(2)}) copy-start(f32[512,2048]{1,0:T(8,128)} %fusion.66) | copy-start | bytes 12582916
  71.7 0.9 copy-start.3
  138.6 1.3 copy-start.4

commit v9 on v8

--- a/solution.py
+++ b/solution.py
@@ -173,9 +173,10 @@
         ).reshape(channels, block)
         outgoing = jnp.concatenate(sends)
         plane_sums = jnp.sum(outgoing, axis=1, dtype=jnp.float32) + jnp.sum(local, axis=1, dtype=jnp.float32)
-        placed = jnp.zeros((parts * channels,), jnp.float32)
-        placed = lax.dynamic_update_slice_in_dim(placed, plane_sums, side * channels, axis=0)
-        channel_sums = gathered_sum(placed, ("freq", "row", "col"))
+        count = devices
+        spread = jnp.broadcast_to(plane_sums[None], (count, channels))
+        gathered = lax.all_to_all(spread, ("freq", "row", "col"), 0, 0, tiled=True)
+        channel_sums = jnp.sum(gathered.reshape(parts, count // parts, channels), axis=1).reshape(parts * channels)
         means = channel_sums / total_pixels
         shift = jnp.dot(whitening.astype(jnp.float32), means, precision=lax.Precision.HIGHEST)
         mine = lax.dynamic_slice_in_dim(whitening, side * channels, channels, axis=1)

time: 140 us -> 140 us (level)
    unnamed x23 -> x25, local copies, waits for them, and re-layouts: 3.7 us -> 3.72 us
where the time goes in v9:
time: 140 us
  blocking collectives  49.8 us (36%)
  matrix products  33.9 us (24%)
  starting transfers between devices  26.6 us (19%)
  local copies, waits for them, and re-layouts  13.7 us (10%)
  waiting for transfers between devices  7.97 us (6%)
  other arithmetic  4.42 us (3%)
  between operations  3.13 us (2%)
    all_to_all x2, blocking collectives, total_sum(): gathered = lax.all_to_all(spread, axes, 0, 0, tiled=True)  25.2 us
    all_to_all x2, blocking collectives, total_sum(): pieces = lax.all_to_all(flat, axes, 0, 0, tiled=True)  24.6 us
    conv_general_dilated x15, matrix products, depthwise(): lax.conv_general_dilated(cells[None], kernel, window_strides=(1, 1), padd...  15.2 us
    ppermute x4, starting transfers between devices, flat_permute(): return lax.ppermute(cells, axis, pairs)  8.62 us
    all_to_all x1, starting transfers between devices, shards(): gathered = lax.all_to_all(spread, ('freq', 'row', 'col'), 0, 0, tiled=True)  8.19 us
    ppermute x2, starting transfers between devices, flat_permute(): return lax.ppermute(flat, axis, pairs).reshape(cells.shape)  7.64 us
    all_to_all x1, waiting for transfers between devices, shards(): gathered = lax.all_to_all(spread, ('freq', 'row', 'col'), 0, 0, tiled=True)  4.56 us
    unnamed x25, local copies, waits for them, and re-layouts  3.72 us
  transfers between devices with their start and end apart: 9, of which 3 were waited for; matrix products, arithmetic and copies ran while one was open for 19% of the time, Pallas kernels for 0%

profile of v9, /device:TPU:0, one launch (start us, length us, event | category | flops | bytes accessed | tf_op | source)
XLA Modules:
  0.0 139.5 jit_solution(2453311570244524791)
XLA Ops:
  0.6 1.3 fusion.134
  2.0 1.1 copy.523
  3.1 1.3 collective-permute-start.1
  4.4 1.1 copy.522
  5.5 6.4 %collective-permute-start = (bf16[256,1024]{0,1:T(8,128)(2,1)}, bf16[256,1024]{0,1:T(8,128)(2,1)}, u32[]{:S(2)}, u32[]{:S(2)}) collective-permute-start(bf16[256,1024]{0,1:T(8,128)(2,1)} %bitcast), channel_id=1, source_target_pairs={{0,4},{4,8},{8,12},{1,5},{5,9},{9,13},{2,6},{6,10},{10,14},{3,7},{... | collective-permute-start | bytes 1572872 | tf_op jit(solution)/shard_map/ppermute | solution.py:60
  11.9 3.0 %copy.475 = bf16[256,32,128]{0,2,1:T(8,128)(2,1)S(1)} copy(bf16[256,32,128]{2,1,0:T(8,128)(2,1)} %param.4) | data formatting | bytes 4194304 | tf_op args[0]
  15.1 4.1 %fusion.11 = bf16[16,8,16,256]{3,1,2,0:T(8,128)(2,1)S(1)} fusion(bf16[256,32,8,16]{0,3,2,1:T(8,128)(2,1)S(1)} %bitcast.181, bf16[256,1,17,1]{0,2,3,1:T(8,128)(2,1)S(1)} %bitcast.210), kind=kOutput, calls=%fused_computation.22 | convolution fusion | flops 18350080 | bytes 3154432 | tf_op jit(solution)/shard_map/conv_general_dilated | solution.py:44
  19.3 1.2 copy.482
  20.6 1.9 %collective-permute-done = bf16[256,1024]{0,1:T(8,128)(2,1)} collective-permute-done((bf16[256,1024]{0,1:T(8,128)(2,1)}, bf16[256,1024]{0,1:T(8,128)(2,1)}, u32[]{:S(2)}, u32[]{:S(2)}) %collective-permute-start) | collective-permute-done | bytes 524320 | tf_op jit(solution)/shard_map/ppermute | solution.py:60
  22.6 1.3 pad_maximum_fusion.1
  23.9 1.7 %fusion.14 = bf16[8,8,16,256]{3,1,2,0:T(8,128)(2,1)S(1)} fusion(bf16[256,24,8,16]{0,3,2,1:T(8,128)(2,1)S(1)} %bitcast.199, bf16[256,1,17,1]{0,2,3,1:T(8,128)(2,1)S(1)} %bitcast.211), kind=kOutput, calls=%fused_computation.23 | convolution fusion | flops 9175040 | bytes 2105856 | tf_op jit(solution)/shard_map/conv_general_dilated | solution.py:44
  25.7 1.7 %fusion.17 = bf16[8,8,16,256]{3,1,2,0:T(8,128)(2,1)S(1)} fusion(bf16[256,24,8,16]{0,3,2,1:T(8,128)(2,1)S(1)} %bitcast.198, bf16[256,1,17,1]{0,2,3,1:T(8,128)(2,1)S(1)} %bitcast.212), kind=kOutput, calls=%fused_computation.24 | convolution fusion | flops 9175040 | bytes 2105856 | tf_op jit(solution)/shard_map/conv_general_dilated | solution.py:44
  28.0 1.3 collective-permute-start.2
  29.3 1.3 collective-permute-start.3
  31.0 1.4 fusion.23
  32.9 1.5 %collective-permute-done.3 = bf16[128,32,8]{0,2,1:T(8,128)(2,1)S(1)} collective-permute-done((bf16[128,32,8]{0,2,1:T(8,128)(2,1)S(1)}, bf16[128,32,8]{0,2,1:T(8,128)(2,1)S(1)}, u32[]{:S(2)}, u32[]{:S(2)}) %collective-permute-start.3) | collective-permute-done | bytes 65568 | tf_op jit(solution)/shard_map/ppermute | solution.py:58
  34.8 1.6 %collective-permute-start.6 = (bf16[128,2048]{0,1:T(8,128)(2,1)S(1)}, bf16[128,2048]{0,1:T(8,128)(2,1)S(1)}, u32[]{:S(2)}, u32[]{:S(2)}) collective-permute-start(bf16[128,2048]{0,1:T(8,128)(2,1)S(1)} %bitcast.184), channel_id=1, source_target_pairs={{0,16},{16,0},{1,17},{17,1},{2,18},{18,2},{3,19},{19,3},{4,20},{20... | collective-permute-start | bytes 1572872 | tf_op jit(solution)/shard_map/ppermute | solution.py:162
  36.6 4.6 %collective-permute-start.4 = (bf16[128,32,8]{0,2,1:T(8,128)(2,1)S(1)}, bf16[128,32,8]{0,2,1:T(8,128)(2,1)S(1)}, u32[]{:S(2)}, u32[]{:S(2)}) collective-permute-start(bf16[128,32,8]{0,2,1:T(8,128)(2,1)S(1)} %get-tuple-element.22), channel_id=1, source_target_pairs={{0,1},{1,2},{2,3},{4,5},{5,6},{6,7},{8,9},{9,10},{10,11},{12,13},{... | collective-permute-start | bytes 196616 | tf_op jit(solution)/shard_map/ppermute | solution.py:58
  41.2 1.5 %collective-permute-start.5 = (bf16[128,32,8]{0,2,1:T(8,128)(2,1)S(1)}, bf16[128,32,8]{0,2,1:T(8,128)(2,1)S(1)}, u32[]{:S(2)}, u32[]{:S(2)}) collective-permute-start(bf16[128,32,8]{0,2,1:T(8,128)(2,1)S(1)} %get-tuple-element.23), channel_id=1, source_target_pairs={{1,0},{2,1},{3,2},{5,4},{6,5},{7,6},{9,8},{10,9},{11,10},{13,12},{... | collective-permute-start | bytes 196616 | tf_op jit(solution)/shard_map/ppermute | solution.py:58
  43.0 1.4 fusion.22
  48.4 1.4 fusion.20
  50.1 1.4 fusion.21
  53.0 8.2 %all-to-all-start = ((f32[32,1,256]{2,1,0:T(1,128)}), f32[32,1,256]{2,1,0:T(1,128)S(1)}, u32[]{:S(2)}, u32[]{:S(2)}) async-start(f32[32,1,256]{2,1,0:T(1,128)} %broadcast_in_dim.89), calls=%async_computation | async-start | bytes 65536 | tf_op jit(solution)/shard_map/all_to_all | solution.py:178
  61.2 2.7 %fusion.66 = f32[512,2048]{1,0:T(8,128)} fusion(bf16[256,2048]{0,1:T(8,128)(2,1)S(1)} %bitcast.183, bf16[512,512]{1,0:T(8,128)(2,1)S(1)} %copy-done, s32[]{:T(128)S(6)} %select_n.8), kind=kOutput, calls=%fused_computation.101 | convolution fusion | flops 536870912 | bytes 5505028 | tf_op jit(solution)/shard_map/dot_general | solution.py:183
  63.9 4.6 %all-to-all-done = f32[32,1,256]{2,1,0:T(1,128)S(1)} async-done(((f32[32,1,256]{2,1,0:T(1,128)}), f32[32,1,256]{2,1,0:T(1,128)S(1)}, u32[]{:S(2)}, u32[]{:S(2)}) %all-to-all-start) | async-done | bytes 32800 | tf_op jit(solution)/shard_map/all_to_all | solution.py:178
  69.0 1.9 %fusion.76 = f32[512,2048]{1,0:T(8,128)S(1)} fusion(bf16[128,2048]{0,1:T(8,128)(2,1)} %collective-permute-done.7, bf16[512,512]{1,0:T(8,128)(2,1)S(1)} %copy-done, s32[]{:T(128)S(6)} %add.61), kind=kOutput, calls=%fused_computation.111 | convolution fusion | flops 268435456 | bytes 4849668 | tf_op jit(solution)/shard_map/dot_general | solution.py:166
  72.3 2.1 %fusion.24 = f32[128,512]{1,0:T(8,128)S(1)} fusion(bf16[512,2048]{1,0:T(8,128)(2,1)S(1)} %subtract_convert_fusion, f32[128,512]{1,0:T(8,128)S(1)} %copy-done.3), kind=kOutput, calls=%fused_computation.33 | convolution fusion | flops 537722880 | bytes 2621440 | tf_op jit(solution)/shard_map/dot_general | solution.py:115
  74.8 12.0 %all_to_all.38 = f32[32,1,2048]{2,1,0:T(1,128)S(1)} all-to-all(f32[32,1,2048]{2,1,0:T(1,128)S(1)} %all_to_all.31), channel_id=1, replica_groups=mesh['freq'=2,'row'=4,'col'=4] {'freq','row','col'}, dimensions={0} | all-to-all | bytes 524288 | tf_op jit(solution)/shard_map/all_to_all | solution.py:125
  87.1 12.5 %all_to_all.39 = f32[32,1,2048]{2,1,0:T(1,128)S(1)} all-to-all(f32[32,1,2048]{2,1,0:T(1,128)S(1)} %broadcast_in_dim.90), channel_id=1, replica_groups=mesh['freq'=2,'row'=4,'col'=4] {'freq','row','col'}, dimensions={0} | all-to-all | bytes 524288 | tf_op jit(solution)/shard_map/all_to_all | solution.py:128
  106.9 12.6 %all_to_all.40 = f32[32,1,2048]{2,1,0:T(1,128)S(1)} all-to-all(f32[32,1,2048]{2,1,0:T(1,128)S(1)} %all_to_all.32), channel_id=1, replica_groups=mesh['freq'=2,'row'=4,'col'=4] {'freq','row','col'}, dimensions={0} | all-to-all | bytes 524288 | tf_op jit(solution)/shard_map/all_to_all | solution.py:125
  119.8 12.6 %all_to_all.41 = f32[32,1,2048]{2,1,0:T(1,128)S(1)} all-to-all(f32[32,1,2048]{2,1,0:T(1,128)S(1)} %broadcast_in_dim.91), channel_id=1, replica_groups=mesh['freq'=2,'row'=4,'col'=4] {'freq','row','col'}, dimensions={0} | all-to-all | bytes 524288 | tf_op jit(solution)/shard_map/all_to_all | solution.py:128
  138.3 1.2 convolution_convert_fusion
  (146 shorter events, 22.6 us)
Async XLA Ops:
  0.6 60.6 %copy-start = (bf16[512,512]{1,0:T(8,128)(2,1)S(1)}, bf16[512,512]{1,0:T(8,128)(2,1)}, u32[]{:S(2)}) copy-start(bf16[512,512]{1,0:T(8,128)(2,1)} %param.6) | copy-start | bytes 1572868
  3.1 17.5 %collective-permute-start.1 = (bf16[256,1024]{0,1:T(8,128)(2,1)}, bf16[256,1024]{0,1:T(8,128)(2,1)S(1)}, u32[]{:S(2)}, u32[]{:S(2)}) collective-permute-start(bf16[256,1024]{0,1:T(8,128)(2,1)} %bitcast.11), channel_id=1, source_target_pairs={{4,0},{8,4},{12,8},{5,1},{9,5},{13,9},{6,2},{10,6},{14,10},{7,3},{... | collective-permute-start | bytes 1572872 | tf_op jit(solution)/shard_map/ppermute | solution.py:60
  5.5 17.0 %collective-permute-start = (bf16[256,1024]{0,1:T(8,128)(2,1)}, bf16[256,1024]{0,1:T(8,128)(2,1)}, u32[]{:S(2)}, u32[]{:S(2)}) collective-permute-start(bf16[256,1024]{0,1:T(8,128)(2,1)} %bitcast), channel_id=1, source_target_pairs={{0,4},{4,8},{8,12},{1,5},{5,9},{9,13},{2,6},{6,10},{10,14},{3,7},{... | collective-permute-start | bytes 1572872 | tf_op jit(solution)/shard_map/ppermute | solution.py:60
  11.9 3.0 %copy-start.5 = (f32[256]{0:T(256)S(1)}, f32[256]{0:T(256)}, u32[]{:S(2)}) copy-start(f32[256]{0:T(256)} %param.5) | copy-start | bytes 3076
  25.7 1.8 %copy-start.2 = (bf16[16,8,16,256]{3,2,1,0:T(8,128)(2,1)S(1)}, bf16[16,8,16,256]{3,2,1,0:T(8,128)(2,1)}, u32[]{:S(2)}) copy-start(bf16[16,8,16,256]{3,2,1,0:T(8,128)(2,1)} %copy.482) | copy-start | bytes 3145732
  28.0 3.0 %copy-start.6 = (pred[8,16]{0,1:T(8,128)(4,1)S(1)}, pred[8,16]{0,1:T(8,128)(4,1)}, u32[]{:S(2)}) copy-start(pred[8,16]{0,1:T(8,128)(4,1)} %constant.93) | copy-start | bytes 388
  28.0 4.5 %collective-permute-start.2 = (bf16[128,32,8]{0,2,1:T(8,128)(2,1)S(1)}, bf16[128,32,8]{0,2,1:T(8,128)(2,1)S(1)}, u32[]{:S(2)}, u32[]{:S(2)}) collective-permute-start(bf16[128,32,8]{0,2,1:T(8,128)(2,1)S(1)} %get-tuple-element.24), channel_id=1, source_target_pairs={{0,1},{1,2},{2,3},{4,5},{5,6},{6,7},{8,9},{9,10},{10,11},{12,13},{... | collective-permute-start | bytes 196616 | tf_op jit(solution)/shard_map/ppermute | solution.py:58
  29.3 5.1 %collective-permute-start.3 = (bf16[128,32,8]{0,2,1:T(8,128)(2,1)S(1)}, bf16[128,32,8]{0,2,1:T(8,128)(2,1)S(1)}, u32[]{:S(2)}, u32[]{:S(2)}) collective-permute-start(bf16[128,32,8]{0,2,1:T(8,128)(2,1)S(1)} %get-tuple-element.25), channel_id=1, source_target_pairs={{1,0},{2,1},{3,2},{5,4},{6,5},{7,6},{9,8},{10,9},{11,10},{13,12},{... | collective-permute-start | bytes 196616 | tf_op jit(solution)/shard_map/ppermute | solution.py:58
  34.8 36.2 %collective-permute-start.6 = (bf16[128,2048]{0,1:T(8,128)(2,1)S(1)}, bf16[128,2048]{0,1:T(8,128)(2,1)S(1)}, u32[]{:S(2)}, u32[]{:S(2)}) collective-permute-start(bf16[128,2048]{0,1:T(8,128)(2,1)S(1)} %bitcast.184), channel_id=1, source_target_pairs={{0,16},{16,0},{1,17},{17,1},{2,18},{18,2},{3,19},{19,3},{4,20},{20... | collective-permute-start | bytes 1572872 | tf_op jit(solution)/shard_map/ppermute | solution.py:162
  36.6 7.9 %collective-permute-start.4 = (bf16[128,32,8]{0,2,1:T(8,128)(2,1)S(1)}, bf16[128,32,8]{0,2,1:T(8,128)(2,1)S(1)}, u32[]{:S(2)}, u32[]{:S(2)}) collective-permute-start(bf16[128,32,8]{0,2,1:T(8,128)(2,1)S(1)} %get-tuple-element.22), channel_id=1, source_target_pairs={{0,1},{1,2},{2,3},{4,5},{5,6},{6,7},{8,9},{9,10},{10,11},{12,13},{... | collective-permute-start | bytes 196616 | tf_op jit(solution)/shard_map/ppermute | solution.py:58
  41.2 3.7 %collective-permute-start.5 = (bf16[128,32,8]{0,2,1:T(8,128)(2,1)S(1)}, bf16[128,32,8]{0,2,1:T(8,128)(2,1)S(1)}, u32[]{:S(2)}, u32[]{:S(2)}) collective-permute-start(bf16[128,32,8]{0,2,1:T(8,128)(2,1)S(1)} %get-tuple-element.23), channel_id=1, source_target_pairs={{1,0},{2,1},{3,2},{5,4},{6,5},{7,6},{9,8},{10,9},{11,10},{13,12},{... | collective-permute-start | bytes 196616 | tf_op jit(solution)/shard_map/ppermute | solution.py:58
  46.1 22.9 %collective-permute-start.7 = (bf16[128,2048]{0,1:T(8,128)(2,1)S(1)}, bf16[128,2048]{0,1:T(8,128)(2,1)}, u32[]{:S(2)}, u32[]{:S(2)}) collective-permute-start(bf16[128,2048]{0,1:T(8,128)(2,1)S(1)} %bitcast.186), channel_id=1, source_target_pairs={{0,16},{16,0},{1,17},{17,1},{2,18},{18,2},{3,19},{19,3},{4,20},{20... | collective-permute-start | bytes 1572872 | tf_op jit(solution)/shard_map/ppermute | solution.py:162
  53.0 15.4 %all-to-all-start = ((f32[32,1,256]{2,1,0:T(1,128)}), f32[32,1,256]{2,1,0:T(1,128)S(1)}, u32[]{:S(2)}, u32[]{:S(2)}) async-start(f32[32,1,256]{2,1,0:T(1,128)} %broadcast_in_dim.89), calls=%async_computation | async-start | bytes 65536 | tf_op jit(solution)/shard_map/all_to_all | solution.py:178
  69.0 2.4 %copy-start.1 = (f32[512,2048]{1,0:T(8,128)S(1)}, f32[512,2048]{1,0:T(8,128)}, u32[]{:S(2)}) copy-start(f32[512,2048]{1,0:T(8,128)} %fusion.66) | copy-start | bytes 12582916
  71.4 0.9 copy-start.3
  138.3 1.3 copy-start.4
